TPU v7x, 32 devices: a whole 2x2x4 slice. The times are simulated.
32 devices in a mesh: days: 2 (over y), chan: 4 (over z), win: 4 (over x, core).
Axes of the slice: x: 2, y: 2, z: 4, core: 2. Of those that a mesh axis runs over, the one named last changes fastest.
Arguments:
- spectra: bfloat16 [2560, 32, 1024], P(('days', 'chan'), 'win'), parts along dimension 0, may hold values from -17 to 17
- pair_anchor: int32 [2048], P('chan'), may hold values from 0 to 319
- pair_offset: int32 [2048], P('chan'), may hold values from 0 to 2
- pair_partner: int32 [2048], P('chan'), may hold values from 0 to 319
- pair_count: int32 [4], P('chan'), may hold values from 1 to 512, as said below
- window_bins: int32 [64], P(('days', 'win')), parts along dimension 0, may hold values from 0 to 7
- bin_gain: float32 [8], replicated, may hold values from 0.2 to 5
Outputs:
- ref_stack: float32 [4096, 128], P(('days', 'chan')), parts along dimension 0
- restack: float32 [4096, 128], P(('days', 'chan')), parts along dimension 0
There are 2 independent parts, one for each index of `days`. A program takes and returns all parts, laid end to end along the dimension named above; an argument that names none is the same for every part. Nothing has to cross between parts.
Inputs may be any that keep to these rules, and one draw needn't show every extreme that they name: `pair_count`: each block holds from 1 to 512 live pair slots, the first ones of its slots; some block holds 512 in every draw.
All inputs are finite; a program needn't handle non-finite values.
Results may differ from a plain program's by a relative error of at most 0.0062.
Values may be sent and summed in bfloat16 or wider, within the bound.
No kernel may reach another device: no remote copies, remote signals or barrier semaphores. Data moves between devices by JAX's collectives and lax.ppermute only.
A program may use at most 128 MiB of HBM per device.

v0:
```python
import jax
import jax.numpy as jnp
from jax import lax
from jax.experimental import pallas as pl
from jax.experimental.pallas import tpu as pltpu
from jax.sharding import PartitionSpec as P

LAG = 128


EPS_POWER = 1e-05
EPS_LAG = 1e-06


def whiten(spectra):
    spectra_f = spectra.astype(jnp.float32)
    power_mean = jnp.mean(spectra_f * spectra_f, axis=-1, keepdims=True)
    return (spectra_f * lax.rsqrt(power_mean + EPS_POWER)).astype(jnp.bfloat16)


def lag_table(freq_count, lag_count):
    freq_ids = lax.broadcasted_iota(jnp.float32, (freq_count, lag_count), 0)
    lag_ids = lax.broadcasted_iota(jnp.float32, (freq_count, lag_count), 1) - lag_count // 2
    angles = 2.0 * jnp.pi / (2 * freq_count) * freq_ids * lag_ids
    norm_scale = 1.0 / jnp.sqrt(jnp.float32(freq_count))
    return jnp.concatenate(
        [jnp.cos(angles) * norm_scale, -jnp.sin(angles) * norm_scale], axis=0
    ).astype(jnp.bfloat16)


def cross_spectra(anchors, partners):
    half_width = anchors.shape[-1] // 2
    anchor_f = anchors.astype(jnp.float32)
    partner_f = partners.astype(jnp.float32)
    anchor_re = anchor_f[..., :half_width]
    anchor_im = anchor_f[..., half_width:]
    partner_re = partner_f[..., :half_width]
    partner_im = partner_f[..., half_width:]
    cross_re = anchor_re * partner_re + anchor_im * partner_im
    cross_im = anchor_im * partner_re - anchor_re * partner_im
    return jnp.concatenate([cross_re, cross_im], axis=-1).astype(jnp.bfloat16)


def window_gains(bins, gains):
    levels = lax.broadcasted_iota(jnp.int32, (bins.shape[0], gains.shape[0]), 1)
    return jnp.sum(jnp.where(bins[:, None] == levels, gains[None, :], jnp.float32(0.0)), axis=1)


def window_weights(lag_corr, ref_sum, window_gain):
    corr_f = lag_corr.astype(jnp.float32)
    inner_prod = jnp.mean(corr_f * ref_sum[:, None, :], axis=-1)
    corr_rms = jnp.sqrt(jnp.mean(corr_f * corr_f, axis=-1) + EPS_LAG)
    ref_rms = jnp.sqrt(jnp.mean(ref_sum * ref_sum, axis=-1) + EPS_LAG)
    coherence = inner_prod / (corr_rms * ref_rms[:, None])
    weights = window_gain[None, :] * jnp.exp(2.0 * coherence)
    numerator = jnp.sum(weights[:, :, None] * corr_f, axis=1)
    denominator = jnp.sum(weights, axis=1)
    return (numerator, denominator)


def select_rows(selector, rows):
    return jnp.einsum("sc,cwf->swf", selector, rows, preferred_element_type=jnp.bfloat16)


def butterfly_sum(value, axis):
    peers = lax.axis_size(axis)
    if peers & (peers - 1):
        return lax.psum(value, axis)
    step = 1
    while step < peers:
        pairs = [(i, i ^ step) for i in range(peers)]
        value = jax.tree.map(jnp.add, value, lax.ppermute(value, axis, pairs))
        step *= 2
    return value


def ring_exchange(up_rows, down_rows, axis):
    peers = lax.axis_size(axis)
    up = [(i, (i + 1) % peers) for i in range(peers)]
    down = [(j, i) for i, j in up]
    return lax.ppermute(up_rows, axis, up), lax.ppermute(down_rows, axis, down)


def onehot(index, size, mask):
    return (index[:, None] == lax.broadcasted_iota(jnp.int32, (index.shape[0], size), 1)) & mask[:, None]


def window_weights_wm(corr_f, ref_sum, window_gain):
    inner_prod = jnp.mean(corr_f * ref_sum[None, :, :], axis=-1)
    corr_rms = jnp.sqrt(jnp.mean(corr_f * corr_f, axis=-1) + EPS_LAG)
    ref_rms = jnp.sqrt(jnp.mean(ref_sum * ref_sum, axis=-1) + EPS_LAG)
    coherence = inner_prod / (corr_rms * ref_rms[None, :])
    weights = window_gain[:, None] * jnp.exp(2.0 * coherence)
    numerator = jnp.sum(weights[:, :, None] * corr_f, axis=0)
    denominator = jnp.sum(weights, axis=0)
    return (numerator, denominator)


def block_needs(offs, parts, count, block_chans):
    live = lax.broadcasted_iota(jnp.int32, offs.shape, 0) < count
    hit = parts[:, None] == lax.broadcasted_iota(jnp.int32, (1, block_chans), 1)
    need_minus = jnp.any(hit & (live & (offs == 0))[:, None], axis=0)
    need_plus = jnp.any(hit & (live & (offs == 2))[:, None], axis=0)
    pos_minus = jnp.cumsum(need_minus, dtype=jnp.int32) - 1
    pos_plus = jnp.cumsum(need_plus, dtype=jnp.int32) - 1
    return need_minus, need_plus, pos_minus, pos_plus


def cross_kernel(spill_ref, anchor_ref, own_ref, sbf_ref, saf_ref, sbs_ref, sas_ref,
                 bf_ref, af_ref, bs_ref, as_ref, t_ref, corr_ref):
    wins = anchor_ref.shape[0]
    half = anchor_ref.shape[2] // 2
    t_re = t_ref[:half, :]
    t_im = t_ref[half:, :]
    sbf, saf = sbf_ref[...], saf_ref[...]
    for w in range(wins):
        part = (
            own_ref[w].astype(jnp.float32)
            + jnp.dot(sbf, bf_ref[w], preferred_element_type=jnp.float32)
            + jnp.dot(saf, af_ref[w], preferred_element_type=jnp.float32)
        )

        def add_spill(p):
            return (
                p
                + jnp.dot(sbs_ref[...], bs_ref[w], preferred_element_type=jnp.float32)
                + jnp.dot(sas_ref[...], as_ref[w], preferred_element_type=jnp.float32)
            )

        part = lax.cond(spill_ref[0] != 0, add_spill, lambda p: p, part)
        anc = anchor_ref[w].astype(jnp.float32)
        a_re, a_im = anc[:, :half], anc[:, half:]
        p_re, p_im = part[:, :half], part[:, half:]
        c_re = (a_re * p_re + a_im * p_im).astype(jnp.bfloat16)
        c_im = (a_im * p_re - a_re * p_im).astype(jnp.bfloat16)
        corr_ref[w] = jnp.dot(c_re, t_re, preferred_element_type=jnp.float32) + jnp.dot(
            c_im, t_im, preferred_element_type=jnp.float32
        )


def halo_cross(spill, anchors, own, sels, bufs, transform):
    wins, slots, width = anchors.shape
    lag_count = transform.shape[1]
    group = min(128, slots)
    row_spec = pl.BlockSpec((wins, group, width), lambda i, s: (0, i, 0))
    sel_specs = [pl.BlockSpec((group, sel.shape[1]), lambda i, s: (i, 0)) for sel in sels]
    buf_specs = [pl.BlockSpec(buf.shape, lambda i, s: (0, 0, 0)) for buf in bufs]
    grid_spec = pltpu.PrefetchScalarGridSpec(
        num_scalar_prefetch=1,
        grid=(slots // group,),
        in_specs=[row_spec, row_spec] + sel_specs + buf_specs
        + [pl.BlockSpec(transform.shape, lambda i, s: (0, 0))],
        out_specs=pl.BlockSpec((wins, group, lag_count), lambda i, s: (0, i, 0)),
    )
    return pl.pallas_call(
        cross_kernel,
        grid_spec=grid_spec,
        out_shape=jax.ShapeDtypeStruct((wins, slots, lag_count), jnp.float32),
        compiler_params=pltpu.CompilerParams(vmem_limit_bytes=56 * 1024 * 1024),
    )(spill, anchors, own, *sels, *bufs, transform)


def local(spectra, pair_anchor, pair_offset, pair_partner, pair_count, window_bins, bin_gain):
    block_chans, local_wins, spec_width = spectra.shape
    pair_slots = pair_anchor.shape[0]
    fast_rows = (block_chans // 2 + 15) // 16 * 16
    spill_rows = block_chans - fast_rows

    table = jnp.concatenate([pair_offset, pair_partner, pair_count])
    table_before, table_after = ring_exchange(table, table, "chan")

    def needs_of(tab):
        return block_needs(tab[:pair_slots], tab[pair_slots:2 * pair_slots], tab[2 * pair_slots], block_chans)

    own_minus, own_plus, own_pos_minus, own_pos_plus = needs_of(table)
    up_need, _, up_pos, _ = needs_of(table_after)
    _, down_need, _, down_pos = needs_of(table_before)
    own_most = jnp.maximum(jnp.sum(own_minus, dtype=jnp.int32), jnp.sum(own_plus, dtype=jnp.int32))
    need_most = lax.pmax(own_most.astype(jnp.float32), "chan")

    white = whiten(spectra)

    def send_selector(need, pos, first, rows):
        return onehot(pos - first, rows, need).T.astype(jnp.bfloat16)

    def gather_rows(first, rows):
        up_rows = jnp.einsum("jc,cwf->wjf", send_selector(up_need, up_pos, first, rows), white,
                             preferred_element_type=jnp.bfloat16)
        down_rows = jnp.einsum("jc,cwf->wjf", send_selector(down_need, down_pos, first, rows), white,
                               preferred_element_type=jnp.bfloat16)
        return ring_exchange(up_rows, down_rows, "chan")

    before_fast, after_fast = gather_rows(0, fast_rows)
    spill = need_most > fast_rows

    def do_spill(_):
        return gather_rows(fast_rows, spill_rows)

    def no_spill(_):
        empty = jnp.zeros((local_wins, spill_rows, spec_width), jnp.bfloat16)
        return empty, empty

    before_spill, after_spill = lax.cond(spill, do_spill, no_spill, 0)

    transform = lag_table(spec_width // 2, LAG)
    lag_count = transform.shape[1]
    live_count = pair_count[0]
    slot_ids = lax.broadcasted_iota(jnp.int32, (pair_slots,), 0)
    live = slot_ids < live_count

    def pick(selector, rows):
        return jnp.einsum("sc,cwf->wsf", selector.astype(jnp.bfloat16), rows, preferred_element_type=jnp.bfloat16)

    anchors = pick(onehot(pair_anchor, block_chans, live), white)
    own = pick(onehot(pair_partner, block_chans, live & (pair_offset == 1)), white)
    own_hit = onehot(pair_partner, block_chans, live)
    before_row = jnp.sum(jnp.where(own_hit, own_pos_minus[None, :], 0), axis=1)
    after_row = jnp.sum(jnp.where(own_hit, own_pos_plus[None, :], 0), axis=1)
    use_before = live & (pair_offset == 0)
    use_after = live & (pair_offset == 2)
    sels = [
        onehot(before_row, fast_rows, use_before).astype(jnp.bfloat16),
        onehot(after_row, fast_rows, use_after).astype(jnp.bfloat16),
        onehot(before_row - fast_rows, spill_rows, use_before).astype(jnp.bfloat16),
        onehot(after_row - fast_rows, spill_rows, use_after).astype(jnp.bfloat16),
    ]
    corr_full = halo_cross(
        spill.astype(jnp.int32).reshape(1), anchors, own, sels,
        [before_fast, after_fast, before_spill, after_spill], transform,
    )
    corr_all = corr_full.astype(jnp.bfloat16).astype(jnp.float32)
    running = jnp.sum(corr_full, axis=0)

    ref_sum = butterfly_sum(running, "win")
    norm_scale = jnp.sqrt(jnp.float32(local_wins * lax.axis_size("win")))
    ref_stack = jnp.where(live[:, None], ref_sum / norm_scale, 0.0)
    window_gain = window_gains(window_bins, bin_gain)
    numerator, denominator = window_weights_wm(corr_all, ref_sum, window_gain)
    numerator, denominator = butterfly_sum((numerator, denominator), "win")
    restack = jnp.where(live[:, None], norm_scale * numerator / denominator[:, None], 0.0)
    return (ref_stack, restack)


def solution(mesh):
    in_specs = (
        P(("days", "chan"), "win", None),
        P("chan"),
        P("chan"),
        P("chan"),
        P("chan"),
        P(("days", "win")),
        P(),
    )
    out_specs = (P(("days", "chan"), None), P(("days", "chan"), None))
    return jax.shard_map(local, mesh=mesh, in_specs=in_specs, out_specs=out_specs, check_vma=False)
```

profile of v0, /device:TPU:0, one launch (start us, length us, event | category | flops | bytes accessed | tf_op | source)
XLA Modules:
  0.0 228.3 jit_solution(11828801707618532497)
XLA Ops:
  0.6 0.0 copy-start.2
  1.4 0.8 constant_dynamic-update-slice_fusion.2
  2.3 0.7 constant_dynamic-update-slice_fusion.1
  3.0 3.0 %collective-permute-start.4 = (s32[1025]{0:T(1024)S(1)}, s32[1025]{0:T(1024)S(1)}, u32[]{:S(2)}, u32[]{:S(2)}) collective-permute-start(s32[1025]{0:T(1024)S(1)} %constant_dynamic-update-slice_fusion), channel_id=1, source_target_pairs={{0,4},{4,8},{8,12},{12,0},{1,5},{5,9},{9,13},{13,1},{2,6},{6,10},{... | collective-permute-start | bytes 12308 | tf_op jit(solution)/shard_map/ppermute | solution.py:81
  6.0 2.1 collective-permute-start.2
  8.1 0.7 compare_and_fusion
  8.8 0.9 fusion.20
  9.7 0.7 convert_reduce_fusion
  10.4 7.9 %fusion.10 = f32[320,8]{0,1:T(8,128)S(1)} fusion(bf16[320,8,1024]{2,1,0:T(8,128)(2,1)} %param.9), kind=kLoop, calls=%fused_computation.16 | loop fusion | flops 7861760 | bytes 5253120 | tf_op jit(solution)/shard_map/reduce_sum | solution.py:17
  18.4 6.5 %fusion.11 = bf16[320,8,1024]{2,0,1:T(8,128)(2,1)} fusion(f32[320,8]{0,1:T(8,128)S(1)} %add_rsqrt_fusion, bf16[320,8,1024]{2,1,0:T(8,128)(2,1)S(1)} %copy-done.2), kind=kLoop, calls=%fused_computation.17 | loop fusion | flops 7864320 | bytes 10496000 | tf_op jit(solution)/shard_map/convert_element_type | solution.py:18
  25.0 0.3 reduce-window.36
  25.3 0.1 slice.61
  25.4 0.1 slice_reduce_fusion.2
  25.5 0.1 add_bitcast_fusion.2
  25.6 0.3 reduce-window.34
  25.9 0.1 slice.58
  26.0 1.3 fusion.43
  27.3 0.7 pad_maximum_fusion.t_ref
  28.1 0.1 slice_reduce_fusion.3
  29.5 0.5 slice.80
  30.1 0.6 fusion.58
  30.7 0.2 fusion.29
  30.9 0.3 reduce-window.50
  31.2 0.1 slice.73
  31.3 0.1 slice_reduce_fusion
  31.5 0.1 add_bitcast_fusion
  31.5 0.5 slice.77
  32.1 0.6 fusion.57
  32.7 0.2 fusion.27
  32.9 0.3 reduce-window.48
  33.2 0.1 slice.67
  33.3 0.1 slice_reduce_fusion.1
  33.5 0.1 add_bitcast_fusion.1
  33.5 4.7 %convolution_bitcast_fusion.5 = bf16[8,160,1024]{2,1,0:T(8,128)(2,1)S(1)} fusion(bf16[320,8,1024]{2,0,1:T(8,128)(2,1)} %fusion.11, s32[320]{0:T(512)S(1)} %slice_add_fusion.1, pred[320]{0:T(512)(128)(4,1)S(1)} %fusion.27), kind=kOutput, calls=%fused_computation.27 | convolution fusion | flops 838963200 | bytes 7865920 | tf_op jit(solution)/shard_map/jc,cwf->wjf/dot_general | solution.py:187
  38.3 0.1 collective-permute-start.3
  38.4 3.6 %convolution_bitcast_fusion.4 = bf16[8,160,1024]{2,1,0:T(8,128)(2,1)} fusion(bf16[320,8,1024]{2,0,1:T(8,128)(2,1)S(1)} %copy-done, s32[320]{0:T(512)S(1)} %slice_add_fusion, pred[320]{0:T(512)(128)(4,1)S(1)} %fusion.29), kind=kOutput, calls=%fused_computation.26 | convolution fusion | flops 838963200 | bytes 7865920 | tf_op jit(solution)/shard_map/jc,cwf->wjf/dot_general | solution.py:189
  42.0 3.8 %collective-permute-start.5 = (bf16[8,160,1024]{2,1,0:T(8,128)(2,1)}, bf16[8,160,1024]{2,1,0:T(8,128)(2,1)}, u32[]{:S(2)}, u32[]{:S(2)}) collective-permute-start(bf16[8,160,1024]{2,1,0:T(8,128)(2,1)} %convolution_bitcast_fusion.4), channel_id=1, source_target_pairs={{4,0},{8,4},{12,8},{0,12},{5,1},{9,5},{13,9},{1,13},{6,2},{10,6},{... | collective-permute-start | bytes 7864328 | tf_op jit(solution)/shard_map/ppermute | solution.py:81
  45.8 111.4 %pmax.7 = f32[]{:T(128)} all-reduce(f32[]{:T(128)S(6)} %convert_element_type.51), channel_id=1, replica_groups=mesh['days'=2,'chan'=4,'win'=4] {'chan'}, use_global_device_ids=true, to_apply=%region_4.5 | all-reduce | flops 1 | bytes 8 | tf_op jit(solution)/shard_map/pmax | solution.py:179
  157.9 0.1 add_bitcast_fusion.3
  158.0 0.2 select_reduce_fusion
  158.2 1.5 fusion.35
  159.7 10.4 %convolution_bitcast_fusion.2.own_ref = bf16[8,512,1024]{2,1,0:T(8,128)(2,1)} fusion(bf16[320,8,1024]{2,0,1:T(8,128)(2,1)} %fusion.11, s32[512]{0:T(512)S(1)} %copy-done.3, pred[512]{0:T(512)(128)(4,1)S(1)} %get-tuple-element.33), kind=kOutput, calls=%fused_computation.18 | convolution fusion | flops 2684682240 | bytes 13634048 | tf_op jit(solution)/shard_map/sc,cwf->wsf/dot_general | solution.py:212
  170.1 7.1 %convolution_bitcast_fusion.3.anchor_ref = bf16[8,512,1024]{2,1,0:T(8,128)(2,1)} fusion(bf16[320,8,1024]{2,0,1:T(8,128)(2,1)S(1)} %bitcast.59, s32[512]{0:T(512)S(1)} %copy-done.4, pred[512]{0:T(512)(128)(4,1)S(1)} %iota_compare_fusion.15), kind=kOutput, calls=%fused_computation.19 | convolution fusion | flops 2684682240 | bytes 13634048 | tf_op jit(solution)/shard_map/sc,cwf->wsf/dot_general | solution.py:212
  177.2 3.7 %conditional.1 = (bf16[8,160,1024]{2,1,0:T(8,128)(2,1)}, bf16[8,160,1024]{2,1,0:T(8,128)(2,1)}) conditional(s32[]{:T(128)} %convert_element_type.52, () %tuple.16, (s32[320]{0:T(512)S(1)}, pred[320]{0:T(512)(128)(4,1)S(1)}, bf16[320,8,1024]{2,0,1:T(8,128)(2,1)S(1)}, s32[320]{0:T(512)S(1)}, pred[320]{0:T(512)(128)(4,1)S(1)}) %tuple.35), branch_computations={%region_18.19_spmd, %region_19.20_spmd} | conditional | flops 1677927040 | bytes 36708576 | solution.py:203
  177.2 1.9 broadcast.141
  179.1 1.8 broadcast.141.clone
  180.9 22.2 %shard_map.86 = f32[8,512,128]{2,1,0:T(8,128)} custom-call(s32[1]{0:T(128)} %bitcast.5.spill_ref, bf16[8,512,1024]{2,1,0:T(8,128)(2,1)} %convolution_bitcast_fusion.3.anchor_ref, bf16[8,512,1024]{2,1,0:T(8,128)(2,1)} %convolution_bitcast_fusion.2.own_ref, bf16[512,160]{1,0:T(8,128)(2,1)} %get-tuple-element.41.sbf_ref, ...), custom_call_target="tpu_custom_call" | custom-call | tf_op jit(solution)/shard_map/pallas_call | solution.py:155
  203.1 1.9 reduce_sum.113
  205.0 0.1 collective-permute-start.6
  205.1 1.5 collective-permute-done.6
  206.7 1.6 collective-permute-start.7
  208.2 0.2 select_reduce_fusion.2
  208.4 6.7 %collective-permute-done.7 = f32[512,128]{1,0:T(8,128)S(1)} collective-permute-done((f32[512,128]{1,0:T(8,128)S(1)}, f32[512,128]{1,0:T(8,128)S(1)}, u32[]{:S(2)}, u32[]{:S(2)}) %collective-permute-start.7) | collective-permute-done | bytes 262176 | tf_op jit(solution)/shard_map/ppermute | solution.py:72
  215.1 0.1 multiply_reduce_fusion
  215.2 1.2 fusion.12
  216.4 0.1 fusion.59
  216.5 0.7 fusion.14
  217.2 0.1 collective-permute-start.8
  217.3 1.5 collective-permute-done.8
  218.8 1.6 collective-permute-start.9
  220.4 1.2 collective-permute-done.10
  221.6 0.5 collective-permute-start.11
  222.1 5.2 %collective-permute-done.11 = f32[512]{0:T(512)S(1)} collective-permute-done((f32[512]{0:T(512)S(1)}, f32[512]{0:T(512)S(1)}, u32[]{:S(2)}, u32[]{:S(2)}) %collective-permute-start.11) | collective-permute-done | bytes 2080 | tf_op jit(solution)/shard_map/ppermute | solution.py:72
  227.3 1.0 divide_select_fusion
  (53 shorter events, 0.4 us)
Async XLA Ops:
  0.6 17.8 %copy-start.2 = (bf16[320,8,1024]{2,1,0:T(8,128)(2,1)S(1)}, bf16[320,8,1024]{2,1,0:T(8,128)(2,1)}, u32[]{:S(2)}) copy-start(bf16[320,8,1024]{2,1,0:T(8,128)(2,1)} %param.9) | copy-start | bytes 15728644
  3.0 26.6 %collective-permute-start.4 = (s32[1025]{0:T(1024)S(1)}, s32[1025]{0:T(1024)S(1)}, u32[]{:S(2)}, u32[]{:S(2)}) collective-permute-start(s32[1025]{0:T(1024)S(1)} %constant_dynamic-update-slice_fusion), channel_id=1, source_target_pairs={{0,4},{4,8},{8,12},{12,0},{1,5},{5,9},{9,13},{13,1},{2,6},{6,10},{... | collective-permute-start | bytes 12308 | tf_op jit(solution)/shard_map/ppermute | solution.py:81
  6.0 25.5 %collective-permute-start.2 = (s32[1025]{0:T(1024)S(1)}, s32[1025]{0:T(1024)S(1)}, u32[]{:S(2)}, u32[]{:S(2)}) collective-permute-start(s32[1025]{0:T(1024)S(1)} %constant_dynamic-update-slice_fusion), channel_id=1, source_target_pairs={{4,0},{8,4},{12,8},{0,12},{5,1},{9,5},{13,9},{1,13},{6,2},{10,6},{... | collective-permute-start | bytes 12308 | tf_op jit(solution)/shard_map/ppermute | solution.py:81
  33.3 5.0 %copy-start = (bf16[320,8,1024]{2,0,1:T(8,128)(2,1)S(1)}, bf16[320,8,1024]{2,0,1:T(8,128)(2,1)}, u32[]{:S(2)}) copy-start(bf16[320,8,1024]{2,0,1:T(8,128)(2,1)} %fusion.11) | copy-start | bytes 15728644
  38.3 119.7 %copy-start.3 = (s32[512]{0:T(512)S(1)}, s32[512]{0:T(512)}, u32[]{:S(2)}) copy-start(s32[512]{0:T(512)} %param.12) | copy-start | bytes 6148
  38.3 142.6 %collective-permute-start.3 = (bf16[8,160,1024]{2,1,0:T(8,128)(2,1)S(1)}, bf16[8,160,1024]{2,1,0:T(8,128)(2,1)}, u32[]{:S(2)}, u32[]{:S(2)}) collective-permute-start(bf16[8,160,1024]{2,1,0:T(8,128)(2,1)S(1)} %convolution_bitcast_fusion.5), channel_id=1, source_target_pairs={{0,4},{4,8},{8,12},{12,0},{1,5},{5,9},{9,13},{13,1},{2,6},{6,10},{... | collective-permute-start | bytes 7864328 | tf_op jit(solution)/shard_map/ppermute | solution.py:81
  42.0 138.9 %collective-permute-start.5 = (bf16[8,160,1024]{2,1,0:T(8,128)(2,1)}, bf16[8,160,1024]{2,1,0:T(8,128)(2,1)}, u32[]{:S(2)}, u32[]{:S(2)}) collective-permute-start(bf16[8,160,1024]{2,1,0:T(8,128)(2,1)} %convolution_bitcast_fusion.4), channel_id=1, source_target_pairs={{4,0},{8,4},{12,8},{0,12},{5,1},{9,5},{13,9},{1,13},{6,2},{10,6},{... | collective-permute-start | bytes 7864328 | tf_op jit(solution)/shard_map/ppermute | solution.py:81
  158.2 11.9 %slice-start = ((s8[5242880]{0:T(1024)(128)(4,1)}), s8[4194304]{0:T(1024)(128)(4,1)S(1)}, s32[]{:S(2)}) async-start(s8[5242880]{0:T(1024)(128)(4,1)} %bitcast.58), calls=%async_computation | async-start | bytes 8388608
  159.7 10.4 %slice-start.1 = ((s8[5242880]{0:T(1024)(128)(4,1)}), s8[1048576]{0:T(1024)(128)(4,1)S(1)}, s32[]{:S(2)}) async-start(s8[5242880]{0:T(1024)(128)(4,1)} %bitcast.58), calls=%async_computation.1 | async-start | bytes 2097152
  159.7 10.4 %copy-start.4 = (s32[512]{0:T(512)S(1)}, s32[512]{0:T(512)}, u32[]{:S(2)}) copy-start(s32[512]{0:T(512)} %param.10) | copy-start | bytes 6148
  180.9 27.3 %copy-start.5 = (f32[8]{0:T(128)S(1)}, f32[8]{0:T(128)}, u32[]{:S(2)}) copy-start(f32[8]{0:T(128)} %param.15) | copy-start | bytes 100
  180.9 27.3 %copy-start.6 = (s32[8]{0:T(128)S(1)}, s32[8]{0:T(128)}, u32[]{:S(2)}) copy-start(s32[8]{0:T(128)} %param.14) | copy-start | bytes 100
  203.1 12.1 %copy-start.1 = (f32[8,512,128]{2,1,0:T(8,128)S(1)}, f32[8,512,128]{2,1,0:T(8,128)}, u32[]{:S(2)}) copy-start(f32[8,512,128]{2,1,0:T(8,128)} %shard_map.86) | copy-start | bytes 6291460
  205.0 1.6 collective-permute-start.6
  206.7 8.4 %collective-permute-start.7 = (f32[512,128]{1,0:T(8,128)S(1)}, f32[512,128]{1,0:T(8,128)S(1)}, u32[]{:S(2)}, u32[]{:S(2)}) collective-permute-start(f32[512,128]{1,0:T(8,128)S(1)} %add.73), channel_id=1, source_target_pairs={{0,2},{1,3},{2,0},{3,1},{4,6},{5,7},{6,4},{7,5},{8,10},{9,11},{10,... | collective-permute-start | bytes 786440 | tf_op jit(solution)/shard_map/ppermute | solution.py:72
  217.2 1.6 collective-permute-start.8
  218.8 8.5 %collective-permute-start.9 = (f32[512,128]{1,0:T(8,128)S(1)}, f32[512,128]{1,0:T(8,128)S(1)}, u32[]{:S(2)}, u32[]{:S(2)}) collective-permute-start(f32[512,128]{1,0:T(8,128)S(1)} %add.79), channel_id=1, source_target_pairs={{0,2},{1,3},{2,0},{3,1},{4,6},{5,7},{6,4},{7,5},{8,10},{9,11},{10,... | collective-permute-start | bytes 786440 | tf_op jit(solution)/shard_map/ppermute | solution.py:72
  220.4 1.2 collective-permute-start.10
  221.6 5.7 %collective-permute-start.11 = (f32[512]{0:T(512)S(1)}, f32[512]{0:T(512)S(1)}, u32[]{:S(2)}, u32[]{:S(2)}) collective-permute-start(f32[512]{0:T(512)S(1)} %add.81), channel_id=1, source_target_pairs={{0,2},{1,3},{2,0},{3,1},{4,6},{5,7},{6,4},{7,5},{8,10},{9,11},{10,... | collective-permute-start | bytes 6152 | tf_op jit(solution)/shard_map/ppermute | solution.py:72
where the time goes:
time: 229 us; the launch traced here: 228 us
  blocking collectives  111 us (48%)
  other arithmetic  29.2 us (13%)
  matrix products  25.8 us (11%)
  Pallas kernels  22.2 us (10%)
  waiting for transfers between devices  16.1 us (7%)
  starting transfers between devices  12.8 us (6%)
  local copies, waits for them, and re-layouts  7.12 us (3%)
  between operations  3.66 us (2%)
    pmax x1, blocking collectives, local(): need_most = lax.pmax(own_most.astype(jnp.float32), 'chan')  111 us
    pallas_call x1, Pallas kernels, halo_cross(): pl.pallas_call(cross_kernel, grid_spec=grid_spec, out_shape=jax.ShapeDtyp...  22.2 us
    dot_general x2, matrix products, pick(): jnp.einsum('sc,cwf->wsf', selector.astype(jnp.bfloat16), rows, preferred_...  17.5 us
    ppermute x6, waiting for transfers between devices, butterfly_sum(): value = jax.tree.map(jnp.add, value, lax.ppermute(value, axis, pairs))  16.1 us
    reduce_sum x1, other arithmetic, whiten(): power_mean = jnp.mean(spectra_f * spectra_f, axis=-1, keepdims=True)  7.95 us
    convert_element_type x1, other arithmetic, whiten(): return (spectra_f * lax.rsqrt(power_mean + EPS_POWER)).astype(jnp.bfloat16)  6.55 us
    ppermute x2, starting transfers between devices, ring_exchange(): lax.ppermute(down_rows, axis, down)  5.89 us
    dot_general x1, matrix products, gather_rows(): jnp.einsum('jc,cwf->wjf', send_selector(up_need, up_pos, first, rows), wh...  4.73 us
  transfers between devices with their start and end apart: 10, of which 5 were waited for; matrix products, arithmetic and copies ran while one was open for 21% of the time, Pallas kernels for 0%

commit v1 on v0

--- a/solution.py
+++ b/solution.py
@@ -79,6 +79,21 @@
     up = [(i, (i + 1) % peers) for i in range(peers)]
     down = [(j, i) for i, j in up]
     return lax.ppermute(up_rows, axis, up), lax.ppermute(down_rows, axis, down)
+
+
+def gather_blocks(row, axis):
+    peers = lax.axis_size(axis)
+    if peers & (peers - 1):
+        return lax.all_gather(row, axis)
+    me = lax.axis_index(axis)
+    acc = row[None]
+    step = 1
+    while step < peers:
+        pairs = [(i, i ^ step) for i in range(peers)]
+        got = lax.ppermute(acc, axis, pairs)
+        acc = jnp.where((me & step) == 0, jnp.concatenate([acc, got]), jnp.concatenate([got, acc]))
+        step *= 2
+    return acc
 
 
 def onehot(index, size, mask):
@@ -138,13 +153,15 @@
         )
 
 
-def halo_cross(spill, anchors, own, sels, bufs, transform):
-    wins, slots, width = anchors.shape
+def halo_cross(spill, chunk, wins, anchors, own, sels, bufs, transform):
+    _, slots, width = anchors.shape
     lag_count = transform.shape[1]
     group = min(128, slots)
-    row_spec = pl.BlockSpec((wins, group, width), lambda i, s: (0, i, 0))
+    row_spec = pl.BlockSpec((wins, group, width), lambda i, s: (chunk, i, 0))
     sel_specs = [pl.BlockSpec((group, sel.shape[1]), lambda i, s: (i, 0)) for sel in sels]
-    buf_specs = [pl.BlockSpec(buf.shape, lambda i, s: (0, 0, 0)) for buf in bufs]
+    buf_specs = [
+        pl.BlockSpec((wins,) + buf.shape[1:], lambda i, s, c=(chunk if buf.shape[0] > wins else 0): (c, 0, 0)) for buf in bufs
+    ]
     grid_spec = pltpu.PrefetchScalarGridSpec(
         num_scalar_prefetch=1,
         grid=(slots // group,),
@@ -166,8 +183,12 @@
     fast_rows = (block_chans // 2 + 15) // 16 * 16
     spill_rows = block_chans - fast_rows
 
+    blocks = lax.axis_size("chan")
+    block = lax.axis_index("chan")
     table = jnp.concatenate([pair_offset, pair_partner, pair_count])
-    table_before, table_after = ring_exchange(table, table, "chan")
+    tables = gather_blocks(table, "chan")
+    table_before = tables[(block + blocks - 1) % blocks]
+    table_after = tables[(block + 1) % blocks]
 
     def needs_of(tab):
         return block_needs(tab[:pair_slots], tab[pair_slots:2 * pair_slots], tab[2 * pair_slots], block_chans)
@@ -175,26 +196,31 @@
     own_minus, own_plus, own_pos_minus, own_pos_plus = needs_of(table)
     up_need, _, up_pos, _ = needs_of(table_after)
     _, down_need, _, down_pos = needs_of(table_before)
-    own_most = jnp.maximum(jnp.sum(own_minus, dtype=jnp.int32), jnp.sum(own_plus, dtype=jnp.int32))
-    need_most = lax.pmax(own_most.astype(jnp.float32), "chan")
+    all_needs = jax.vmap(needs_of)(tables)
+    need_most = jnp.maximum(
+        jnp.max(jnp.sum(all_needs[0], axis=1, dtype=jnp.int32)),
+        jnp.max(jnp.sum(all_needs[1], axis=1, dtype=jnp.int32)),
+    )
 
     white = whiten(spectra)
 
     def send_selector(need, pos, first, rows):
         return onehot(pos - first, rows, need).T.astype(jnp.bfloat16)
 
-    def gather_rows(first, rows):
-        up_rows = jnp.einsum("jc,cwf->wjf", send_selector(up_need, up_pos, first, rows), white,
+    def gather_rows(first, rows, source):
+        up_rows = jnp.einsum("jc,cwf->wjf", send_selector(up_need, up_pos, first, rows), source,
                              preferred_element_type=jnp.bfloat16)
-        down_rows = jnp.einsum("jc,cwf->wjf", send_selector(down_need, down_pos, first, rows), white,
+        down_rows = jnp.einsum("jc,cwf->wjf", send_selector(down_need, down_pos, first, rows), source,
                                preferred_element_type=jnp.bfloat16)
         return ring_exchange(up_rows, down_rows, "chan")
 
-    before_fast, after_fast = gather_rows(0, fast_rows)
+    chunks = 2 if local_wins % 2 == 0 else 1
+    chunk_wins = local_wins // chunks
+    fast = [gather_rows(0, fast_rows, white[:, c * chunk_wins:(c + 1) * chunk_wins]) for c in range(chunks)]
     spill = need_most > fast_rows
 
     def do_spill(_):
-        return gather_rows(fast_rows, spill_rows)
+        return gather_rows(fast_rows, spill_rows, white)
 
     def no_spill(_):
         empty = jnp.zeros((local_wins, spill_rows, spec_width), jnp.bfloat16)
@@ -224,11 +250,14 @@
         onehot(before_row - fast_rows, spill_rows, use_before).astype(jnp.bfloat16),
         onehot(after_row - fast_rows, spill_rows, use_after).astype(jnp.bfloat16),
     ]
-    corr_full = halo_cross(
-        spill.astype(jnp.int32).reshape(1), anchors, own, sels,
-        [before_fast, after_fast, before_spill, after_spill], transform,
-    )
-    corr_all = corr_full.astype(jnp.bfloat16).astype(jnp.float32)
+    corr_full = jnp.concatenate([
+        halo_cross(
+            spill.astype(jnp.int32).reshape(1), c, chunk_wins, anchors, own, sels,
+            [fast[c][0], fast[c][1], before_spill, after_spill], transform,
+        )
+        for c in range(chunks)
+    ])
+    corr_all = lax.reduce_precision(corr_full, exponent_bits=8, mantissa_bits=7)
     running = jnp.sum(corr_full, axis=0)
 
     ref_sum = butterfly_sum(running, "win")

time: 229 us -> 200 us (0.87)
  blocking collectives: 111 us -> 0 us
  waiting for transfers between devices: 16.1 us -> 85.2 us
  matrix products: 25.8 us -> 31.7 us
  starting transfers between devices: 12.8 us -> 17.2 us
  other arithmetic: 29.2 us -> 32.5 us
  Pallas kernels: 22.2 us -> 24.8 us
    pmax x1 -> x0, blocking collectives: 111 us -> none  [local(): need_most = lax.pmax(own_most.astype(jnp.float32), 'chan')]
    ppermute x2, waiting for transfers between devices: 0.01 us -> 67 us  [ring_exchange(): lax.ppermute(down_rows, axis, down)]
    ppermute x0 -> x2, starting transfers between devices: none -> 5.74 us  [gather_blocks(): got = lax.ppermute(acc, axis, pairs)]
    dot_general x2, matrix products: 17.5 us -> 20.4 us  [pick(): jnp.einsum('sc,cwf->wsf', selector.astype(jnp.bfloat16), rows, preferred_...]
    ppermute x2, starting transfers between devices: 3.08 us -> 0.18 us  [ring_exchange(): lax.ppermute(up_rows, axis, up)]
    pallas_call x1 -> x2, Pallas kernels: 22.2 us -> 24.8 us  [halo_cross(): pl.pallas_call(cross_kernel, grid_spec=grid_spec, out_shape=jax.ShapeDtyp...]
    dot_general x1 -> x2, matrix products: 4.73 us -> 6.27 us  [gather_rows(): jnp.einsum('jc,cwf->wjf', send_selector(up_need, up_pos, first, rows), so...]
    dot_general x1 -> x2, matrix products: 3.61 us -> 5.01 us  [gather_rows(): jnp.einsum('jc,cwf->wjf', send_selector(down_need, down_pos, first, rows)...]
  transfers between devices with their start and end apart: 10 -> 12, of which waited for: 5 -> 9; matrix products, arithmetic and copies ran while one was open for 21% -> 23% of each run, Pallas kernels for 0% -> 6%
where the time goes in v1:
time: 200 us
  waiting for transfers between devices  85.2 us (43%)
  other arithmetic  32.5 us (16%)
  matrix products  31.7 us (16%)
  Pallas kernels  24.8 us (12%)
  starting transfers between devices  17.2 us (9%)
  local copies, waits for them, and re-layouts  5.42 us (3%)
  between operations  3.12 us (2%)
    ppermute x2, waiting for transfers between devices, ring_exchange(): lax.ppermute(down_rows, axis, down)  67 us
    pallas_call x2, Pallas kernels, halo_cross(): pl.pallas_call(cross_kernel, grid_spec=grid_spec, out_shape=jax.ShapeDtyp...  24.8 us
    dot_general x2, matrix products, pick(): jnp.einsum('sc,cwf->wsf', selector.astype(jnp.bfloat16), rows, preferred_...  20.4 us
    ppermute x6, waiting for transfers between devices, butterfly_sum(): value = jax.tree.map(jnp.add, value, lax.ppermute(value, axis, pairs))  16.1 us
    reduce_sum x1, other arithmetic, whiten(): power_mean = jnp.mean(spectra_f * spectra_f, axis=-1, keepdims=True)  7.95 us
    ppermute x2, starting transfers between devices, ring_exchange(): lax.ppermute(down_rows, axis, down)  7.52 us
    convert_element_type x1, other arithmetic, whiten(): return (spectra_f * lax.rsqrt(power_mean + EPS_POWER)).astype(jnp.bfloat16)  6.48 us
    dot_general x2, matrix products, gather_rows(): jnp.einsum('jc,cwf->wjf', send_selector(up_need, up_pos, first, rows), so...  6.27 us
  transfers between devices with their start and end apart: 12, of which 9 were waited for; matrix products, arithmetic and copies ran while one was open for 23% of the time, Pallas kernels for 6%

profile of v1, /device:TPU:0, one launch (start us, length us, event | category | flops | bytes accessed | tf_op | source)
XLA Modules:
  0.0 200.0 jit_solution(8766539990079830483)
XLA Ops:
  1.4 0.9 pad_add_fusion
  2.3 3.1 %collective-permute-start.2 = (s32[1,1025]{1,0:T(1,128)S(1)}, s32[1,1025]{1,0:T(1,128)S(1)}, u32[]{:S(2)}, u32[]{:S(2)}) collective-permute-start(s32[1,1025]{1,0:T(1,128)S(1)} %broadcast_in_dim.45), channel_id=1, source_target_pairs={{0,4},{4,0},{8,12},{12,8},{1,5},{5,1},{9,13},{13,9},{2,6},{6,2},{1... | collective-permute-start | bytes 12308 | tf_op jit(solution)/shard_map/ppermute | solution.py:93
  5.4 7.9 %fusion.10 = f32[320,8]{0,1:T(8,128)S(1)} fusion(bf16[320,8,1024]{2,1,0:T(8,128)(2,1)} %param.9), kind=kLoop, calls=%fused_computation.16 | loop fusion | flops 7861760 | bytes 5253120 | tf_op jit(solution)/shard_map/reduce_sum | solution.py:17
  13.4 6.5 %fusion.11 = bf16[320,8,1024]{2,0,1:T(8,128)(2,1)} fusion(f32[320,8]{0,1:T(8,128)S(1)} %add_rsqrt_fusion, bf16[320,8,1024]{2,1,0:T(8,128)(2,1)S(1)} %copy-done.1), kind=kLoop, calls=%fused_computation.17 | loop fusion | flops 7864320 | bytes 10496000 | tf_op jit(solution)/shard_map/convert_element_type | solution.py:18
  19.9 0.2 fusion.26
  20.1 0.3 reduce-window.36
  20.5 0.1 slice.85
  20.6 0.1 slice_reduce_fusion.3
  20.8 0.3 reduce-window.34
  21.2 0.1 slice_reduce_fusion.4
  21.4 0.2 select_reduce_fusion
  21.7 1.6 fusion.36
  23.3 2.7 %collective-permute-start.3 = (s32[2,1025]{1,0:T(2,128)S(1)}, s32[2,1025]{1,0:T(2,128)S(1)}, u32[]{:S(2)}, u32[]{:S(2)}) collective-permute-start(s32[2,1025]{1,0:T(2,128)S(1)} %add_select_fusion.1), channel_id=1, source_target_pairs={{0,8},{4,12},{8,0},{12,4},{1,9},{5,13},{9,1},{13,5},{2,10},{6,14},... | collective-permute-start | bytes 24608 | tf_op jit(solution)/shard_map/ppermute | solution.py:93
  26.0 1.1 fusion.44
  27.2 0.8 collective-permute-done.3
  28.0 0.1 slice_reduce_fusion
  28.1 0.7 fusion.69
  28.8 0.1 fusion.70
  28.9 1.3 fusion.66
  30.2 0.2 fusion.30
  30.4 0.3 reduce-window.50
  30.8 0.1 slice_reduce_fusion.1
  31.0 0.2 fusion.28
  31.2 0.3 reduce-window.48
  31.6 0.1 slice_reduce_fusion.2
  31.8 4.1 %convolution_bitcast_fusion.7 = bf16[4,160,1024]{2,1,0:T(8,128)(2,1)} fusion(bf16[320,8,1024]{2,0,1:T(8,128)(2,1)} %fusion.11, s32[320]{0:T(512)S(1)} %slice_add_fusion.1, pred[320]{0:T(512)(128)(4,1)S(1)} %fusion.28), kind=kOutput, calls=%fused_computation.32 | convolution fusion | flops 419532800 | bytes 6555200 | tf_op jit(solution)/shard_map/jc,cwf->wjf/dot_general | solution.py:211
  35.9 2.8 %convolution_bitcast_fusion.6 = bf16[4,160,1024]{2,1,0:T(8,128)(2,1)S(1)} fusion(bf16[320,8,1024]{2,0,1:T(8,128)(2,1)} %fusion.11, s32[320]{0:T(512)S(1)} %slice_add_fusion, pred[320]{0:T(512)(128)(4,1)S(1)} %fusion.30), kind=kOutput, calls=%fused_computation.31 | convolution fusion | flops 419532800 | bytes 6555200 | tf_op jit(solution)/shard_map/jc,cwf->wjf/dot_general | solution.py:213
  38.7 2.2 %convolution_bitcast_fusion.5 = bf16[4,160,1024]{2,1,0:T(8,128)(2,1)} fusion(bf16[320,8,1024]{2,0,1:T(8,128)(2,1)S(1)} %bitcast.69, s32[320]{0:T(512)S(1)} %slice_add_fusion.1, pred[320]{0:T(512)(128)(4,1)S(1)} %fusion.28), kind=kOutput, calls=%fused_computation.30 | convolution fusion | flops 419532800 | bytes 6555200 | tf_op jit(solution)/shard_map/jc,cwf->wjf/dot_general | solution.py:211
  40.9 2.2 %convolution_bitcast_fusion.4 = bf16[4,160,1024]{2,1,0:T(8,128)(2,1)} fusion(bf16[320,8,1024]{2,0,1:T(8,128)(2,1)S(1)} %bitcast.69, s32[320]{0:T(512)S(1)} %slice_add_fusion, pred[320]{0:T(512)(128)(4,1)S(1)} %fusion.30), kind=kOutput, calls=%fused_computation.29 | convolution fusion | flops 419532800 | bytes 6555200 | tf_op jit(solution)/shard_map/jc,cwf->wjf/dot_general | solution.py:213
  43.1 0.1 fusion.65
  43.2 0.8 fusion.15
  44.0 0.1 convert_reduce_fusion
  44.2 0.7 reduce_max.18
  44.9 0.7 reduce_max.19
  47.0 0.2 collective-permute-start.4
  47.2 3.7 %collective-permute-start.5 = (bf16[4,160,1024]{2,1,0:T(8,128)(2,1)S(1)}, bf16[4,160,1024]{2,1,0:T(8,128)(2,1)}, u32[]{:S(2)}, u32[]{:S(2)}) collective-permute-start(bf16[4,160,1024]{2,1,0:T(8,128)(2,1)S(1)} %convolution_bitcast_fusion.6), channel_id=1, source_target_pairs={{4,0},{8,4},{12,8},{0,12},{5,1},{9,5},{13,9},{1,13},{6,2},{10,6},{... | collective-permute-start | bytes 3932168 | tf_op jit(solution)/shard_map/ppermute | solution.py:81
  50.9 3.7 %conditional.1 = (bf16[8,160,1024]{2,1,0:T(8,128)(2,1)}, bf16[8,160,1024]{2,1,0:T(8,128)(2,1)}) conditional(s32[]{:T(128)} %convert_element_type.45, () %tuple.16, (s32[320]{0:T(512)S(1)}, pred[320]{0:T(512)(128)(4,1)S(1)}, bf16[320,8,1024]{2,0,1:T(8,128)(2,1)}, s32[320]{0:T(512)S(1)}, pred[320]{0:T(512)(128)(4,1)S(1)}) %tuple.17), branch_computations={%region_21.22_spmd, %region_22.23_spmd} | conditional | flops 1677927040 | bytes 57680124 | solution.py:229
  50.9 1.8 broadcast.164
  52.7 1.9 broadcast.164.clone
  54.6 3.8 %collective-permute-start.7 = (bf16[4,160,1024]{2,1,0:T(8,128)(2,1)}, bf16[4,160,1024]{2,1,0:T(8,128)(2,1)}, u32[]{:S(2)}, u32[]{:S(2)}) collective-permute-start(bf16[4,160,1024]{2,1,0:T(8,128)(2,1)} %convolution_bitcast_fusion.4), channel_id=1, source_target_pairs={{4,0},{8,4},{12,8},{0,12},{5,1},{9,5},{13,9},{1,13},{6,2},{10,6},{... | collective-permute-start | bytes 3932168 | tf_op jit(solution)/shard_map/ppermute | solution.py:81
  58.4 0.7 pad_maximum_fusion.t_ref
  59.1 10.2 %convolution_bitcast_fusion.2.own_ref = bf16[8,512,1024]{2,1,0:T(8,128)(2,1)} fusion(bf16[320,8,1024]{2,0,1:T(8,128)(2,1)} %fusion.11, s32[512]{0:T(512)S(1)} %copy-done.5, pred[512]{0:T(512)(128)(4,1)S(1)} %get-tuple-element.44), kind=kOutput, calls=%fused_computation.18 | convolution fusion | flops 2684682240 | bytes 13634048 | tf_op jit(solution)/shard_map/sc,cwf->wsf/dot_general | solution.py:238
  69.3 10.2 %convolution_bitcast_fusion.3.anchor_ref = bf16[8,512,1024]{2,1,0:T(8,128)(2,1)} fusion(bf16[320,8,1024]{2,0,1:T(8,128)(2,1)} %fusion.11, s32[512]{0:T(512)S(1)} %copy-done.7, pred[512]{0:T(512)(128)(4,1)S(1)} %iota_compare_fusion.17), kind=kOutput, calls=%fused_computation.19 | convolution fusion | flops 2684682240 | bytes 13634048 | tf_op jit(solution)/shard_map/sc,cwf->wsf/dot_general | solution.py:238
  79.5 1.3 collective-permute-done.4.bf_ref
  80.9 51.4 %collective-permute-done.5.af_ref = bf16[4,160,1024]{2,1,0:T(8,128)(2,1)} collective-permute-done((bf16[4,160,1024]{2,1,0:T(8,128)(2,1)S(1)}, bf16[4,160,1024]{2,1,0:T(8,128)(2,1)}, u32[]{:S(2)}, u32[]{:S(2)}) %collective-permute-start.5) | collective-permute-done | bytes 1310752 | tf_op jit(solution)/shard_map/ppermute | solution.py:81
  132.3 12.4 %shard_map.86 = f32[4,512,128]{2,1,0:T(8,128)} custom-call(s32[1]{0:T(128)} %bitcast.5.spill_ref, bf16[8,512,1024]{2,1,0:T(8,128)(2,1)} %convolution_bitcast_fusion.3.anchor_ref, bf16[8,512,1024]{2,1,0:T(8,128)(2,1)} %convolution_bitcast_fusion.2.own_ref, bf16[512,160]{1,0:T(8,128)(2,1)} %get-tuple-element.51.sbf_ref, ...), custom_call_target="tpu_custom_call" | custom-call | tf_op jit(solution)/shard_map/pallas_call | solution.py:172
  144.7 1.3 reduce_sum.121
  146.1 15.5 %collective-permute-done.7.af_ref = bf16[4,160,1024]{2,1,0:T(8,128)(2,1)} collective-permute-done((bf16[4,160,1024]{2,1,0:T(8,128)(2,1)}, bf16[4,160,1024]{2,1,0:T(8,128)(2,1)}, u32[]{:S(2)}, u32[]{:S(2)}) %collective-permute-start.7) | collective-permute-done | bytes 1310752 | tf_op jit(solution)/shard_map/ppermute | solution.py:81
  161.6 12.4 %shard_map.87 = f32[4,512,128]{2,1,0:T(8,128)} custom-call(s32[1]{0:T(128)} %bitcast.5.spill_ref, bf16[8,512,1024]{2,1,0:T(8,128)(2,1)} %convolution_bitcast_fusion.3.anchor_ref, bf16[8,512,1024]{2,1,0:T(8,128)(2,1)} %convolution_bitcast_fusion.2.own_ref, bf16[512,160]{1,0:T(8,128)(2,1)} %get-tuple-element.51.sbf_ref, ...), custom_call_target="tpu_custom_call" | custom-call | tf_op jit(solution)/shard_map/pallas_call | solution.py:172
  174.0 1.4 reduce_sum.122
  175.6 1.5 collective-permute-done.8
  177.1 1.5 collective-permute-start.9
  178.7 0.2 select_reduce_fusion.2
  178.9 6.7 %collective-permute-done.9 = f32[512,128]{1,0:T(8,128)S(1)} collective-permute-done((f32[512,128]{1,0:T(8,128)S(1)}, f32[512,128]{1,0:T(8,128)S(1)}, u32[]{:S(2)}, u32[]{:S(2)}) %collective-permute-start.9) | collective-permute-done | bytes 262176 | tf_op jit(solution)/shard_map/ppermute | solution.py:72
  185.5 0.2 multiply_reduce_fusion.3
  185.7 2.4 %multiply_reduce_fusion.2 = (f32[8,512]{1,0:T(8,128)S(1)}, f32[8,512]{1,0:T(8,128)S(1)}) fusion(f32[4,512,128]{2,1,0:T(8,128)} %shard_map.87, f32[4,512,128]{2,1,0:T(8,128)S(1)} %copy-done.2, f32[512,128]{1,0:T(8,128)S(1)} %get-tuple-element.34), kind=kLoop, calls=%fused_computation.28 | loop fusion | flops 3137536 | bytes 2392064 | tf_op jit(solution)/shard_map/reduce_sum | solution.py:104
  188.1 0.1 fusion.68
  188.2 0.7 multiply_reduce_fusion
  189.0 1.5 collective-permute-done.10
  190.6 1.5 collective-permute-start.11
  192.1 1.2 collective-permute-done.12
  193.3 0.5 collective-permute-start.13
  193.8 5.2 %collective-permute-done.13 = f32[512]{0:T(512)S(1)} collective-permute-done((f32[512]{0:T(512)S(1)}, f32[512]{0:T(512)S(1)}, u32[]{:S(2)}, u32[]{:S(2)}) %collective-permute-start.13) | collective-permute-done | bytes 2080 | tf_op jit(solution)/shard_map/ppermute | solution.py:72
  199.0 1.0 divide_select_fusion
  (67 shorter events, 1.2 us)
Async XLA Ops:
  0.6 12.7 %copy-start.1 = (bf16[320,8,1024]{2,1,0:T(8,128)(2,1)S(1)}, bf16[320,8,1024]{2,1,0:T(8,128)(2,1)}, u32[]{:S(2)}) copy-start(bf16[320,8,1024]{2,1,0:T(8,128)(2,1)} %param.9) | copy-start | bytes 15728644
  2.3 21.0 %collective-permute-start.2 = (s32[1,1025]{1,0:T(1,128)S(1)}, s32[1,1025]{1,0:T(1,128)S(1)}, u32[]{:S(2)}, u32[]{:S(2)}) collective-permute-start(s32[1,1025]{1,0:T(1,128)S(1)} %broadcast_in_dim.45), channel_id=1, source_target_pairs={{0,4},{4,0},{8,12},{12,8},{1,5},{5,1},{9,13},{13,9},{2,6},{6,2},{1... | collective-permute-start | bytes 12308 | tf_op jit(solution)/shard_map/ppermute | solution.py:93
  13.4 6.5 %copy-start.6 = (s32[512]{0:T(512)S(1)}, s32[512]{0:T(512)}, u32[]{:S(2)}) copy-start(s32[512]{0:T(512)} %param.11) | copy-start | bytes 6148
  13.4 6.5 %copy-start.5 = (s32[512]{0:T(512)S(1)}, s32[512]{0:T(512)}, u32[]{:S(2)}) copy-start(s32[512]{0:T(512)} %param.12) | copy-start | bytes 6148
  21.6 17.1 %slice-start = ((s8[5242880]{0:T(1024)(128)(4,1)}), s8[1048576]{0:T(1024)(128)(4,1)S(1)}, s32[]{:S(2)}) async-start(s8[5242880]{0:T(1024)(128)(4,1)} %bitcast.68), calls=%async_computation | async-start | bytes 2097152
  23.3 4.6 %collective-permute-start.3 = (s32[2,1025]{1,0:T(2,128)S(1)}, s32[2,1025]{1,0:T(2,128)S(1)}, u32[]{:S(2)}, u32[]{:S(2)}) collective-permute-start(s32[2,1025]{1,0:T(2,128)S(1)} %add_select_fusion.1), channel_id=1, source_target_pairs={{0,8},{4,12},{8,0},{12,4},{1,9},{5,13},{9,1},{13,5},{2,10},{6,14},... | collective-permute-start | bytes 24608 | tf_op jit(solution)/shard_map/ppermute | solution.py:93
  31.8 6.9 %slice-start.1 = ((s8[5242880]{0:T(1024)(128)(4,1)}), s8[4194304]{0:T(1024)(128)(4,1)S(1)}, s32[]{:S(2)}) async-start(s8[5242880]{0:T(1024)(128)(4,1)} %bitcast.68), calls=%async_computation.1 | async-start | bytes 8388608
  47.0 33.9 %collective-permute-start.4 = (bf16[4,160,1024]{2,1,0:T(8,128)(2,1)}, bf16[4,160,1024]{2,1,0:T(8,128)(2,1)}, u32[]{:S(2)}, u32[]{:S(2)}) collective-permute-start(bf16[4,160,1024]{2,1,0:T(8,128)(2,1)} %convolution_bitcast_fusion.7), channel_id=1, source_target_pairs={{0,4},{4,8},{8,12},{12,0},{1,5},{5,9},{9,13},{13,1},{2,6},{6,10},{... | collective-permute-start | bytes 3932168 | tf_op jit(solution)/shard_map/ppermute | solution.py:81
  47.2 85.1 %collective-permute-start.5 = (bf16[4,160,1024]{2,1,0:T(8,128)(2,1)S(1)}, bf16[4,160,1024]{2,1,0:T(8,128)(2,1)}, u32[]{:S(2)}, u32[]{:S(2)}) collective-permute-start(bf16[4,160,1024]{2,1,0:T(8,128)(2,1)S(1)} %convolution_bitcast_fusion.6), channel_id=1, source_target_pairs={{4,0},{8,4},{12,8},{0,12},{5,1},{9,5},{13,9},{1,13},{6,2},{10,6},{... | collective-permute-start | bytes 3932168 | tf_op jit(solution)/shard_map/ppermute | solution.py:81
  50.8 95.2 %collective-permute-start.6 = (bf16[4,160,1024]{2,1,0:T(8,128)(2,1)}, bf16[4,160,1024]{2,1,0:T(8,128)(2,1)S(1)}, u32[]{:S(2)}, u32[]{:S(2)}) collective-permute-start(bf16[4,160,1024]{2,1,0:T(8,128)(2,1)} %convolution_bitcast_fusion.5), channel_id=1, source_target_pairs={{0,4},{4,8},{8,12},{12,0},{1,5},{5,9},{9,13},{13,1},{2,6},{6,10},{... | collective-permute-start | bytes 3932168 | tf_op jit(solution)/shard_map/ppermute | solution.py:81
  54.6 107.0 %collective-permute-start.7 = (bf16[4,160,1024]{2,1,0:T(8,128)(2,1)}, bf16[4,160,1024]{2,1,0:T(8,128)(2,1)}, u32[]{:S(2)}, u32[]{:S(2)}) collective-permute-start(bf16[4,160,1024]{2,1,0:T(8,128)(2,1)} %convolution_bitcast_fusion.4), channel_id=1, source_target_pairs={{4,0},{8,4},{12,8},{0,12},{5,1},{9,5},{13,9},{1,13},{6,2},{10,6},{... | collective-permute-start | bytes 3932168 | tf_op jit(solution)/shard_map/ppermute | solution.py:81
  59.1 10.2 %copy-start.7 = (s32[512]{0:T(512)S(1)}, s32[512]{0:T(512)}, u32[]{:S(2)}) copy-start(s32[512]{0:T(512)} %param.10) | copy-start | bytes 6148
  146.0 32.6 %copy-start.8 = (f32[8]{0:T(128)S(1)}, f32[8]{0:T(128)}, u32[]{:S(2)}) copy-start(f32[8]{0:T(128)} %param.15) | copy-start | bytes 100
  146.0 32.6 %copy-start.9 = (s32[8]{0:T(128)S(1)}, s32[8]{0:T(128)}, u32[]{:S(2)}) copy-start(s32[8]{0:T(128)} %param.14) | copy-start | bytes 100
  146.0 39.6 %copy-start.2 = (f32[4,512,128]{2,1,0:T(8,128)S(1)}, f32[4,512,128]{2,1,0:T(8,128)}, u32[]{:S(2)}) copy-start(f32[4,512,128]{2,1,0:T(8,128)} %shard_map.86) | copy-start | bytes 3145732
  146.1 15.6 %copy-start.4 = (bf16[4,160,1024]{2,1,0:T(8,128)(2,1)}, bf16[4,160,1024]{2,1,0:T(8,128)(2,1)S(1)}, u32[]{:S(2)}) copy-start(bf16[4,160,1024]{2,1,0:T(8,128)(2,1)S(1)} %collective-permute-done.6.bf_ref) | copy-start | bytes 3932164
  174.0 14.2 %copy-start.3 = (f32[4,512,128]{2,1,0:T(8,128)S(1)}, f32[4,512,128]{2,1,0:T(8,128)}, u32[]{:S(2)}) copy-start(f32[4,512,128]{2,1,0:T(8,128)} %shard_map.87) | copy-start | bytes 3145732
  175.5 1.6 collective-permute-start.8
  177.1 8.4 %collective-permute-start.9 = (f32[512,128]{1,0:T(8,128)S(1)}, f32[512,128]{1,0:T(8,128)S(1)}, u32[]{:S(2)}, u32[]{:S(2)}) collective-permute-start(f32[512,128]{1,0:T(8,128)S(1)} %add.94), channel_id=1, source_target_pairs={{0,2},{1,3},{2,0},{3,1},{4,6},{5,7},{6,4},{7,5},{8,10},{9,11},{10,... | collective-permute-start | bytes 786440 | tf_op jit(solution)/shard_map/ppermute | solution.py:72
  188.9 1.6 collective-permute-start.10
  190.6 8.5 %collective-permute-start.11 = (f32[512,128]{1,0:T(8,128)S(1)}, f32[512,128]{1,0:T(8,128)S(1)}, u32[]{:S(2)}, u32[]{:S(2)}) collective-permute-start(f32[512,128]{1,0:T(8,128)S(1)} %add.100), channel_id=1, source_target_pairs={{0,2},{1,3},{2,0},{3,1},{4,6},{5,7},{6,4},{7,5},{8,10},{9,11},{10,... | collective-permute-start | bytes 786440 | tf_op jit(solution)/shard_map/ppermute | solution.py:72
  192.1 1.2 collective-permute-start.12
  193.3 5.7 %collective-permute-start.13 = (f32[512]{0:T(512)S(1)}, f32[512]{0:T(512)S(1)}, u32[]{:S(2)}, u32[]{:S(2)}) collective-permute-start(f32[512]{0:T(512)S(1)} %add.102), channel_id=1, source_target_pairs={{0,2},{1,3},{2,0},{3,1},{4,6},{5,7},{6,4},{7,5},{8,10},{9,11},{10,... | collective-permute-start | bytes 6152 | tf_op jit(solution)/shard_map/ppermute | solution.py:72

commit v2 on v1

--- a/solution.py
+++ b/solution.py
@@ -128,11 +128,10 @@
     t_re = t_ref[:half, :]
     t_im = t_ref[half:, :]
     sbf, saf = sbf_ref[...], saf_ref[...]
-    for w in range(wins):
-        part = (
-            own_ref[w].astype(jnp.float32)
-            + jnp.dot(sbf, bf_ref[w], preferred_element_type=jnp.float32)
-            + jnp.dot(saf, af_ref[w], preferred_element_type=jnp.float32)
+
+    def one_window(w, carry):
+        raw = jnp.dot(sbf, bf_ref[w], preferred_element_type=jnp.float32) + jnp.dot(
+            saf, af_ref[w], preferred_element_type=jnp.float32
         )
 
         def add_spill(p):
@@ -142,7 +141,10 @@
                 + jnp.dot(sas_ref[...], as_ref[w], preferred_element_type=jnp.float32)
             )
 
-        part = lax.cond(spill_ref[0] != 0, add_spill, lambda p: p, part)
+        raw = lax.cond(spill_ref[0] != 0, add_spill, lambda p: p, raw)
+        power = jnp.mean(raw * raw, axis=-1, keepdims=True)
+        halo = (raw * lax.rsqrt(power + EPS_POWER)).astype(jnp.bfloat16)
+        part = own_ref[w].astype(jnp.float32) + halo.astype(jnp.float32)
         anc = anchor_ref[w].astype(jnp.float32)
         a_re, a_im = anc[:, :half], anc[:, half:]
         p_re, p_im = part[:, :half], part[:, half:]
@@ -151,6 +153,9 @@
         corr_ref[w] = jnp.dot(c_re, t_re, preferred_element_type=jnp.float32) + jnp.dot(
             c_im, t_im, preferred_element_type=jnp.float32
         )
+        return carry
+
+    lax.fori_loop(0, wins, one_window, 0)
 
 
 def halo_cross(spill, chunk, wins, anchors, own, sels, bufs, transform):
@@ -216,11 +221,11 @@
 
     chunks = 2 if local_wins % 2 == 0 else 1
     chunk_wins = local_wins // chunks
-    fast = [gather_rows(0, fast_rows, white[:, c * chunk_wins:(c + 1) * chunk_wins]) for c in range(chunks)]
+    fast = [gather_rows(0, fast_rows, spectra[:, c * chunk_wins:(c + 1) * chunk_wins]) for c in range(chunks)]
     spill = need_most > fast_rows
 
     def do_spill(_):
-        return gather_rows(fast_rows, spill_rows, white)
+        return gather_rows(fast_rows, spill_rows, spectra)
 
     def no_spill(_):
         empty = jnp.zeros((local_wins, spill_rows, spec_width), jnp.bfloat16)

time: 200 us -> 208 us (1.040)
  Pallas kernels: 24.8 us -> 34.1 us
  other arithmetic: 32.5 us -> 23.3 us
  local copies, waits for them, and re-layouts: 5.42 us -> 13.8 us
  waiting for transfers between devices: 85.2 us -> 77.2 us
  matrix products: 31.7 us -> 38.9 us
    pallas_call x2, Pallas kernels: 24.8 us -> 34.1 us  [halo_cross(): pl.pallas_call(cross_kernel, grid_spec=grid_spec, out_shape=jax.ShapeDtyp...]
    slice x1 -> x2, local copies, waits for them, and re-layouts: 0.07 us -> 8.24 us  [the longest x1 8.16 us: local(): spectra[:, c * chunk_wins:(c + 1) * chunk_wins]]
    ppermute x2, waiting for transfers between devices: 67 us -> 59.9 us  [ring_exchange(): lax.ppermute(down_rows, axis, down)]
    reduce_sum x1, other arithmetic: 7.95 us -> 1.09 us  [whiten(): power_mean = jnp.mean(spectra_f * spectra_f, axis=-1, keepdims=True)]
    dot_general x2, matrix products: 20.4 us -> 25.3 us  [pick(): jnp.einsum('sc,cwf->wsf', selector.astype(jnp.bfloat16), rows, preferred_...]
  transfers between devices with their start and end apart: 12 -> 12, of which waited for: 9 -> 8; matrix products, arithmetic and copies ran while one was open for 23% -> 24% of each run, Pallas kernels for 6% -> 8%
where the time goes in v2:
time: 208 us; the launch traced here: 207 us
  waiting for transfers between devices  77.2 us (37%)
  matrix products  38.9 us (19%)
  Pallas kernels  34.1 us (16%)
  other arithmetic  23.3 us (11%)
  starting transfers between devices  17.2 us (8%)
  local copies, waits for them, and re-layouts  13.8 us (7%)
  between operations  2.84 us (1%)
    ppermute x2, waiting for transfers between devices, ring_exchange(): lax.ppermute(down_rows, axis, down)  59.9 us
    pallas_call x2, Pallas kernels, halo_cross(): pl.pallas_call(cross_kernel, grid_spec=grid_spec, out_shape=jax.ShapeDtyp...  34.1 us
    dot_general x2, matrix products, pick(): jnp.einsum('sc,cwf->wsf', selector.astype(jnp.bfloat16), rows, preferred_...  25.3 us
    ppermute x6, waiting for transfers between devices, butterfly_sum(): value = jax.tree.map(jnp.add, value, lax.ppermute(value, axis, pairs))  16.1 us
    slice x1, local copies, waits for them, and re-layouts, local(): spectra[:, c * chunk_wins:(c + 1) * chunk_wins]  8.16 us
    dot_general x2, matrix products, gather_rows(): jnp.einsum('jc,cwf->wjf', send_selector(up_need, up_pos, first, rows), so...  7.74 us
    ppermute x2, starting transfers between devices, ring_exchange(): lax.ppermute(down_rows, axis, down)  7.26 us
    dot_general x2, matrix products, gather_rows(): jnp.einsum('jc,cwf->wjf', send_selector(down_need, down_pos, first, rows)...  5.82 us
  transfers between devices with their start and end apart: 12, of which 8 were waited for; matrix products, arithmetic and copies ran while one was open for 24% of the time, Pallas kernels for 8%

profile of v2, /device:TPU:0, one launch (start us, length us, event | category | flops | bytes accessed | tf_op | source)
XLA Modules:
  0.0 207.4 jit_solution(10624086468068646101)
XLA Ops:
  1.3 0.7 pad_add_fusion
  2.0 3.1 %collective-permute-start.2 = (s32[1,1025]{1,0:T(1,128)S(1)}, s32[1,1025]{1,0:T(1,128)S(1)}, u32[]{:S(2)}, u32[]{:S(2)}) collective-permute-start(s32[1,1025]{1,0:T(1,128)S(1)} %broadcast_in_dim.45), channel_id=1, source_target_pairs={{0,4},{4,0},{8,12},{12,8},{1,5},{5,1},{9,13},{13,9},{2,6},{6,2},{1... | collective-permute-start | bytes 12308 | tf_op jit(solution)/shard_map/ppermute | solution.py:93
  5.1 8.2 %fusion.101 = (bf16[320,4,1024]{2,1,0:T(4,128)(2,1)S(1)}, bf16[320,4,1024]{2,1,0:T(4,128)(2,1)}) fusion(bf16[320,8,1024]{2,1,0:T(8,128)(2,1)} %param.9), kind=kLoop, calls=%fused_computation.152 | loop fusion | bytes 10485760 | tf_op jit(solution)/shard_map/slice | solution.py:224
  13.3 1.1 fusion.20
  14.4 0.2 fusion.58
  14.7 0.3 reduce-window.36
  15.1 0.1 slice_reduce_fusion.3
  15.3 0.3 reduce-window.34
  15.7 0.1 slice_reduce_fusion.4
  15.9 0.2 select_reduce_fusion
  16.3 0.2 copy.49
  16.4 5.7 %fusion.21 = bf16[320,8,1024]{2,1,0:T(8,128)(2,1)} fusion(bf16[320,8,1024]{2,1,0:T(8,128)(2,1)} %param.9, f32[320,8]{1,0:T(8,128)S(1)} %copy.49), kind=kLoop, calls=%fused_computation.21 | loop fusion | flops 7864320 | bytes 10496000 | tf_op jit(solution)/shard_map/convert_element_type | solution.py:18
  22.1 1.4 fusion.68
  23.6 1.1 fusion.76
  24.8 2.7 %collective-permute-start.3 = (s32[2,1025]{1,0:T(2,128)S(1)}, s32[2,1025]{1,0:T(2,128)S(1)}, u32[]{:S(2)}, u32[]{:S(2)}) collective-permute-start(s32[2,1025]{1,0:T(2,128)S(1)} %add_select_fusion.1), channel_id=1, source_target_pairs={{0,8},{4,12},{8,0},{12,4},{1,9},{5,13},{9,1},{13,5},{2,10},{6,14},... | collective-permute-start | bytes 24608 | tf_op jit(solution)/shard_map/ppermute | solution.py:93
  27.4 0.7 pad_maximum_fusion.t_ref
  28.1 1.3 collective-permute-done.3
  29.4 0.1 slice_reduce_fusion
  29.6 0.7 fusion.102
  30.2 0.1 fusion.103
  30.3 1.3 fusion.98
  31.6 0.2 fusion.62
  31.8 0.3 reduce-window.50
  32.2 0.1 slice_reduce_fusion.1
  32.4 0.2 fusion.60
  32.6 0.3 reduce-window.48
  33.0 0.1 slice_reduce_fusion.2
  33.2 4.8 %fusion.36 = bf16[4,160,1024]{2,1,0:T(8,128)(2,1)} fusion(bf16[320,4,1024]{2,1,0:T(4,128)(2,1)} %get-tuple-element.66, s32[320]{0:T(512)S(1)} %slice_add_fusion.1, pred[320]{0:T(512)(128)(4,1)S(1)} %fusion.60), kind=kOutput, calls=%fused_computation.43 | convolution fusion | flops 419532800 | bytes 3933760 | tf_op jit(solution)/shard_map/jc,cwf->wjf/dot_general | solution.py:216
  38.0 2.9 %fusion.39 = bf16[4,160,1024]{2,1,0:T(8,128)(2,1)} fusion(bf16[320,4,1024]{2,1,0:T(4,128)(2,1)S(1)} %copy-done.3, s32[320]{0:T(512)S(1)} %slice_add_fusion, pred[320]{0:T(512)(128)(4,1)S(1)} %fusion.62), kind=kOutput, calls=%fused_computation.44 | convolution fusion | flops 419532800 | bytes 3933760 | tf_op jit(solution)/shard_map/jc,cwf->wjf/dot_general | solution.py:218
  40.9 2.9 %fusion.42 = bf16[4,160,1024]{2,1,0:T(8,128)(2,1)} fusion(bf16[320,4,1024]{2,1,0:T(4,128)(2,1)S(1)} %get-tuple-element.65, s32[320]{0:T(512)S(1)} %slice_add_fusion.1, pred[320]{0:T(512)(128)(4,1)S(1)} %fusion.60), kind=kOutput, calls=%fused_computation.45 | convolution fusion | flops 419532800 | bytes 3933760 | tf_op jit(solution)/shard_map/jc,cwf->wjf/dot_general | solution.py:216
  43.9 2.9 %fusion.45 = bf16[4,160,1024]{2,1,0:T(8,128)(2,1)} fusion(bf16[320,4,1024]{2,1,0:T(4,128)(2,1)S(1)} %get-tuple-element.65, s32[320]{0:T(512)S(1)} %slice_add_fusion, pred[320]{0:T(512)(128)(4,1)S(1)} %fusion.62), kind=kOutput, calls=%fused_computation.46 | convolution fusion | flops 419532800 | bytes 3933760 | tf_op jit(solution)/shard_map/jc,cwf->wjf/dot_general | solution.py:218
  46.8 0.1 fusion.97
  46.9 0.8 fusion.27
  47.7 0.1 convert_reduce_fusion
  47.8 0.7 reduce_max.18
  48.5 0.7 reduce_max.19
  50.5 0.4 collective-permute-start.4
  50.9 3.4 %collective-permute-start.5 = (bf16[4,160,1024]{2,1,0:T(8,128)(2,1)}, bf16[4,160,1024]{2,1,0:T(8,128)(2,1)}, u32[]{:S(2)}, u32[]{:S(2)}) collective-permute-start(bf16[4,160,1024]{2,1,0:T(8,128)(2,1)} %fusion.39), channel_id=1, source_target_pairs={{4,0},{8,4},{12,8},{0,12},{5,1},{9,5},{13,9},{1,13},{6,2},{10,6},{... | collective-permute-start | bytes 3932168 | tf_op jit(solution)/shard_map/ppermute | solution.py:81
  54.4 3.7 %conditional.1 = (bf16[8,160,1024]{2,1,0:T(8,128)(2,1)}, bf16[8,160,1024]{2,1,0:T(8,128)(2,1)}) conditional(s32[]{:T(128)} %convert_element_type.45, () %tuple.16, (s32[320]{0:T(512)S(1)}, pred[320]{0:T(512)(128)(4,1)S(1)}, bf16[320,8,1024]{2,1,0:T(8,128)(2,1)}, s32[320]{0:T(512)S(1)}, pred[320]{0:T(512)(128)(4,1)S(1)}) %tuple.17), branch_computations={%region_21.22_spmd, %region_22.23_spmd} | conditional | flops 1677927040 | bytes 57680124 | solution.py:234
  54.4 1.8 broadcast.164
  56.2 1.9 broadcast.164.clone
  58.1 3.8 %collective-permute-start.7 = (bf16[4,160,1024]{2,1,0:T(8,128)(2,1)}, bf16[4,160,1024]{2,1,0:T(8,128)(2,1)}, u32[]{:S(2)}, u32[]{:S(2)}) collective-permute-start(bf16[4,160,1024]{2,1,0:T(8,128)(2,1)} %fusion.45), channel_id=1, source_target_pairs={{4,0},{8,4},{12,8},{0,12},{5,1},{9,5},{13,9},{1,13},{6,2},{10,6},{... | collective-permute-start | bytes 3932168 | tf_op jit(solution)/shard_map/ppermute | solution.py:81
  61.9 12.6 %convolution_bitcast_fusion.own_ref = bf16[8,512,1024]{2,1,0:T(8,128)(2,1)} fusion(bf16[320,8,1024]{2,1,0:T(8,128)(2,1)} %fusion.21, s32[512]{0:T(512)S(1)} %copy-done.6, pred[512]{0:T(512)(128)(4,1)S(1)} %get-tuple-element.76), kind=kOutput, calls=%fused_computation.22 | convolution fusion | flops 2684682240 | bytes 13634048 | tf_op jit(solution)/shard_map/sc,cwf->wsf/dot_general | solution.py:243
  74.6 12.7 %convolution_bitcast_fusion.1.anchor_ref = bf16[8,512,1024]{2,1,0:T(8,128)(2,1)} fusion(bf16[320,8,1024]{2,1,0:T(8,128)(2,1)} %fusion.21, s32[512]{0:T(512)S(1)} %copy-done.8, pred[512]{0:T(512)(128)(4,1)S(1)} %iota_compare_fusion.17), kind=kOutput, calls=%fused_computation.23 | convolution fusion | flops 2684682240 | bytes 13634048 | tf_op jit(solution)/shard_map/sc,cwf->wsf/dot_general | solution.py:243
  87.2 48.7 %collective-permute-done.5.af_ref = bf16[4,160,1024]{2,1,0:T(8,128)(2,1)} collective-permute-done((bf16[4,160,1024]{2,1,0:T(8,128)(2,1)}, bf16[4,160,1024]{2,1,0:T(8,128)(2,1)}, u32[]{:S(2)}, u32[]{:S(2)}) %collective-permute-start.5) | collective-permute-done | bytes 1310752 | tf_op jit(solution)/shard_map/ppermute | solution.py:81
  135.9 17.0 %shard_map.86 = f32[4,512,128]{2,1,0:T(8,128)} custom-call(s32[1]{0:T(128)} %bitcast.5.spill_ref, bf16[8,512,1024]{2,1,0:T(8,128)(2,1)} %convolution_bitcast_fusion.1.anchor_ref, bf16[8,512,1024]{2,1,0:T(8,128)(2,1)} %convolution_bitcast_fusion.own_ref, bf16[512,160]{1,0:T(8,128)(2,1)} %get-tuple-element.83.sbf_ref, ...), custom_call_target="tpu_custom_call" | custom-call | tf_op jit(solution)/shard_map/pallas_call | solution.py:177
  152.9 1.3 reduce_sum.121
  154.3 11.2 %collective-permute-done.7.af_ref = bf16[4,160,1024]{2,1,0:T(8,128)(2,1)} collective-permute-done((bf16[4,160,1024]{2,1,0:T(8,128)(2,1)}, bf16[4,160,1024]{2,1,0:T(8,128)(2,1)}, u32[]{:S(2)}, u32[]{:S(2)}) %collective-permute-start.7) | collective-permute-done | bytes 1310752 | tf_op jit(solution)/shard_map/ppermute | solution.py:81
  165.5 17.1 %shard_map.87 = f32[4,512,128]{2,1,0:T(8,128)} custom-call(s32[1]{0:T(128)} %bitcast.5.spill_ref, bf16[8,512,1024]{2,1,0:T(8,128)(2,1)} %convolution_bitcast_fusion.1.anchor_ref, bf16[8,512,1024]{2,1,0:T(8,128)(2,1)} %convolution_bitcast_fusion.own_ref, bf16[512,160]{1,0:T(8,128)(2,1)} %get-tuple-element.83.sbf_ref, ...), custom_call_target="tpu_custom_call" | custom-call | tf_op jit(solution)/shard_map/pallas_call | solution.py:177
  182.6 1.5 reduce_sum.122
  184.2 1.5 collective-permute-done.8
  185.7 1.6 collective-permute-start.9
  187.3 0.2 select_reduce_fusion.2
  187.5 6.7 %collective-permute-done.9 = f32[512,128]{1,0:T(8,128)S(1)} collective-permute-done((f32[512,128]{1,0:T(8,128)S(1)}, f32[512,128]{1,0:T(8,128)S(1)}, u32[]{:S(2)}, u32[]{:S(2)}) %collective-permute-start.9) | collective-permute-done | bytes 262176 | tf_op jit(solution)/shard_map/ppermute | solution.py:72
  194.1 0.1 multiply_reduce_fusion.3
  194.3 1.2 multiply_reduce_fusion.2
  195.5 0.1 fusion.100
  195.6 0.7 multiply_reduce_fusion
  196.4 1.5 collective-permute-done.10
  197.9 1.6 collective-permute-start.11
  199.5 1.2 collective-permute-done.12
  200.7 0.5 collective-permute-start.13
  201.2 5.2 %collective-permute-done.13 = f32[512]{0:T(512)S(1)} collective-permute-done((f32[512]{0:T(512)S(1)}, f32[512]{0:T(512)S(1)}, u32[]{:S(2)}, u32[]{:S(2)}) %collective-permute-start.13) | collective-permute-done | bytes 2080 | tf_op jit(solution)/shard_map/ppermute | solution.py:72
  206.4 1.0 divide_select_fusion
  (72 shorter events, 1.3 us)
Async XLA Ops:
  2.0 11.3 %slice-start = ((s8[5242880]{0:T(1024)(128)(4,1)}), s8[4194304]{0:T(1024)(128)(4,1)S(1)}, s32[]{:S(2)}) async-start(s8[5242880]{0:T(1024)(128)(4,1)} %bitcast.60), calls=%async_computation | async-start | bytes 8388608
  2.0 11.3 %slice-start.1 = ((s8[5242880]{0:T(1024)(128)(4,1)}), s8[1048576]{0:T(1024)(128)(4,1)S(1)}, s32[]{:S(2)}) async-start(s8[5242880]{0:T(1024)(128)(4,1)} %bitcast.60), calls=%async_computation.1 | async-start | bytes 2097152
  2.0 22.7 %collective-permute-start.2 = (s32[1,1025]{1,0:T(1,128)S(1)}, s32[1,1025]{1,0:T(1,128)S(1)}, u32[]{:S(2)}, u32[]{:S(2)}) collective-permute-start(s32[1,1025]{1,0:T(1,128)S(1)} %broadcast_in_dim.45), channel_id=1, source_target_pairs={{0,4},{4,0},{8,12},{12,8},{1,5},{5,1},{9,13},{13,9},{2,6},{6,2},{1... | collective-permute-start | bytes 12308 | tf_op jit(solution)/shard_map/ppermute | solution.py:93
  13.3 1.1 copy-start.7
  13.3 1.1 copy-start.6
  24.8 4.6 %collective-permute-start.3 = (s32[2,1025]{1,0:T(2,128)S(1)}, s32[2,1025]{1,0:T(2,128)S(1)}, u32[]{:S(2)}, u32[]{:S(2)}) collective-permute-start(s32[2,1025]{1,0:T(2,128)S(1)} %add_select_fusion.1), channel_id=1, source_target_pairs={{0,8},{4,12},{8,0},{12,4},{1,9},{5,13},{9,1},{13,5},{2,10},{6,14},... | collective-permute-start | bytes 24608 | tf_op jit(solution)/shard_map/ppermute | solution.py:93
  33.0 5.0 %copy-start.3 = (bf16[320,4,1024]{2,1,0:T(4,128)(2,1)S(1)}, bf16[320,4,1024]{2,1,0:T(4,128)(2,1)}, u32[]{:S(2)}) copy-start(bf16[320,4,1024]{2,1,0:T(4,128)(2,1)} %get-tuple-element.66) | copy-start | bytes 7864324
  50.5 36.7 %collective-permute-start.4 = (bf16[4,160,1024]{2,1,0:T(8,128)(2,1)}, bf16[4,160,1024]{2,1,0:T(8,128)(2,1)S(1)}, u32[]{:S(2)}, u32[]{:S(2)}) collective-permute-start(bf16[4,160,1024]{2,1,0:T(8,128)(2,1)} %fusion.36), channel_id=1, source_target_pairs={{0,4},{4,8},{8,12},{12,0},{1,5},{5,9},{9,13},{13,1},{2,6},{6,10},{... | collective-permute-start | bytes 3932168 | tf_op jit(solution)/shard_map/ppermute | solution.py:81
  50.9 85.0 %collective-permute-start.5 = (bf16[4,160,1024]{2,1,0:T(8,128)(2,1)}, bf16[4,160,1024]{2,1,0:T(8,128)(2,1)}, u32[]{:S(2)}, u32[]{:S(2)}) collective-permute-start(bf16[4,160,1024]{2,1,0:T(8,128)(2,1)} %fusion.39), channel_id=1, source_target_pairs={{4,0},{8,4},{12,8},{0,12},{5,1},{9,5},{13,9},{1,13},{6,2},{10,6},{... | collective-permute-start | bytes 3932168 | tf_op jit(solution)/shard_map/ppermute | solution.py:81
  54.4 99.9 %collective-permute-start.6 = (bf16[4,160,1024]{2,1,0:T(8,128)(2,1)}, bf16[4,160,1024]{2,1,0:T(8,128)(2,1)S(1)}, u32[]{:S(2)}, u32[]{:S(2)}) collective-permute-start(bf16[4,160,1024]{2,1,0:T(8,128)(2,1)} %fusion.42), channel_id=1, source_target_pairs={{0,4},{4,8},{8,12},{12,0},{1,5},{5,9},{9,13},{13,1},{2,6},{6,10},{... | collective-permute-start | bytes 3932168 | tf_op jit(solution)/shard_map/ppermute | solution.py:81
  58.1 107.4 %collective-permute-start.7 = (bf16[4,160,1024]{2,1,0:T(8,128)(2,1)}, bf16[4,160,1024]{2,1,0:T(8,128)(2,1)}, u32[]{:S(2)}, u32[]{:S(2)}) collective-permute-start(bf16[4,160,1024]{2,1,0:T(8,128)(2,1)} %fusion.45), channel_id=1, source_target_pairs={{4,0},{8,4},{12,8},{0,12},{5,1},{9,5},{13,9},{1,13},{6,2},{10,6},{... | collective-permute-start | bytes 3932168 | tf_op jit(solution)/shard_map/ppermute | solution.py:81
  61.9 12.7 %copy-start.8 = (s32[512]{0:T(512)S(1)}, s32[512]{0:T(512)}, u32[]{:S(2)}) copy-start(s32[512]{0:T(512)} %param.10) | copy-start | bytes 6148
  87.2 48.7 %copy-start.5 = (bf16[4,160,1024]{2,1,0:T(8,128)(2,1)}, bf16[4,160,1024]{2,1,0:T(8,128)(2,1)S(1)}, u32[]{:S(2)}) copy-start(bf16[4,160,1024]{2,1,0:T(8,128)(2,1)S(1)} %collective-permute-done.4.bf_ref) | copy-start | bytes 3932164
  154.3 11.3 %copy-start.4 = (bf16[4,160,1024]{2,1,0:T(8,128)(2,1)}, bf16[4,160,1024]{2,1,0:T(8,128)(2,1)S(1)}, u32[]{:S(2)}) copy-start(bf16[4,160,1024]{2,1,0:T(8,128)(2,1)S(1)} %collective-permute-done.6.bf_ref) | copy-start | bytes 3932164
  182.6 4.7 %copy-start.9 = (f32[8]{0:T(128)S(1)}, f32[8]{0:T(128)}, u32[]{:S(2)}) copy-start(f32[8]{0:T(128)} %param.15) | copy-start | bytes 100
  182.6 4.7 %copy-start.10 = (s32[8]{0:T(128)S(1)}, s32[8]{0:T(128)}, u32[]{:S(2)}) copy-start(s32[8]{0:T(128)} %param.14) | copy-start | bytes 100
  182.6 11.7 %copy-start.1 = (f32[4,512,128]{2,1,0:T(8,128)S(1)}, f32[4,512,128]{2,1,0:T(8,128)}, u32[]{:S(2)}) copy-start(f32[4,512,128]{2,1,0:T(8,128)} %shard_map.86) | copy-start | bytes 3145732
  182.6 11.7 %copy-start.2 = (f32[4,512,128]{2,1,0:T(8,128)S(1)}, f32[4,512,128]{2,1,0:T(8,128)}, u32[]{:S(2)}) copy-start(f32[4,512,128]{2,1,0:T(8,128)} %shard_map.87) | copy-start | bytes 3145732
  184.1 1.6 collective-permute-start.8
  185.7 8.4 %collective-permute-start.9 = (f32[512,128]{1,0:T(8,128)S(1)}, f32[512,128]{1,0:T(8,128)S(1)}, u32[]{:S(2)}, u32[]{:S(2)}) collective-permute-start(f32[512,128]{1,0:T(8,128)S(1)} %add.94), channel_id=1, source_target_pairs={{0,2},{1,3},{2,0},{3,1},{4,6},{5,7},{6,4},{7,5},{8,10},{9,11},{10,... | collective-permute-start | bytes 786440 | tf_op jit(solution)/shard_map/ppermute | solution.py:72
  196.3 1.6 collective-permute-start.10
  197.9 8.5 %collective-permute-start.11 = (f32[512,128]{1,0:T(8,128)S(1)}, f32[512,128]{1,0:T(8,128)S(1)}, u32[]{:S(2)}, u32[]{:S(2)}) collective-permute-start(f32[512,128]{1,0:T(8,128)S(1)} %add.100), channel_id=1, source_target_pairs={{0,2},{1,3},{2,0},{3,1},{4,6},{5,7},{6,4},{7,5},{8,10},{9,11},{10,... | collective-permute-start | bytes 786440 | tf_op jit(solution)/shard_map/ppermute | solution.py:72
  199.5 1.2 collective-permute-start.12
  200.7 5.7 %collective-permute-start.13 = (f32[512]{0:T(512)S(1)}, f32[512]{0:T(512)S(1)}, u32[]{:S(2)}, u32[]{:S(2)}) collective-permute-start(f32[512]{0:T(512)S(1)} %add.102), channel_id=1, source_target_pairs={{0,2},{1,3},{2,0},{3,1},{4,6},{5,7},{6,4},{7,5},{8,10},{9,11},{10,... | collective-permute-start | bytes 6152 | tf_op jit(solution)/shard_map/ppermute | solution.py:72

commit v3 on v1

--- a/solution.py
+++ b/solution.py
@@ -187,8 +187,7 @@
     block = lax.axis_index("chan")
     table = jnp.concatenate([pair_offset, pair_partner, pair_count])
     tables = gather_blocks(table, "chan")
-    table_before = tables[(block + blocks - 1) % blocks]
-    table_after = tables[(block + 1) % blocks]
+    table_before, table_after = ring_exchange(table, table, "chan")
 
     def needs_of(tab):
         return block_needs(tab[:pair_slots], tab[pair_slots:2 * pair_slots], tab[2 * pair_slots], block_chans)
@@ -202,8 +201,6 @@
         jnp.max(jnp.sum(all_needs[1], axis=1, dtype=jnp.int32)),
     )
 
-    white = whiten(spectra)
-
     def send_selector(need, pos, first, rows):
         return onehot(pos - first, rows, need).T.astype(jnp.bfloat16)
 
@@ -212,15 +209,20 @@
                              preferred_element_type=jnp.bfloat16)
         down_rows = jnp.einsum("jc,cwf->wjf", send_selector(down_need, down_pos, first, rows), source,
                                preferred_element_type=jnp.bfloat16)
-        return ring_exchange(up_rows, down_rows, "chan")
+        return ring_exchange(up_rows, down_rows, "chan"), (up_rows, down_rows)
 
     chunks = 2 if local_wins % 2 == 0 else 1
     chunk_wins = local_wins // chunks
-    fast = [gather_rows(0, fast_rows, white[:, c * chunk_wins:(c + 1) * chunk_wins]) for c in range(chunks)]
+    fast_sent = [gather_rows(0, fast_rows, spectra[:, c * chunk_wins:(c + 1) * chunk_wins]) for c in range(chunks)]
+    fast = [got for got, _ in fast_sent]
+    spectra_late, _ = lax.optimization_barrier((spectra, [sent for _, sent in fast_sent]))
+    white = whiten(spectra_late)
+    fast = [(whiten(b), whiten(a)) for b, a in fast]
     spill = need_most > fast_rows
 
     def do_spill(_):
-        return gather_rows(fast_rows, spill_rows, white)
+        (got_before, got_after), _ = gather_rows(fast_rows, spill_rows, spectra)
+        return whiten(got_before), whiten(got_after)
 
     def no_spill(_):
         empty = jnp.zeros((local_wins, spill_rows, spec_width), jnp.bfloat16)

time: 200 us -> 221 us (1.10); the launches traced: 200 us -> 217 us
  loops' own time: 0.01 us -> 9.09 us
  local copies, waits for them, and re-layouts: 5.42 us -> 13.9 us
  other arithmetic: 32.5 us -> 40.7 us
  matrix products: 31.7 us -> 26.5 us
  waiting for transfers between devices: 85.2 us -> 82 us
    another operation x1, loops' own time: 0.01 us -> 9.09 us  [local(): before_spill, after_spill = lax.cond(spill, do_spill, no_spill, 0)]
    slice x1 -> x2, local copies, waits for them, and re-layouts: 0.07 us -> 8.25 us  [the longest x1 8.17 us: local(): spectra[:, c * chunk_wins:(c + 1) * chunk_wins]]
    convert_element_type x1 -> x5, other arithmetic: 6.48 us -> 14.1 us  [whiten(): return (spectra_f * lax.rsqrt(power_mean + EPS_POWER)).astype(jnp.bfloat16)]
    dot_general x2, matrix products: 20.4 us -> 14.8 us  [pick(): jnp.einsum('sc,cwf->wsf', selector.astype(jnp.bfloat16), rows, preferred_...]
    ppermute x2 -> x3, starting transfers between devices: 0.18 us -> 3.64 us  [ring_exchange(): lax.ppermute(up_rows, axis, up)]
    ppermute x2, starting transfers between devices: 5.74 us -> 2.58 us  [gather_blocks(): got = lax.ppermute(acc, axis, pairs)]
    reduce_sum x1 -> x5, other arithmetic: 7.95 us -> 10.2 us  [whiten(): power_mean = jnp.mean(spectra_f * spectra_f, axis=-1, keepdims=True)]
    ppermute x2 -> x3, waiting for transfers between devices: 67 us -> 65.9 us  [ring_exchange(): lax.ppermute(down_rows, axis, down)]
  transfers between devices with their start and end apart: 12 -> 14, of which waited for: 9 -> 7; matrix products, arithmetic and copies ran while one was open for 23% -> 28% of each run, Pallas kernels for 6% -> 0%
where the time goes in v3:
time: 221 us; the launch traced here: 217 us
  waiting for transfers between devices  82 us (37%)
  other arithmetic  40.7 us (18%)
  matrix products  26.5 us (12%)
  Pallas kernels  24.3 us (11%)
  starting transfers between devices  17.4 us (8%)
  local copies, waits for them, and re-layouts  13.9 us (6%)
  loops' own time  9.09 us (4%)
  between operations  3.1 us (1%)
    ppermute x3, waiting for transfers between devices, ring_exchange(): lax.ppermute(down_rows, axis, down)  65.9 us
    pallas_call x2, Pallas kernels, halo_cross(): pl.pallas_call(cross_kernel, grid_spec=grid_spec, out_shape=jax.ShapeDtyp...  24.3 us
    ppermute x6, waiting for transfers between devices, butterfly_sum(): value = jax.tree.map(jnp.add, value, lax.ppermute(value, axis, pairs))  16.1 us
    dot_general x2, matrix products, pick(): jnp.einsum('sc,cwf->wsf', selector.astype(jnp.bfloat16), rows, preferred_...  14.8 us
    convert_element_type x5, other arithmetic, whiten(): return (spectra_f * lax.rsqrt(power_mean + EPS_POWER)).astype(jnp.bfloat16)  14.1 us
    reduce_sum x5, other arithmetic, whiten(): power_mean = jnp.mean(spectra_f * spectra_f, axis=-1, keepdims=True)  10.2 us
    another operation x1, loops' own time, local(): before_spill, after_spill = lax.cond(spill, do_spill, no_spill, 0)  9.09 us
    slice x1, local copies, waits for them, and re-layouts, local(): spectra[:, c * chunk_wins:(c + 1) * chunk_wins]  8.17 us
  transfers between devices with their start and end apart: 14, of which 7 were waited for; matrix products, arithmetic and copies ran while one was open for 28% of the time, Pallas kernels for 0%

profile of v3, /device:TPU:0, one launch (start us, length us, event | category | flops | bytes accessed | tf_op | source)
XLA Modules:
  0.0 216.9 jit_solution(7479427503565112700)
XLA Ops:
  1.3 0.7 constant_dynamic-update-slice_fusion.2
  2.0 0.7 constant_dynamic-update-slice_fusion.1
  2.7 3.0 %collective-permute-start.5 = (s32[1025]{0:T(1024)S(1)}, s32[1025]{0:T(1024)S(1)}, u32[]{:S(2)}, u32[]{:S(2)}) collective-permute-start(s32[1025]{0:T(1024)S(1)} %constant_dynamic-update-slice_fusion), channel_id=1, source_target_pairs={{0,4},{4,8},{8,12},{12,0},{1,5},{5,9},{9,13},{13,1},{2,6},{6,10},{... | collective-permute-start | bytes 12308 | tf_op jit(solution)/shard_map/ppermute | solution.py:81
  5.7 2.1 collective-permute-start.4
  7.8 8.2 %fusion.113 = (bf16[320,4,1024]{2,1,0:T(4,128)(2,1)}, bf16[320,4,1024]{2,1,0:T(4,128)(2,1)S(1)}) fusion(bf16[320,8,1024]{2,1,0:T(8,128)(2,1)} %param.9), kind=kLoop, calls=%fused_computation.184 | loop fusion | bytes 10485760 | tf_op jit(solution)/shard_map/slice | solution.py:216
  16.0 0.2 fusion.74
  16.3 0.3 reduce-window.50
  16.9 0.3 reduce-window.48
  17.5 0.2 select_reduce_fusion
  17.8 2.0 fusion.80
  19.8 1.1 fusion.88
  20.9 0.7 pad_maximum_fusion.t_ref
  21.6 0.5 slice.103
  22.1 0.6 fusion.111
  22.8 0.2 fusion.67
  23.0 0.3 reduce-window.36
  23.6 0.5 slice.100
  24.1 0.6 fusion.110
  24.7 0.2 fusion.65
  24.9 0.3 reduce-window.34
  25.6 2.9 %fusion.51 = bf16[4,160,1024]{2,1,0:T(8,128)(2,1)} fusion(bf16[320,4,1024]{2,1,0:T(4,128)(2,1)S(1)} %get-tuple-element.66, s32[320]{0:T(512)S(1)} %slice_add_fusion.2, pred[320]{0:T(512)(128)(4,1)S(1)} %fusion.67), kind=kOutput, calls=%fused_computation.70 | convolution fusion | flops 419532800 | bytes 3933760 | tf_op jit(solution)/shard_map/jc,cwf->wjf/dot_general | solution.py:210
  28.5 2.9 %fusion.57 = bf16[4,160,1024]{2,1,0:T(8,128)(2,1)} fusion(bf16[320,4,1024]{2,1,0:T(4,128)(2,1)S(1)} %copy-done.3, s32[320]{0:T(512)S(1)} %slice_add_fusion.2, pred[320]{0:T(512)(128)(4,1)S(1)} %fusion.67), kind=kOutput, calls=%fused_computation.72 | convolution fusion | flops 419532800 | bytes 3933760 | tf_op jit(solution)/shard_map/jc,cwf->wjf/dot_general | solution.py:210
  31.4 2.9 %fusion.54 = bf16[4,160,1024]{2,1,0:T(8,128)(2,1)} fusion(bf16[320,4,1024]{2,1,0:T(4,128)(2,1)S(1)} %copy-done.3, s32[320]{0:T(512)S(1)} %slice_add_fusion.3, pred[320]{0:T(512)(128)(4,1)S(1)} %fusion.65), kind=kOutput, calls=%fused_computation.71 | convolution fusion | flops 419532800 | bytes 3933760 | tf_op jit(solution)/shard_map/jc,cwf->wjf/dot_general | solution.py:208
  34.3 2.6 %collective-permute-start.3 = (s32[2,1025]{1,0:T(2,128)S(1)}, s32[2,1025]{1,0:T(2,128)S(1)}, u32[]{:S(2)}, u32[]{:S(2)}) collective-permute-start(s32[2,1025]{1,0:T(2,128)S(1)} %add_select_fusion.1), channel_id=1, source_target_pairs={{0,8},{4,12},{8,0},{12,4},{1,9},{5,13},{9,1},{13,5},{2,10},{6,14},... | collective-permute-start | bytes 24608 | tf_op jit(solution)/shard_map/ppermute | solution.py:93
  36.9 2.9 %fusion.48 = bf16[4,160,1024]{2,1,0:T(8,128)(2,1)} fusion(bf16[320,4,1024]{2,1,0:T(4,128)(2,1)S(1)} %get-tuple-element.66, s32[320]{0:T(512)S(1)} %slice_add_fusion.3, pred[320]{0:T(512)(128)(4,1)S(1)} %fusion.65), kind=kOutput, calls=%fused_computation.69 | convolution fusion | flops 419532800 | bytes 3933760 | tf_op jit(solution)/shard_map/jc,cwf->wjf/dot_general | solution.py:208
  39.8 1.9 collective-permute-start.7
  41.9 0.4 collective-permute-start.8
  42.5 0.8 fusion.39
  43.5 0.7 reduce_max.18
  44.2 0.7 reduce_max.19
  46.1 11.2 %conditional.1 = (bf16[8,160,1024]{2,1,0:T(8,128)(2,1)S(1)}, bf16[8,160,1024]{2,1,0:T(8,128)(2,1)}) conditional(s32[]{:T(128)} %convert_element_type.81, () %tuple.18, (s32[320]{0:T(512)S(1)}, pred[320]{0:T(512)(128)(4,1)S(1)}, bf16[320,8,1024]{2,1,0:T(8,128)(2,1)}, s32[320]{0:T(512)S(1)}, pred[320]{0:T(512)(128)(4,1)S(1)}) %tuple.19), branch_computations={%region_23.24_spmd, %region_24.27_spmd} | conditional | flops 1693658240 | bytes 73449728 | solution.py:231
  46.1 0.3 broadcast.218
  46.5 1.8 broadcast.218.clone
  57.4 3.4 %collective-permute-start.9 = (bf16[4,160,1024]{2,1,0:T(8,128)(2,1)}, bf16[4,160,1024]{2,1,0:T(8,128)(2,1)}, u32[]{:S(2)}, u32[]{:S(2)}) collective-permute-start(bf16[4,160,1024]{2,1,0:T(8,128)(2,1)} %fusion.57), channel_id=1, source_target_pairs={{4,0},{8,4},{12,8},{0,12},{5,1},{9,5},{13,9},{1,13},{6,2},{10,6},{... | collective-permute-start | bytes 3932168 | tf_op jit(solution)/shard_map/ppermute | solution.py:81
  60.8 3.6 %fusion.24 = f32[320,8]{1,0:T(8,128)S(1)} fusion(bf16[320,8,1024]{2,1,0:T(8,128)(2,1)} %param.9), kind=kLoop, calls=%fused_computation.30 | loop fusion | flops 7861760 | bytes 5253120 | tf_op jit(solution)/shard_map/reduce_sum | solution.py:17
  64.6 3.4 %fusion.25 = bf16[320,8,1024]{2,1,0:T(8,128)(2,1)S(1)} fusion(bf16[320,8,1024]{2,1,0:T(8,128)(2,1)} %param.9, f32[320,8]{1,0:T(8,128)S(1)} %copy.51), kind=kLoop, calls=%fused_computation.31 | loop fusion | flops 7864320 | bytes 10496000 | tf_op jit(solution)/shard_map/convert_element_type | solution.py:18
  68.1 7.4 %convolution_bitcast_fusion.own_ref = bf16[8,512,1024]{2,1,0:T(8,128)(2,1)} fusion(bf16[320,8,1024]{2,1,0:T(8,128)(2,1)S(1)} %fusion.25, s32[512]{0:T(512)S(1)} %copy-done.4, pred[512]{0:T(512)(128)(4,1)S(1)} %get-tuple-element.72), kind=kOutput, calls=%fused_computation.32 | convolution fusion | flops 2684682240 | bytes 13634048 | tf_op jit(solution)/shard_map/sc,cwf->wsf/dot_general | solution.py:240
  75.5 7.4 %convolution_bitcast_fusion.1.anchor_ref = bf16[8,512,1024]{2,1,0:T(8,128)(2,1)} fusion(bf16[320,8,1024]{2,1,0:T(8,128)(2,1)S(1)} %fusion.25, s32[512]{0:T(512)S(1)} %copy-done.6, pred[512]{0:T(512)(128)(4,1)S(1)} %iota_compare_fusion.17), kind=kOutput, calls=%fused_computation.33 | convolution fusion | flops 2684682240 | bytes 13634048 | tf_op jit(solution)/shard_map/sc,cwf->wsf/dot_general | solution.py:240
  82.9 45.2 %collective-permute-done.7 = bf16[4,160,1024]{2,1,0:T(8,128)(2,1)} collective-permute-done((bf16[4,160,1024]{2,1,0:T(8,128)(2,1)}, bf16[4,160,1024]{2,1,0:T(8,128)(2,1)}, u32[]{:S(2)}, u32[]{:S(2)}) %collective-permute-start.7) | collective-permute-done | bytes 1310752 | tf_op jit(solution)/shard_map/ppermute | solution.py:81
  128.0 1.7 fusion.30
  129.7 1.7 fusion.28
  131.4 1.7 fusion.32
  133.1 20.8 %collective-permute-done.9 = bf16[4,160,1024]{2,1,0:T(8,128)(2,1)} collective-permute-done((bf16[4,160,1024]{2,1,0:T(8,128)(2,1)}, bf16[4,160,1024]{2,1,0:T(8,128)(2,1)}, u32[]{:S(2)}, u32[]{:S(2)}) %collective-permute-start.9) | collective-permute-done | bytes 1310752 | tf_op jit(solution)/shard_map/ppermute | solution.py:81
  153.8 1.7 fusion.34
  155.5 2.7 %fusion.31.af_ref = bf16[4,160,1024]{2,1,0:T(8,128)(2,1)} fusion(bf16[4,160,1024]{2,1,0:T(8,128)(2,1)} %collective-permute-done.7, f32[4,160]{1,0:T(4,128)S(1)} %add_rsqrt_fusion.5), kind=kLoop, calls=%fused_computation.47 | loop fusion | flops 1966080 | bytes 2624000 | tf_op jit(solution)/shard_map/convert_element_type | solution.py:18
  158.2 2.7 %fusion.29.bf_ref = bf16[4,160,1024]{2,1,0:T(8,128)(2,1)} fusion(bf16[4,160,1024]{2,1,0:T(8,128)(2,1)} %collective-permute-done.6, f32[4,160]{1,0:T(4,128)S(1)} %add_rsqrt_fusion.6), kind=kLoop, calls=%fused_computation.45 | loop fusion | flops 1966080 | bytes 2624000 | tf_op jit(solution)/shard_map/convert_element_type | solution.py:18
  160.8 12.0 %shard_map.86 = f32[4,512,128]{2,1,0:T(8,128)} custom-call(s32[1]{0:T(128)} %bitcast.5.spill_ref, bf16[8,512,1024]{2,1,0:T(8,128)(2,1)} %convolution_bitcast_fusion.1.anchor_ref, bf16[8,512,1024]{2,1,0:T(8,128)(2,1)} %convolution_bitcast_fusion.own_ref, bf16[512,160]{1,0:T(8,128)(2,1)} %get-tuple-element.79.sbf_ref, ...), custom_call_target="tpu_custom_call" | custom-call | tf_op jit(solution)/shard_map/pallas_call | solution.py:172
  172.9 1.3 reduce_sum.177
  174.2 2.7 %fusion.33.bf_ref = bf16[4,160,1024]{2,1,0:T(8,128)(2,1)} fusion(bf16[4,160,1024]{2,1,0:T(8,128)(2,1)} %collective-permute-done.8, f32[4,160]{1,0:T(4,128)S(1)} %add_rsqrt_fusion.4), kind=kLoop, calls=%fused_computation.49 | loop fusion | flops 1966080 | bytes 2624000 | tf_op jit(solution)/shard_map/convert_element_type | solution.py:18
  176.9 2.7 %fusion.35.af_ref = bf16[4,160,1024]{2,1,0:T(8,128)(2,1)} fusion(bf16[4,160,1024]{2,1,0:T(8,128)(2,1)} %collective-permute-done.9, f32[4,160]{1,0:T(4,128)S(1)} %add_rsqrt_fusion.3), kind=kLoop, calls=%fused_computation.51 | loop fusion | flops 1966080 | bytes 2624000 | tf_op jit(solution)/shard_map/convert_element_type | solution.py:18
  179.6 12.3 %shard_map.87 = f32[4,512,128]{2,1,0:T(8,128)} custom-call(s32[1]{0:T(128)} %bitcast.5.spill_ref, bf16[8,512,1024]{2,1,0:T(8,128)(2,1)} %convolution_bitcast_fusion.1.anchor_ref, bf16[8,512,1024]{2,1,0:T(8,128)(2,1)} %convolution_bitcast_fusion.own_ref, bf16[512,160]{1,0:T(8,128)(2,1)} %get-tuple-element.79.sbf_ref, ...), custom_call_target="tpu_custom_call" | custom-call | tf_op jit(solution)/shard_map/pallas_call | solution.py:172
  191.9 1.5 reduce_sum.180
  193.4 1.5 collective-permute-done.10
  195.0 1.6 collective-permute-start.11
  196.6 0.2 select_reduce_fusion.2
  196.8 6.7 %collective-permute-done.11 = f32[512,128]{1,0:T(8,128)S(1)} collective-permute-done((f32[512,128]{1,0:T(8,128)S(1)}, f32[512,128]{1,0:T(8,128)S(1)}, u32[]{:S(2)}, u32[]{:S(2)}) %collective-permute-start.11) | collective-permute-done | bytes 262176 | tf_op jit(solution)/shard_map/ppermute | solution.py:72
  203.6 1.2 multiply_reduce_fusion.2
  204.9 0.7 multiply_reduce_fusion
  205.7 1.5 collective-permute-done.12
  207.2 1.6 collective-permute-start.13
  208.8 1.2 collective-permute-done.14
  209.9 0.5 collective-permute-start.15
  210.5 5.2 %collective-permute-done.15 = f32[512]{0:T(512)S(1)} collective-permute-done((f32[512]{0:T(512)S(1)}, f32[512]{0:T(512)S(1)}, u32[]{:S(2)}, u32[]{:S(2)}) %collective-permute-start.15) | collective-permute-done | bytes 2080 | tf_op jit(solution)/shard_map/ppermute | solution.py:72
  215.7 1.0 divide_select_fusion
  (84 shorter events, 2.7 us)
Async XLA Ops:
  2.7 18.9 %collective-permute-start.5 = (s32[1025]{0:T(1024)S(1)}, s32[1025]{0:T(1024)S(1)}, u32[]{:S(2)}, u32[]{:S(2)}) collective-permute-start(s32[1025]{0:T(1024)S(1)} %constant_dynamic-update-slice_fusion), channel_id=1, source_target_pairs={{0,4},{4,8},{8,12},{12,0},{1,5},{5,9},{9,13},{13,1},{2,6},{6,10},{... | collective-permute-start | bytes 12308 | tf_op jit(solution)/shard_map/ppermute | solution.py:81
  5.7 17.9 %collective-permute-start.4 = (s32[1025]{0:T(1024)S(1)}, s32[1025]{0:T(1024)S(1)}, u32[]{:S(2)}, u32[]{:S(2)}) collective-permute-start(s32[1025]{0:T(1024)S(1)} %constant_dynamic-update-slice_fusion), channel_id=1, source_target_pairs={{4,0},{8,4},{12,8},{0,12},{5,1},{9,5},{13,9},{1,13},{6,2},{10,6},{... | collective-permute-start | bytes 12308 | tf_op jit(solution)/shard_map/ppermute | solution.py:81
  7.8 26.5 %collective-permute-start.2 = (s32[1,1025]{1,0:T(1,128)S(1)}, s32[1,1025]{1,0:T(1,128)S(1)}, u32[]{:S(2)}, u32[]{:S(2)}) collective-permute-start(s32[1,1025]{1,0:T(1,128)S(1)} %broadcast_in_dim.43), channel_id=1, source_target_pairs={{0,4},{4,0},{8,12},{12,8},{1,5},{5,1},{9,13},{13,9},{2,6},{6,2},{1... | collective-permute-start | bytes 12308 | tf_op jit(solution)/shard_map/ppermute | solution.py:93
  7.8 8.2 %copy-start.5 = (s32[512]{0:T(512)S(1)}, s32[512]{0:T(512)}, u32[]{:S(2)}) copy-start(s32[512]{0:T(512)} %param.11) | copy-start | bytes 6148
  7.8 8.2 %copy-start.4 = (s32[512]{0:T(512)S(1)}, s32[512]{0:T(512)}, u32[]{:S(2)}) copy-start(s32[512]{0:T(512)} %param.12) | copy-start | bytes 6148
  25.4 3.1 %copy-start.3 = (bf16[320,4,1024]{2,1,0:T(4,128)(2,1)S(1)}, bf16[320,4,1024]{2,1,0:T(4,128)(2,1)}, u32[]{:S(2)}) copy-start(bf16[320,4,1024]{2,1,0:T(4,128)(2,1)} %get-tuple-element.65) | copy-start | bytes 7864324
  34.3 8.0 %collective-permute-start.3 = (s32[2,1025]{1,0:T(2,128)S(1)}, s32[2,1025]{1,0:T(2,128)S(1)}, u32[]{:S(2)}, u32[]{:S(2)}) collective-permute-start(s32[2,1025]{1,0:T(2,128)S(1)} %add_select_fusion.1), channel_id=1, source_target_pairs={{0,8},{4,12},{8,0},{12,4},{1,9},{5,13},{9,1},{13,5},{2,10},{6,14},... | collective-permute-start | bytes 24608 | tf_op jit(solution)/shard_map/ppermute | solution.py:93
  39.8 88.2 %collective-permute-start.7 = (bf16[4,160,1024]{2,1,0:T(8,128)(2,1)}, bf16[4,160,1024]{2,1,0:T(8,128)(2,1)}, u32[]{:S(2)}, u32[]{:S(2)}) collective-permute-start(bf16[4,160,1024]{2,1,0:T(8,128)(2,1)} %fusion.51), channel_id=1, source_target_pairs={{4,0},{8,4},{12,8},{0,12},{5,1},{9,5},{13,9},{1,13},{6,2},{10,6},{... | collective-permute-start | bytes 3932168 | tf_op jit(solution)/shard_map/ppermute | solution.py:81
  41.7 88.0 %collective-permute-start.6 = (bf16[4,160,1024]{2,1,0:T(8,128)(2,1)}, bf16[4,160,1024]{2,1,0:T(8,128)(2,1)}, u32[]{:S(2)}, u32[]{:S(2)}) collective-permute-start(bf16[4,160,1024]{2,1,0:T(8,128)(2,1)} %fusion.48), channel_id=1, source_target_pairs={{0,4},{4,8},{8,12},{12,0},{1,5},{5,9},{9,13},{13,1},{2,6},{6,10},{... | collective-permute-start | bytes 3932168 | tf_op jit(solution)/shard_map/ppermute | solution.py:81
  41.9 89.5 %collective-permute-start.8 = (bf16[4,160,1024]{2,1,0:T(8,128)(2,1)}, bf16[4,160,1024]{2,1,0:T(8,128)(2,1)}, u32[]{:S(2)}, u32[]{:S(2)}) collective-permute-start(bf16[4,160,1024]{2,1,0:T(8,128)(2,1)} %fusion.54), channel_id=1, source_target_pairs={{0,4},{4,8},{8,12},{12,0},{1,5},{5,9},{9,13},{13,1},{2,6},{6,10},{... | collective-permute-start | bytes 3932168 | tf_op jit(solution)/shard_map/ppermute | solution.py:81
  57.4 96.4 %collective-permute-start.9 = (bf16[4,160,1024]{2,1,0:T(8,128)(2,1)}, bf16[4,160,1024]{2,1,0:T(8,128)(2,1)}, u32[]{:S(2)}, u32[]{:S(2)}) collective-permute-start(bf16[4,160,1024]{2,1,0:T(8,128)(2,1)} %fusion.57), channel_id=1, source_target_pairs={{4,0},{8,4},{12,8},{0,12},{5,1},{9,5},{13,9},{1,13},{6,2},{10,6},{... | collective-permute-start | bytes 3932168 | tf_op jit(solution)/shard_map/ppermute | solution.py:81
  68.1 7.4 %copy-start.6 = (s32[512]{0:T(512)S(1)}, s32[512]{0:T(512)}, u32[]{:S(2)}) copy-start(s32[512]{0:T(512)} %param.10) | copy-start | bytes 6148
  191.8 4.7 %copy-start.7 = (f32[8]{0:T(128)S(1)}, f32[8]{0:T(128)}, u32[]{:S(2)}) copy-start(f32[8]{0:T(128)} %param.15) | copy-start | bytes 100
  191.8 4.7 %copy-start.8 = (s32[8]{0:T(128)S(1)}, s32[8]{0:T(128)}, u32[]{:S(2)}) copy-start(s32[8]{0:T(128)} %param.14) | copy-start | bytes 100
  191.8 11.7 %copy-start.1 = (f32[4,512,128]{2,1,0:T(8,128)S(1)}, f32[4,512,128]{2,1,0:T(8,128)}, u32[]{:S(2)}) copy-start(f32[4,512,128]{2,1,0:T(8,128)} %shard_map.86) | copy-start | bytes 3145732
  191.9 11.7 %copy-start.2 = (f32[4,512,128]{2,1,0:T(8,128)S(1)}, f32[4,512,128]{2,1,0:T(8,128)}, u32[]{:S(2)}) copy-start(f32[4,512,128]{2,1,0:T(8,128)} %shard_map.87) | copy-start | bytes 3145732
  193.4 1.6 collective-permute-start.10
  195.0 8.4 %collective-permute-start.11 = (f32[512,128]{1,0:T(8,128)S(1)}, f32[512,128]{1,0:T(8,128)S(1)}, u32[]{:S(2)}, u32[]{:S(2)}) collective-permute-start(f32[512,128]{1,0:T(8,128)S(1)} %add.121), channel_id=1, source_target_pairs={{0,2},{1,3},{2,0},{3,1},{4,6},{5,7},{6,4},{7,5},{8,10},{9,11},{10,... | collective-permute-start | bytes 786440 | tf_op jit(solution)/shard_map/ppermute | solution.py:72
  205.6 1.6 collective-permute-start.12
  207.2 8.5 %collective-permute-start.13 = (f32[512,128]{1,0:T(8,128)S(1)}, f32[512,128]{1,0:T(8,128)S(1)}, u32[]{:S(2)}, u32[]{:S(2)}) collective-permute-start(f32[512,128]{1,0:T(8,128)S(1)} %add.127), channel_id=1, source_target_pairs={{0,2},{1,3},{2,0},{3,1},{4,6},{5,7},{6,4},{7,5},{8,10},{9,11},{10,... | collective-permute-start | bytes 786440 | tf_op jit(solution)/shard_map/ppermute | solution.py:72
  208.8 1.2 collective-permute-start.14
  209.9 5.7 %collective-permute-start.15 = (f32[512]{0:T(512)S(1)}, f32[512]{0:T(512)S(1)}, u32[]{:S(2)}, u32[]{:S(2)}) collective-permute-start(f32[512]{0:T(512)S(1)} %add.129), channel_id=1, source_target_pairs={{0,2},{1,3},{2,0},{3,1},{4,6},{5,7},{6,4},{7,5},{8,10},{9,11},{10,... | collective-permute-start | bytes 6152 | tf_op jit(solution)/shard_map/ppermute | solution.py:72

commit v4 on v3

--- a/solution.py
+++ b/solution.py
@@ -187,7 +187,8 @@
     block = lax.axis_index("chan")
     table = jnp.concatenate([pair_offset, pair_partner, pair_count])
     tables = gather_blocks(table, "chan")
-    table_before, table_after = ring_exchange(table, table, "chan")
+    table_before = tables[(block + blocks - 1) % blocks]
+    table_after = tables[(block + 1) % blocks]
 
     def needs_of(tab):
         return block_needs(tab[:pair_slots], tab[pair_slots:2 * pair_slots], tab[2 * pair_slots], block_chans)
@@ -209,6 +210,7 @@
                              preferred_element_type=jnp.bfloat16)
         down_rows = jnp.einsum("jc,cwf->wjf", send_selector(down_need, down_pos, first, rows), source,
                                preferred_element_type=jnp.bfloat16)
+        up_rows, down_rows = whiten(up_rows), whiten(down_rows)
         return ring_exchange(up_rows, down_rows, "chan"), (up_rows, down_rows)
 
     chunks = 2 if local_wins % 2 == 0 else 1
@@ -217,12 +219,11 @@
     fast = [got for got, _ in fast_sent]
     spectra_late, _ = lax.optimization_barrier((spectra, [sent for _, sent in fast_sent]))
     white = whiten(spectra_late)
-    fast = [(whiten(b), whiten(a)) for b, a in fast]
     spill = need_most > fast_rows
 
     def do_spill(_):
-        (got_before, got_after), _ = gather_rows(fast_rows, spill_rows, spectra)
-        return whiten(got_before), whiten(got_after)
+        got, _ = gather_rows(fast_rows, spill_rows, spectra)
+        return got
 
     def no_spill(_):
         empty = jnp.zeros((local_wins, spill_rows, spec_width), jnp.bfloat16)

time: 221 us -> 195 us (0.88)
  waiting for transfers between devices: 82 us -> 64.7 us
  other arithmetic: 40.7 us -> 29.1 us
  loops' own time: 9.09 us -> 14.6 us
    ppermute x3 -> x2, waiting for transfers between devices: 65.9 us -> 15.6 us  [ring_exchange(): lax.ppermute(down_rows, axis, down)]
    ppermute x3 -> x2, waiting for transfers between devices: 0.01 us -> 31.7 us  [ring_exchange(): lax.ppermute(up_rows, axis, up)]
    reduce_sum x5 -> x1, other arithmetic: 10.2 us -> 3.58 us  [whiten(): power_mean = jnp.mean(spectra_f * spectra_f, axis=-1, keepdims=True)]
    another operation x1, loops' own time: 9.09 us -> 14.6 us  [local(): before_spill, after_spill = lax.cond(spill, do_spill, no_spill, 0)]
    convert_element_type x5, other arithmetic: 14.1 us -> 8.82 us  [whiten(): return (spectra_f * lax.rsqrt(power_mean + EPS_POWER)).astype(jnp.bfloat16)]
    ppermute x3 -> x2, starting transfers between devices: 3.64 us -> 0.06 us  [ring_exchange(): lax.ppermute(up_rows, axis, up)]
    ppermute x2, starting transfers between devices: 2.58 us -> 5.74 us  [gather_blocks(): got = lax.ppermute(acc, axis, pairs)]
    ppermute x3 -> x2, starting transfers between devices: 7.36 us -> 6.3 us  [ring_exchange(): lax.ppermute(down_rows, axis, down)]
  transfers between devices with their start and end apart: 14 -> 12, of which waited for: 7 -> 10; matrix products, arithmetic and copies ran while one was open for 28% -> 25% of each run, Pallas kernels for 0% -> 7%
where the time goes in v4:
time: 195 us; the launch traced here: 191 us
  waiting for transfers between devices  64.7 us (33%)
  other arithmetic  29.1 us (15%)
  Pallas kernels  25.1 us (13%)
  matrix products  24.7 us (13%)
  starting transfers between devices  15.9 us (8%)
  loops' own time  14.6 us (7%)
  local copies, waits for them, and re-layouts  13.8 us (7%)
  between operations  3.1 us (2%)
    ppermute x2, waiting for transfers between devices, ring_exchange(): lax.ppermute(up_rows, axis, up)  31.7 us
    pallas_call x2, Pallas kernels, halo_cross(): pl.pallas_call(cross_kernel, grid_spec=grid_spec, out_shape=jax.ShapeDtyp...  25.1 us
    ppermute x6, waiting for transfers between devices, butterfly_sum(): value = jax.tree.map(jnp.add, value, lax.ppermute(value, axis, pairs))  16.1 us
    ppermute x2, waiting for transfers between devices, ring_exchange(): lax.ppermute(down_rows, axis, down)  15.6 us
    dot_general x2, matrix products, pick(): jnp.einsum('sc,cwf->wsf', selector.astype(jnp.bfloat16), rows, preferred_...  15 us
    another operation x1, loops' own time, local(): before_spill, after_spill = lax.cond(spill, do_spill, no_spill, 0)  14.6 us
    convert_element_type x5, other arithmetic, whiten(): return (spectra_f * lax.rsqrt(power_mean + EPS_POWER)).astype(jnp.bfloat16)  8.82 us
    slice x1, local copies, waits for them, and re-layouts, local(): spectra[:, c * chunk_wins:(c + 1) * chunk_wins]  8.17 us
  transfers between devices with their start and end apart: 12, of which 10 were waited for; matrix products, arithmetic and copies ran while one was open for 25% of the time, Pallas kernels for 7%

profile of v4, /device:TPU:0, one launch (start us, length us, event | category | flops | bytes accessed | tf_op | source)
XLA Modules:
  0.0 190.9 jit_solution(15222075256544338044)
XLA Ops:
  1.3 0.7 pad_add_fusion
  2.0 3.1 %collective-permute-start.2 = (s32[1,1025]{1,0:T(1,128)S(1)}, s32[1,1025]{1,0:T(1,128)S(1)}, u32[]{:S(2)}, u32[]{:S(2)}) collective-permute-start(s32[1,1025]{1,0:T(1,128)S(1)} %broadcast_in_dim.43), channel_id=1, source_target_pairs={{0,4},{4,0},{8,12},{12,8},{1,5},{5,1},{9,13},{13,9},{2,6},{6,2},{1... | collective-permute-start | bytes 12308 | tf_op jit(solution)/shard_map/ppermute | solution.py:93
  5.1 8.2 %fusion.95 = (bf16[320,4,1024]{2,1,0:T(4,128)(2,1)}, bf16[320,4,1024]{2,1,0:T(4,128)(2,1)S(1)}) fusion(bf16[320,8,1024]{2,1,0:T(8,128)(2,1)} %param.9), kind=kLoop, calls=%fused_computation.176 | loop fusion | bytes 10485760 | tf_op jit(solution)/shard_map/slice | solution.py:218
  13.3 0.2 fusion.56
  13.6 0.3 reduce-window.50
  14.0 0.1 slice_reduce_fusion.1
  14.2 0.3 reduce-window.48
  14.6 0.1 slice_reduce_fusion.2
  14.8 0.2 select_reduce_fusion
  15.1 1.6 fusion.62
  16.7 1.1 fusion.70
  17.9 2.7 %collective-permute-start.3 = (s32[2,1025]{1,0:T(2,128)S(1)}, s32[2,1025]{1,0:T(2,128)S(1)}, u32[]{:S(2)}, u32[]{:S(2)}) collective-permute-start(s32[2,1025]{1,0:T(2,128)S(1)} %add_select_fusion.1), channel_id=1, source_target_pairs={{0,8},{4,12},{8,0},{12,4},{1,9},{5,13},{9,1},{13,5},{2,10},{6,14},... | collective-permute-start | bytes 24608 | tf_op jit(solution)/shard_map/ppermute | solution.py:93
  20.5 0.7 pad_maximum_fusion.t_ref
  21.3 1.3 collective-permute-done.3
  22.6 0.7 fusion.96
  23.3 1.3 fusion.92
  24.6 0.2 fusion.49
  24.8 0.3 reduce-window.36
  25.2 0.1 slice_reduce_fusion.3
  25.4 0.2 fusion.47
  25.6 0.3 reduce-window.34
  26.2 3.8 %fusion.22 = (f32[4,160]{1,0:T(4,128)S(1)}, bf16[160,4,1024]{2,0,1:T(8,128)(2,1)S(1)}) fusion(bf16[320,4,1024]{2,1,0:T(4,128)(2,1)} %get-tuple-element.73, s32[320]{0:T(512)S(1)} %slice_add_fusion.2, pred[320]{0:T(512)(128)(4,1)S(1)} %fusion.49), kind=kOutput, calls=%fused_computation.36 | convolution fusion | flops 421498240 | bytes 3936320 | tf_op jit(solution)/shard_map/jc,cwf->wjf/dot_general | solution.py:211
  30.1 2.0 %fusion.24 = (f32[4,160]{1,0:T(4,128)S(1)}, bf16[160,4,1024]{2,0,1:T(8,128)(2,1)S(1)}) fusion(bf16[320,4,1024]{2,1,0:T(4,128)(2,1)S(1)} %copy-done.3, s32[320]{0:T(512)S(1)} %slice_add_fusion.3, pred[320]{0:T(512)(128)(4,1)S(1)} %fusion.47), kind=kOutput, calls=%fused_computation.40 | convolution fusion | flops 421498240 | bytes 3936320 | tf_op jit(solution)/shard_map/jc,cwf->wjf/dot_general | solution.py:209
  32.0 2.0 %fusion.26 = (f32[4,160]{1,0:T(4,128)S(1)}, bf16[160,4,1024]{2,0,1:T(8,128)(2,1)S(1)}) fusion(bf16[320,4,1024]{2,1,0:T(4,128)(2,1)S(1)} %get-tuple-element.74, s32[320]{0:T(512)S(1)} %slice_add_fusion.2, pred[320]{0:T(512)(128)(4,1)S(1)} %fusion.49), kind=kOutput, calls=%fused_computation.44 | convolution fusion | flops 421498240 | bytes 3936320 | tf_op jit(solution)/shard_map/jc,cwf->wjf/dot_general | solution.py:211
  34.0 2.0 %fusion.28 = (f32[4,160]{1,0:T(4,128)S(1)}, bf16[160,4,1024]{2,0,1:T(8,128)(2,1)S(1)}) fusion(bf16[320,4,1024]{2,1,0:T(4,128)(2,1)S(1)} %get-tuple-element.74, s32[320]{0:T(512)S(1)} %slice_add_fusion.3, pred[320]{0:T(512)(128)(4,1)S(1)} %fusion.47), kind=kOutput, calls=%fused_computation.48 | convolution fusion | flops 421498240 | bytes 3936320 | tf_op jit(solution)/shard_map/jc,cwf->wjf/dot_general | solution.py:209
  36.1 1.4 fusion.27
  37.5 2.5 %collective-permute-start.5 = (bf16[4,160,1024]{2,1,0:T(8,128)(2,1)}, bf16[4,160,1024]{2,1,0:T(8,128)(2,1)S(1)}, u32[]{:S(2)}, u32[]{:S(2)}) collective-permute-start(bf16[4,160,1024]{2,1,0:T(8,128)(2,1)} %fusion.27), channel_id=1, source_target_pairs={{4,0},{8,4},{12,8},{0,12},{5,1},{9,5},{13,9},{1,13},{6,2},{10,6},{... | collective-permute-start | bytes 3932168 | tf_op jit(solution)/shard_map/ppermute | solution.py:81
  39.9 1.3 fusion.29
  41.3 1.3 fusion.23
  42.6 3.8 %collective-permute-start.7 = (bf16[4,160,1024]{2,1,0:T(8,128)(2,1)}, bf16[4,160,1024]{2,1,0:T(8,128)(2,1)S(1)}, u32[]{:S(2)}, u32[]{:S(2)}) collective-permute-start(bf16[4,160,1024]{2,1,0:T(8,128)(2,1)} %fusion.23), channel_id=1, source_target_pairs={{4,0},{8,4},{12,8},{0,12},{5,1},{9,5},{13,9},{1,13},{6,2},{10,6},{... | collective-permute-start | bytes 3932168 | tf_op jit(solution)/shard_map/ppermute | solution.py:81
  46.4 1.4 fusion.25
  47.9 0.8 fusion.33
  48.7 0.1 convert_reduce_fusion
  48.9 0.7 reduce_max.18
  49.5 0.7 reduce_max.19
  51.5 18.3 %conditional.1 = (bf16[8,160,1024]{2,1,0:T(8,128)(2,1)}, bf16[8,160,1024]{2,1,0:T(8,128)(2,1)}) conditional(s32[]{:T(128)} %convert_element_type.99, () %tuple.18, (s32[320]{0:T(512)S(1)}, pred[320]{0:T(512)(128)(4,1)S(1)}, bf16[320,8,1024]{2,1,0:T(8,128)(2,1)}, s32[320]{0:T(512)S(1)}, pred[320]{0:T(512)(128)(4,1)S(1)}) %tuple.19), branch_computations={%region_25.26_spmd, %region_26.29_spmd} | conditional | flops 1693658240 | bytes 68206848 | solution.py:232
  51.5 1.8 broadcast.238
  53.3 1.9 broadcast.238.clone
  69.8 3.6 %fusion.18 = f32[320,8]{1,0:T(8,128)S(1)} fusion(bf16[320,8,1024]{2,1,0:T(8,128)(2,1)} %param.9), kind=kLoop, calls=%fused_computation.28 | loop fusion | flops 7861760 | bytes 5253120 | tf_op jit(solution)/shard_map/reduce_sum | solution.py:17
  73.5 0.2 copy.51
  73.7 3.4 %fusion.19 = bf16[320,8,1024]{2,1,0:T(8,128)(2,1)S(1)} fusion(bf16[320,8,1024]{2,1,0:T(8,128)(2,1)} %param.9, f32[320,8]{1,0:T(8,128)S(1)} %copy.51), kind=kLoop, calls=%fused_computation.29 | loop fusion | flops 7864320 | bytes 10496000 | tf_op jit(solution)/shard_map/convert_element_type | solution.py:18
  77.1 7.5 %convolution_bitcast_fusion.own_ref = bf16[8,512,1024]{2,1,0:T(8,128)(2,1)} fusion(bf16[320,8,1024]{2,1,0:T(8,128)(2,1)S(1)} %fusion.19, s32[512]{0:T(512)S(1)} %copy-done.6, pred[512]{0:T(512)(128)(4,1)S(1)} %get-tuple-element.84), kind=kOutput, calls=%fused_computation.30 | convolution fusion | flops 2684682240 | bytes 13634048 | tf_op jit(solution)/shard_map/sc,cwf->wsf/dot_general | solution.py:241
  84.6 7.5 %convolution_bitcast_fusion.1.anchor_ref = bf16[8,512,1024]{2,1,0:T(8,128)(2,1)} fusion(bf16[320,8,1024]{2,1,0:T(8,128)(2,1)S(1)} %fusion.19, s32[512]{0:T(512)S(1)} %copy-done.8, pred[512]{0:T(512)(128)(4,1)S(1)} %iota_compare_fusion.17), kind=kOutput, calls=%fused_computation.31 | convolution fusion | flops 2684682240 | bytes 13634048 | tf_op jit(solution)/shard_map/sc,cwf->wsf/dot_general | solution.py:241
  92.1 3.3 %collective-permute-done.5.af_ref = bf16[4,160,1024]{2,1,0:T(8,128)(2,1)S(1)} collective-permute-done((bf16[4,160,1024]{2,1,0:T(8,128)(2,1)}, bf16[4,160,1024]{2,1,0:T(8,128)(2,1)S(1)}, u32[]{:S(2)}, u32[]{:S(2)}) %collective-permute-start.5) | collective-permute-done | bytes 1310752 | tf_op jit(solution)/shard_map/ppermute | solution.py:81
  95.4 4.3 %collective-permute-done.4.bf_ref = bf16[4,160,1024]{2,1,0:T(8,128)(2,1)} collective-permute-done((bf16[4,160,1024]{2,1,0:T(8,128)(2,1)}, bf16[4,160,1024]{2,1,0:T(8,128)(2,1)}, u32[]{:S(2)}, u32[]{:S(2)}) %collective-permute-start.4) | collective-permute-done | bytes 1310752 | tf_op jit(solution)/shard_map/ppermute | solution.py:81
  99.6 12.4 %shard_map.86 = f32[4,512,128]{2,1,0:T(8,128)} custom-call(s32[1]{0:T(128)} %bitcast.5.spill_ref, bf16[8,512,1024]{2,1,0:T(8,128)(2,1)} %convolution_bitcast_fusion.1.anchor_ref, bf16[8,512,1024]{2,1,0:T(8,128)(2,1)} %convolution_bitcast_fusion.own_ref, bf16[512,160]{1,0:T(8,128)(2,1)} %get-tuple-element.91.sbf_ref, ...), custom_call_target="tpu_custom_call" | custom-call | tf_op jit(solution)/shard_map/pallas_call | solution.py:172
  112.1 1.3 reduce_sum.179
  113.4 12.3 %collective-permute-done.7.af_ref = bf16[4,160,1024]{2,1,0:T(8,128)(2,1)S(1)} collective-permute-done((bf16[4,160,1024]{2,1,0:T(8,128)(2,1)}, bf16[4,160,1024]{2,1,0:T(8,128)(2,1)S(1)}, u32[]{:S(2)}, u32[]{:S(2)}) %collective-permute-start.7) | collective-permute-done | bytes 1310752 | tf_op jit(solution)/shard_map/ppermute | solution.py:81
  125.7 27.5 %collective-permute-done.6.bf_ref = bf16[4,160,1024]{2,1,0:T(8,128)(2,1)} collective-permute-done((bf16[4,160,1024]{2,1,0:T(8,128)(2,1)}, bf16[4,160,1024]{2,1,0:T(8,128)(2,1)}, u32[]{:S(2)}, u32[]{:S(2)}) %collective-permute-start.6) | collective-permute-done | bytes 1310752 | tf_op jit(solution)/shard_map/ppermute | solution.py:81
  153.2 12.6 %shard_map.87 = f32[4,512,128]{2,1,0:T(8,128)} custom-call(s32[1]{0:T(128)} %bitcast.5.spill_ref, bf16[8,512,1024]{2,1,0:T(8,128)(2,1)} %convolution_bitcast_fusion.1.anchor_ref, bf16[8,512,1024]{2,1,0:T(8,128)(2,1)} %convolution_bitcast_fusion.own_ref, bf16[512,160]{1,0:T(8,128)(2,1)} %get-tuple-element.91.sbf_ref, ...), custom_call_target="tpu_custom_call" | custom-call | tf_op jit(solution)/shard_map/pallas_call | solution.py:172
  165.9 1.5 reduce_sum.180
  167.5 1.5 collective-permute-done.8
  169.0 1.6 collective-permute-start.9
  170.6 0.2 select_reduce_fusion.2
  170.8 6.7 %collective-permute-done.9 = f32[512,128]{1,0:T(8,128)S(1)} collective-permute-done((f32[512,128]{1,0:T(8,128)S(1)}, f32[512,128]{1,0:T(8,128)S(1)}, u32[]{:S(2)}, u32[]{:S(2)}) %collective-permute-start.9) | collective-permute-done | bytes 262176 | tf_op jit(solution)/shard_map/ppermute | solution.py:72
  177.4 0.1 multiply_reduce_fusion.3
  177.6 1.2 multiply_reduce_fusion.2
  178.9 0.7 multiply_reduce_fusion
  179.7 1.5 collective-permute-done.10
  181.2 1.6 collective-permute-start.11
  182.8 1.2 collective-permute-done.12
  183.9 0.5 collective-permute-start.13
  184.5 5.2 %collective-permute-done.13 = f32[512]{0:T(512)S(1)} collective-permute-done((f32[512]{0:T(512)S(1)}, f32[512]{0:T(512)S(1)}, u32[]{:S(2)}, u32[]{:S(2)}) %collective-permute-start.13) | collective-permute-done | bytes 2080 | tf_op jit(solution)/shard_map/ppermute | solution.py:72
  189.7 1.0 divide_select_fusion
  (75 shorter events, 1.9 us)
Async XLA Ops:
  2.0 15.9 %collective-permute-start.2 = (s32[1,1025]{1,0:T(1,128)S(1)}, s32[1,1025]{1,0:T(1,128)S(1)}, u32[]{:S(2)}, u32[]{:S(2)}) collective-permute-start(s32[1,1025]{1,0:T(1,128)S(1)} %broadcast_in_dim.43), channel_id=1, source_target_pairs={{0,4},{4,0},{8,12},{12,8},{1,5},{5,1},{9,13},{13,9},{2,6},{6,2},{1... | collective-permute-start | bytes 12308 | tf_op jit(solution)/shard_map/ppermute | solution.py:93
  5.1 8.2 %copy-start.7 = (s32[512]{0:T(512)S(1)}, s32[512]{0:T(512)}, u32[]{:S(2)}) copy-start(s32[512]{0:T(512)} %param.11) | copy-start | bytes 6148
  5.1 8.2 %copy-start.6 = (s32[512]{0:T(512)S(1)}, s32[512]{0:T(512)}, u32[]{:S(2)}) copy-start(s32[512]{0:T(512)} %param.12) | copy-start | bytes 6148
  17.9 4.6 %collective-permute-start.3 = (s32[2,1025]{1,0:T(2,128)S(1)}, s32[2,1025]{1,0:T(2,128)S(1)}, u32[]{:S(2)}, u32[]{:S(2)}) collective-permute-start(s32[2,1025]{1,0:T(2,128)S(1)} %add_select_fusion.1), channel_id=1, source_target_pairs={{0,8},{4,12},{8,0},{12,4},{1,9},{5,13},{9,1},{13,5},{2,10},{6,14},... | collective-permute-start | bytes 24608 | tf_op jit(solution)/shard_map/ppermute | solution.py:93
  26.2 3.8 %copy-start.3 = (bf16[320,4,1024]{2,1,0:T(4,128)(2,1)S(1)}, bf16[320,4,1024]{2,1,0:T(4,128)(2,1)}, u32[]{:S(2)}) copy-start(bf16[320,4,1024]{2,1,0:T(4,128)(2,1)} %get-tuple-element.73) | copy-start | bytes 7864324
  37.5 57.9 %collective-permute-start.5 = (bf16[4,160,1024]{2,1,0:T(8,128)(2,1)}, bf16[4,160,1024]{2,1,0:T(8,128)(2,1)S(1)}, u32[]{:S(2)}, u32[]{:S(2)}) collective-permute-start(bf16[4,160,1024]{2,1,0:T(8,128)(2,1)} %fusion.27), channel_id=1, source_target_pairs={{4,0},{8,4},{12,8},{0,12},{5,1},{9,5},{13,9},{1,13},{6,2},{10,6},{... | collective-permute-start | bytes 3932168 | tf_op jit(solution)/shard_map/ppermute | solution.py:81
  41.3 58.4 %collective-permute-start.4 = (bf16[4,160,1024]{2,1,0:T(8,128)(2,1)}, bf16[4,160,1024]{2,1,0:T(8,128)(2,1)}, u32[]{:S(2)}, u32[]{:S(2)}) collective-permute-start(bf16[4,160,1024]{2,1,0:T(8,128)(2,1)} %fusion.29), channel_id=1, source_target_pairs={{0,4},{4,8},{8,12},{12,0},{1,5},{5,9},{9,13},{13,1},{2,6},{6,10},{... | collective-permute-start | bytes 3932168 | tf_op jit(solution)/shard_map/ppermute | solution.py:81
  42.6 83.1 %collective-permute-start.7 = (bf16[4,160,1024]{2,1,0:T(8,128)(2,1)}, bf16[4,160,1024]{2,1,0:T(8,128)(2,1)S(1)}, u32[]{:S(2)}, u32[]{:S(2)}) collective-permute-start(bf16[4,160,1024]{2,1,0:T(8,128)(2,1)} %fusion.23), channel_id=1, source_target_pairs={{4,0},{8,4},{12,8},{0,12},{5,1},{9,5},{13,9},{1,13},{6,2},{10,6},{... | collective-permute-start | bytes 3932168 | tf_op jit(solution)/shard_map/ppermute | solution.py:81
  69.8 83.4 %collective-permute-start.6 = (bf16[4,160,1024]{2,1,0:T(8,128)(2,1)}, bf16[4,160,1024]{2,1,0:T(8,128)(2,1)}, u32[]{:S(2)}, u32[]{:S(2)}) collective-permute-start(bf16[4,160,1024]{2,1,0:T(8,128)(2,1)} %fusion.25), channel_id=1, source_target_pairs={{0,4},{4,8},{8,12},{12,0},{1,5},{5,9},{9,13},{13,1},{2,6},{6,10},{... | collective-permute-start | bytes 3932168 | tf_op jit(solution)/shard_map/ppermute | solution.py:81
  77.1 7.5 %copy-start.8 = (s32[512]{0:T(512)S(1)}, s32[512]{0:T(512)}, u32[]{:S(2)}) copy-start(s32[512]{0:T(512)} %param.10) | copy-start | bytes 6148
  95.4 4.3 %copy-start.5 = (bf16[4,160,1024]{2,1,0:T(8,128)(2,1)}, bf16[4,160,1024]{2,1,0:T(8,128)(2,1)S(1)}, u32[]{:S(2)}) copy-start(bf16[4,160,1024]{2,1,0:T(8,128)(2,1)S(1)} %collective-permute-done.5.af_ref) | copy-start | bytes 3932164
  125.7 27.5 %copy-start.4 = (bf16[4,160,1024]{2,1,0:T(8,128)(2,1)}, bf16[4,160,1024]{2,1,0:T(8,128)(2,1)S(1)}, u32[]{:S(2)}) copy-start(bf16[4,160,1024]{2,1,0:T(8,128)(2,1)S(1)} %collective-permute-done.7.af_ref) | copy-start | bytes 3932164
  165.8 4.7 %copy-start.9 = (f32[8]{0:T(128)S(1)}, f32[8]{0:T(128)}, u32[]{:S(2)}) copy-start(f32[8]{0:T(128)} %param.15) | copy-start | bytes 100
  165.9 4.7 %copy-start.10 = (s32[8]{0:T(128)S(1)}, s32[8]{0:T(128)}, u32[]{:S(2)}) copy-start(s32[8]{0:T(128)} %param.14) | copy-start | bytes 100
  165.9 11.7 %copy-start.1 = (f32[4,512,128]{2,1,0:T(8,128)S(1)}, f32[4,512,128]{2,1,0:T(8,128)}, u32[]{:S(2)}) copy-start(f32[4,512,128]{2,1,0:T(8,128)} %shard_map.86) | copy-start | bytes 3145732
  165.9 11.7 %copy-start.2 = (f32[4,512,128]{2,1,0:T(8,128)S(1)}, f32[4,512,128]{2,1,0:T(8,128)}, u32[]{:S(2)}) copy-start(f32[4,512,128]{2,1,0:T(8,128)} %shard_map.87) | copy-start | bytes 3145732
  167.4 1.6 collective-permute-start.8
  169.0 8.4 %collective-permute-start.9 = (f32[512,128]{1,0:T(8,128)S(1)}, f32[512,128]{1,0:T(8,128)S(1)}, u32[]{:S(2)}, u32[]{:S(2)}) collective-permute-start(f32[512,128]{1,0:T(8,128)S(1)} %add.146), channel_id=1, source_target_pairs={{0,2},{1,3},{2,0},{3,1},{4,6},{5,7},{6,4},{7,5},{8,10},{9,11},{10,... | collective-permute-start | bytes 786440 | tf_op jit(solution)/shard_map/ppermute | solution.py:72
  179.6 1.6 collective-permute-start.10
  181.2 8.5 %collective-permute-start.11 = (f32[512,128]{1,0:T(8,128)S(1)}, f32[512,128]{1,0:T(8,128)S(1)}, u32[]{:S(2)}, u32[]{:S(2)}) collective-permute-start(f32[512,128]{1,0:T(8,128)S(1)} %add.152), channel_id=1, source_target_pairs={{0,2},{1,3},{2,0},{3,1},{4,6},{5,7},{6,4},{7,5},{8,10},{9,11},{10,... | collective-permute-start | bytes 786440 | tf_op jit(solution)/shard_map/ppermute | solution.py:72
  182.8 1.2 collective-permute-start.12
  183.9 5.7 %collective-permute-start.13 = (f32[512]{0:T(512)S(1)}, f32[512]{0:T(512)S(1)}, u32[]{:S(2)}, u32[]{:S(2)}) collective-permute-start(f32[512]{0:T(512)S(1)} %add.154), channel_id=1, source_target_pairs={{0,2},{1,3},{2,0},{3,1},{4,6},{5,7},{6,4},{7,5},{8,10},{9,11},{10,... | collective-permute-start | bytes 6152 | tf_op jit(solution)/shard_map/ppermute | solution.py:72

commit v5 on v4

--- a/solution.py
+++ b/solution.py
@@ -121,8 +121,7 @@
     return need_minus, need_plus, pos_minus, pos_plus
 
 
-def cross_kernel(spill_ref, anchor_ref, own_ref, sbf_ref, saf_ref, sbs_ref, sas_ref,
-                 bf_ref, af_ref, bs_ref, as_ref, t_ref, corr_ref):
+def cross_kernel(anchor_ref, own_ref, sbf_ref, saf_ref, bf_ref, af_ref, t_ref, corr_ref):
     wins = anchor_ref.shape[0]
     half = anchor_ref.shape[2] // 2
     t_re = t_ref[:half, :]
@@ -134,15 +133,6 @@
             + jnp.dot(sbf, bf_ref[w], preferred_element_type=jnp.float32)
             + jnp.dot(saf, af_ref[w], preferred_element_type=jnp.float32)
         )
-
-        def add_spill(p):
-            return (
-                p
-                + jnp.dot(sbs_ref[...], bs_ref[w], preferred_element_type=jnp.float32)
-                + jnp.dot(sas_ref[...], as_ref[w], preferred_element_type=jnp.float32)
-            )
-
-        part = lax.cond(spill_ref[0] != 0, add_spill, lambda p: p, part)
         anc = anchor_ref[w].astype(jnp.float32)
         a_re, a_im = anc[:, :half], anc[:, half:]
         p_re, p_im = part[:, :half], part[:, half:]
@@ -153,28 +143,21 @@
         )
 
 
-def halo_cross(spill, chunk, wins, anchors, own, sels, bufs, transform):
+def halo_cross(chunk, wins, anchors, own, sels, bufs, transform):
     _, slots, width = anchors.shape
     lag_count = transform.shape[1]
     group = min(128, slots)
-    row_spec = pl.BlockSpec((wins, group, width), lambda i, s: (chunk, i, 0))
-    sel_specs = [pl.BlockSpec((group, sel.shape[1]), lambda i, s: (i, 0)) for sel in sels]
-    buf_specs = [
-        pl.BlockSpec((wins,) + buf.shape[1:], lambda i, s, c=(chunk if buf.shape[0] > wins else 0): (c, 0, 0)) for buf in bufs
-    ]
-    grid_spec = pltpu.PrefetchScalarGridSpec(
-        num_scalar_prefetch=1,
-        grid=(slots // group,),
-        in_specs=[row_spec, row_spec] + sel_specs + buf_specs
-        + [pl.BlockSpec(transform.shape, lambda i, s: (0, 0))],
-        out_specs=pl.BlockSpec((wins, group, lag_count), lambda i, s: (0, i, 0)),
-    )
+    row_spec = pl.BlockSpec((wins, group, width), lambda i: (chunk, i, 0))
+    sel_specs = [pl.BlockSpec((group, sel.shape[1]), lambda i: (i, 0)) for sel in sels]
+    buf_specs = [pl.BlockSpec((wins,) + buf.shape[1:], lambda i: (0, 0, 0)) for buf in bufs]
     return pl.pallas_call(
         cross_kernel,
-        grid_spec=grid_spec,
+        grid=(slots // group,),
+        in_specs=[row_spec, row_spec] + sel_specs + buf_specs + [pl.BlockSpec(transform.shape, lambda i: (0, 0))],
+        out_specs=pl.BlockSpec((wins, group, lag_count), lambda i: (0, i, 0)),
         out_shape=jax.ShapeDtypeStruct((wins, slots, lag_count), jnp.float32),
         compiler_params=pltpu.CompilerParams(vmem_limit_bytes=56 * 1024 * 1024),
-    )(spill, anchors, own, *sels, *bufs, transform)
+    )(anchors, own, *sels, *bufs, transform)
 
 
 def local(spectra, pair_anchor, pair_offset, pair_partner, pair_count, window_bins, bin_gain):
@@ -220,16 +203,6 @@
     spectra_late, _ = lax.optimization_barrier((spectra, [sent for _, sent in fast_sent]))
     white = whiten(spectra_late)
     spill = need_most > fast_rows
-
-    def do_spill(_):
-        got, _ = gather_rows(fast_rows, spill_rows, spectra)
-        return got
-
-    def no_spill(_):
-        empty = jnp.zeros((local_wins, spill_rows, spec_width), jnp.bfloat16)
-        return empty, empty
-
-    before_spill, after_spill = lax.cond(spill, do_spill, no_spill, 0)
 
     transform = lag_table(spec_width // 2, LAG)
     lag_count = transform.shape[1]
@@ -250,16 +223,28 @@
     sels = [
         onehot(before_row, fast_rows, use_before).astype(jnp.bfloat16),
         onehot(after_row, fast_rows, use_after).astype(jnp.bfloat16),
-        onehot(before_row - fast_rows, spill_rows, use_before).astype(jnp.bfloat16),
-        onehot(after_row - fast_rows, spill_rows, use_after).astype(jnp.bfloat16),
     ]
     corr_full = jnp.concatenate([
-        halo_cross(
-            spill.astype(jnp.int32).reshape(1), c, chunk_wins, anchors, own, sels,
-            [fast[c][0], fast[c][1], before_spill, after_spill], transform,
-        )
+        halo_cross(c, chunk_wins, anchors, own, sels, [fast[c][0], fast[c][1]], transform)
         for c in range(chunks)
     ])
+
+    def add_spill(corr):
+        (got_before, got_after), _ = gather_rows(fast_rows, spill_rows, spectra)
+        spill_sels = [
+            onehot(before_row - fast_rows, spill_rows, use_before).astype(jnp.bfloat16),
+            onehot(after_row - fast_rows, spill_rows, use_after).astype(jnp.bfloat16),
+        ]
+        zero_own = jnp.zeros_like(own)
+        extra = jnp.concatenate([
+            halo_cross(c, chunk_wins, anchors, zero_own, spill_sels,
+                       [got_before[c * chunk_wins:(c + 1) * chunk_wins], got_after[c * chunk_wins:(c + 1) * chunk_wins]],
+                       transform)
+            for c in range(chunks)
+        ])
+        return corr + extra
+
+    corr_full = lax.cond(spill, add_spill, lambda corr: corr, corr_full)
     corr_all = lax.reduce_precision(corr_full, exponent_bits=8, mantissa_bits=7)
     running = jnp.sum(corr_full, axis=0)
 

time: 195 us -> 201 us (1.031)
  waiting for transfers between devices: 64.7 us -> 81.3 us
  loops' own time: 14.6 us -> 2.32 us
  matrix products: 24.7 us -> 30.2 us
  Pallas kernels: 25.1 us -> 19.6 us
    ppermute x2, waiting for transfers between devices: 15.6 us -> 31.6 us  [ring_exchange(): lax.ppermute(down_rows, axis, down)]
    another operation x1, loops' own time: 14.6 us -> 2.32 us  [local(): corr_full = lax.cond(spill, add_spill, lambda corr: corr, corr_full)]
    pallas_call x2, Pallas kernels: 25.1 us -> 19.6 us  [halo_cross(): pl.pallas_call(cross_kernel, grid=(slots // group,), in_specs=[row_spec,...]
    dot_general x2, matrix products: 15 us -> 20.5 us  [pick(): jnp.einsum('sc,cwf->wsf', selector.astype(jnp.bfloat16), rows, preferred_...]
    cond x0 -> x2, local copies, waits for them, and re-layouts: none -> 3.75 us
    another operation x9 -> x7, local copies, waits for them, and re-layouts: 4.39 us -> 0.69 us
    reduce_sum x3 -> x1, other arithmetic: 2.79 us -> 0.12 us  [local(): running = jnp.sum(corr_full, axis=0)]
    reduce_sum x1, other arithmetic: 3.58 us -> 1.09 us  [whiten(): power_mean = jnp.mean(spectra_f * spectra_f, axis=-1, keepdims=True)]
  transfers between devices with their start and end apart: 12 -> 12, of which waited for: 10 -> 10; matrix products, arithmetic and copies ran while one was open for 25% -> 24% of each run, Pallas kernels for 7% -> 5%
where the time goes in v5:
time: 201 us; the launch traced here: 198 us
  waiting for transfers between devices  81.3 us (40%)
  matrix products  30.2 us (15%)
  other arithmetic  30.1 us (15%)
  Pallas kernels  19.6 us (10%)
  starting transfers between devices  16.5 us (8%)
  local copies, waits for them, and re-layouts  14.6 us (7%)
  between operations  3.19 us (2%)
  loops' own time  2.32 us (1%)
    ppermute x2, waiting for transfers between devices, ring_exchange(): lax.ppermute(down_rows, axis, down)  31.6 us
    ppermute x2, waiting for transfers between devices, ring_exchange(): lax.ppermute(up_rows, axis, up)  31.6 us
    dot_general x2, matrix products, pick(): jnp.einsum('sc,cwf->wsf', selector.astype(jnp.bfloat16), rows, preferred_...  20.5 us
    pallas_call x2, Pallas kernels, halo_cross(): pl.pallas_call(cross_kernel, grid=(slots // group,), in_specs=[row_spec,...  19.6 us
    ppermute x6, waiting for transfers between devices, butterfly_sum(): value = jax.tree.map(jnp.add, value, lax.ppermute(value, axis, pairs))  16.1 us
    convert_element_type x5, other arithmetic, whiten(): return (spectra_f * lax.rsqrt(power_mean + EPS_POWER)).astype(jnp.bfloat16)  10.1 us
    slice x1, local copies, waits for them, and re-layouts, local(): spectra[:, c * chunk_wins:(c + 1) * chunk_wins]  8.96 us
    ppermute x2, starting transfers between devices, ring_exchange(): lax.ppermute(down_rows, axis, down)  6.35 us
  transfers between devices with their start and end apart: 12, of which 10 were waited for; matrix products, arithmetic and copies ran while one was open for 24% of the time, Pallas kernels for 5%

profile of v5, /device:TPU:0, one launch (start us, length us, event | category | flops | bytes accessed | tf_op | source)
XLA Modules:
  0.0 197.7 jit_solution(10522022761407116121)
XLA Ops:
  1.3 0.7 pad_add_fusion
  2.0 3.1 %collective-permute-start.2 = (s32[1,1025]{1,0:T(1,128)S(1)}, s32[1,1025]{1,0:T(1,128)S(1)}, u32[]{:S(2)}, u32[]{:S(2)}) collective-permute-start(s32[1,1025]{1,0:T(1,128)S(1)} %broadcast_in_dim.41), channel_id=1, source_target_pairs={{0,4},{4,0},{8,12},{12,8},{1,5},{5,1},{9,13},{13,9},{2,6},{6,2},{1... | collective-permute-start | bytes 12308 | tf_op jit(solution)/shard_map/ppermute | solution.py:93
  5.1 9.0 %fusion.97 = (bf16[320,4,1024]{2,1,0:T(4,128)(2,1)}, bf16[320,4,1024]{2,1,0:T(4,128)(2,1)}) fusion(bf16[320,8,1024]{2,1,0:T(8,128)(2,1)} %param.9), kind=kLoop, calls=%fused_computation.180 | loop fusion | bytes 10485760 | tf_op jit(solution)/shard_map/slice | solution.py:201
  14.1 0.2 fusion.60
  14.4 0.3 reduce-window.50
  14.8 0.1 slice_reduce_fusion.1
  15.0 0.3 reduce-window.48
  15.6 0.2 select_reduce_fusion
  15.8 0.9 fusion.62.sbf_ref
  16.7 0.9 fusion.64.saf_ref
  17.6 1.5 fusion.70
  19.2 2.7 %collective-permute-start.3 = (s32[2,1025]{1,0:T(2,128)S(1)}, s32[2,1025]{1,0:T(2,128)S(1)}, u32[]{:S(2)}, u32[]{:S(2)}) collective-permute-start(s32[2,1025]{1,0:T(2,128)S(1)} %add_select_fusion.1), channel_id=1, source_target_pairs={{0,8},{4,12},{8,0},{12,4},{1,9},{5,13},{9,1},{13,5},{2,10},{6,14},... | collective-permute-start | bytes 24608 | tf_op jit(solution)/shard_map/ppermute | solution.py:93
  21.9 1.9 collective-permute-done.3
  23.8 0.7 fusion.98
  24.6 0.6 fusion.93
  25.2 0.2 fusion.53
  25.4 0.3 reduce-window.36
  26.0 0.6 fusion.92
  26.7 0.2 fusion.51
  26.9 0.3 reduce-window.34
  27.5 3.8 %fusion.26 = (f32[4,160]{1,0:T(4,128)S(1)}, bf16[160,4,1024]{2,0,1:T(8,128)(2,1)S(1)}) fusion(bf16[320,4,1024]{2,1,0:T(4,128)(2,1)} %get-tuple-element.163, s32[320]{0:T(512)S(1)} %slice_add_fusion.2, pred[320]{0:T(512)(128)(4,1)S(1)} %fusion.53), kind=kOutput, calls=%fused_computation.47 | convolution fusion | flops 421498240 | bytes 3936320 | tf_op jit(solution)/shard_map/jc,cwf->wjf/dot_general | solution.py:194
  31.4 2.0 fusion.28
  33.3 2.0 fusion.30
  35.3 1.9 fusion.32
  37.3 0.3 fusion.31
  37.6 2.5 %collective-permute-start.5 = (bf16[4,160,1024]{2,1,0:T(8,128)(2,1)S(1)}, bf16[4,160,1024]{2,1,0:T(8,128)(2,1)}, u32[]{:S(2)}, u32[]{:S(2)}) collective-permute-start(bf16[4,160,1024]{2,1,0:T(8,128)(2,1)S(1)} %fusion.31), channel_id=1, source_target_pairs={{4,0},{8,4},{12,8},{0,12},{5,1},{9,5},{13,9},{1,13},{6,2},{10,6},{... | collective-permute-start | bytes 3932168 | tf_op jit(solution)/shard_map/ppermute | solution.py:81
  40.1 1.4 fusion.33
  41.6 1.4 fusion.27
  42.9 3.8 %collective-permute-start.7 = (bf16[4,160,1024]{2,1,0:T(8,128)(2,1)}, bf16[4,160,1024]{2,1,0:T(8,128)(2,1)}, u32[]{:S(2)}, u32[]{:S(2)}) collective-permute-start(bf16[4,160,1024]{2,1,0:T(8,128)(2,1)} %fusion.27), channel_id=1, source_target_pairs={{4,0},{8,4},{12,8},{0,12},{5,1},{9,5},{13,9},{1,13},{6,2},{10,6},{... | collective-permute-start | bytes 3932168 | tf_op jit(solution)/shard_map/ppermute | solution.py:81
  46.7 1.3 fusion.29
  48.1 0.6 collective-permute-start.6
  48.8 1.1 fusion.22
  50.0 0.2 copy.51
  50.1 5.7 %fusion.23 = bf16[320,8,1024]{2,1,0:T(8,128)(2,1)} fusion(bf16[320,8,1024]{2,1,0:T(8,128)(2,1)} %param.9, f32[320,8]{1,0:T(8,128)S(1)} %copy.51), kind=kLoop, calls=%fused_computation.40 | loop fusion | flops 7864320 | bytes 10496000 | tf_op jit(solution)/shard_map/convert_element_type | solution.py:18
  55.9 0.8 fusion.37
  56.8 0.1 convert_reduce_fusion
  56.9 0.7 reduce_max.18
  57.6 0.7 reduce_max.19
  59.6 13.0 %convolution_bitcast_fusion.own_ref = bf16[8,512,1024]{2,1,0:T(8,128)(2,1)} fusion(bf16[320,8,1024]{2,1,0:T(8,128)(2,1)} %fusion.23, s32[512]{0:T(512)S(1)} %copy-done.8, pred[512]{0:T(512)(128)(4,1)S(1)} %get-tuple-element.174), kind=kOutput, calls=%fused_computation.41 | convolution fusion | flops 2684682240 | bytes 13634048 | tf_op jit(solution)/shard_map/sc,cwf->wsf/dot_general | solution.py:214
  72.6 7.5 %convolution_bitcast_fusion.1.anchor_ref = bf16[8,512,1024]{2,1,0:T(8,128)(2,1)} fusion(bf16[320,8,1024]{2,1,0:T(8,128)(2,1)S(1)} %copy-done.3, s32[512]{0:T(512)S(1)} %copy-done.10, pred[512]{0:T(512)(128)(4,1)S(1)} %get-tuple-element.188), kind=kOutput, calls=%fused_computation.42 | convolution fusion | flops 2684682240 | bytes 13634048 | tf_op jit(solution)/shard_map/sc,cwf->wsf/dot_general | solution.py:214
  80.1 15.4 %collective-permute-done.5.af_ref = bf16[4,160,1024]{2,1,0:T(8,128)(2,1)} collective-permute-done((bf16[4,160,1024]{2,1,0:T(8,128)(2,1)S(1)}, bf16[4,160,1024]{2,1,0:T(8,128)(2,1)}, u32[]{:S(2)}, u32[]{:S(2)}) %collective-permute-start.5) | collective-permute-done | bytes 1310752 | tf_op jit(solution)/shard_map/ppermute | solution.py:81
  95.5 4.2 %collective-permute-done.4.bf_ref = bf16[4,160,1024]{2,1,0:T(8,128)(2,1)} collective-permute-done((bf16[4,160,1024]{2,1,0:T(8,128)(2,1)}, bf16[4,160,1024]{2,1,0:T(8,128)(2,1)}, u32[]{:S(2)}, u32[]{:S(2)}) %collective-permute-start.4) | collective-permute-done | bytes 1310752 | tf_op jit(solution)/shard_map/ppermute | solution.py:81
  99.6 9.8 %shard_map.86 = f32[4,512,128]{2,1,0:T(8,128)} custom-call(bf16[8,512,1024]{2,1,0:T(8,128)(2,1)} %convolution_bitcast_fusion.1.anchor_ref, bf16[8,512,1024]{2,1,0:T(8,128)(2,1)} %convolution_bitcast_fusion.own_ref, bf16[512,160]{1,0:T(8,128)(2,1)} %fusion.62.sbf_ref, bf16[512,160]{1,0:T(8,128)(2,1)} %fusion.64.saf_ref, ...), custom_call_target="tpu_custom_call" | custom-call | tf_op jit(solution)/shard_map/pallas_call | solution.py:153
  109.4 16.3 %collective-permute-done.7.af_ref = bf16[4,160,1024]{2,1,0:T(8,128)(2,1)} collective-permute-done((bf16[4,160,1024]{2,1,0:T(8,128)(2,1)}, bf16[4,160,1024]{2,1,0:T(8,128)(2,1)}, u32[]{:S(2)}, u32[]{:S(2)}) %collective-permute-start.7) | collective-permute-done | bytes 1310752 | tf_op jit(solution)/shard_map/ppermute | solution.py:81
  125.7 27.5 %collective-permute-done.6.bf_ref = bf16[4,160,1024]{2,1,0:T(8,128)(2,1)} collective-permute-done((bf16[4,160,1024]{2,1,0:T(8,128)(2,1)}, bf16[4,160,1024]{2,1,0:T(8,128)(2,1)}, u32[]{:S(2)}, u32[]{:S(2)}) %collective-permute-start.6) | collective-permute-done | bytes 1310752 | tf_op jit(solution)/shard_map/ppermute | solution.py:81
  153.2 9.8 %shard_map.87 = f32[4,512,128]{2,1,0:T(8,128)} custom-call(bf16[8,512,1024]{2,1,0:T(8,128)(2,1)} %convolution_bitcast_fusion.1.anchor_ref, bf16[8,512,1024]{2,1,0:T(8,128)(2,1)} %convolution_bitcast_fusion.own_ref, bf16[512,160]{1,0:T(8,128)(2,1)} %fusion.62.sbf_ref, bf16[512,160]{1,0:T(8,128)(2,1)} %fusion.64.saf_ref, ...), custom_call_target="tpu_custom_call" | custom-call | tf_op jit(solution)/shard_map/pallas_call | solution.py:153
  162.9 1.4 pad_maximum_fusion
  164.3 8.5 %conditional.1 = (f32[8,512,128]{2,1,0:T(8,128)S(1)}, f32[8,512,128]{2,1,0:T(8,128)}, f32[8,512,128]{2,1,0:T(8,128)}, f32[8,512]{1,0:T(8,128)}, f32[8,512]{1,0:T(8,128)S(1)}, /*index=5*/f32[]{:T(128)}, f32[]{:T(128)}) conditional(s32[]{:T(128)} %convert_element_type.97, f32[8,512,128]{2,1,0:T(8,128)S(1)} %pad_maximum_fusion, (s32[512]{0:T(512)S(1)}, ...), branch_computations={%region_25.27_spmd, %region_27.31_spmd} | conditional | flops 1696768128 | bytes 112637296 | solution.py:247
  164.3 2.5 %multiply_reduce_fusion = (f32[8,512]{1,0:T(8,128)}, f32[8,512,128]{2,1,0:T(8,128)}) fusion(f32[8,512,128]{2,1,0:T(8,128)S(1)} %param), kind=kLoop, calls=%fused_computation | loop fusion | flops 1568768 | bytes 4210688 | tf_op jit(solution)/shard_map/reduce_sum | solution.py:105
  166.8 3.0 %copy.113 = f32[8,512,128]{2,1,0:T(8,128)} copy(f32[8,512,128]{2,1,0:T(8,128)} %get-tuple-element.219) | data formatting | bytes 4194304 | tf_op jit(solution)/shard_map/cond
  169.8 0.7 copy.114
  173.1 1.5 collective-permute-done.8
  174.7 1.6 collective-permute-start.9
  176.2 0.2 select_reduce_fusion.2
  176.4 6.7 %collective-permute-done.9 = f32[512,128]{1,0:T(8,128)S(1)} collective-permute-done((f32[512,128]{1,0:T(8,128)S(1)}, f32[512,128]{1,0:T(8,128)S(1)}, u32[]{:S(2)}, u32[]{:S(2)}) %collective-permute-start.9) | collective-permute-done | bytes 262176 | tf_op jit(solution)/shard_map/ppermute | solution.py:72
  183.1 0.1 multiply_reduce_fusion.4
  183.2 2.2 %multiply_reduce_fusion.3 = f32[8,512]{1,0:T(8,128)S(1)} fusion(f32[8,512,128]{2,1,0:T(8,128)} %get-tuple-element.60, f32[512,128]{1,0:T(8,128)S(1)} %get-tuple-element.150), kind=kLoop, calls=%fused_computation.76 | loop fusion | flops 1044480 | bytes 2375680 | tf_op jit(solution)/shard_map/reduce_sum | solution.py:104
  185.5 0.7 multiply_reduce_fusion.2
  186.4 1.5 collective-permute-done.10
  187.9 1.6 collective-permute-start.11
  189.5 1.2 collective-permute-done.12
  190.7 0.5 collective-permute-start.13
  191.2 5.2 %collective-permute-done.13 = f32[512]{0:T(512)S(1)} collective-permute-done((f32[512]{0:T(512)S(1)}, f32[512]{0:T(512)S(1)}, u32[]{:S(2)}, u32[]{:S(2)}) %collective-permute-start.13) | collective-permute-done | bytes 2080 | tf_op jit(solution)/shard_map/ppermute | solution.py:72
  196.4 1.0 divide_select_fusion
  (79 shorter events, 2.1 us)
Async XLA Ops:
  2.0 17.1 %collective-permute-start.2 = (s32[1,1025]{1,0:T(1,128)S(1)}, s32[1,1025]{1,0:T(1,128)S(1)}, u32[]{:S(2)}, u32[]{:S(2)}) collective-permute-start(s32[1,1025]{1,0:T(1,128)S(1)} %broadcast_in_dim.41), channel_id=1, source_target_pairs={{0,4},{4,0},{8,12},{12,8},{1,5},{5,1},{9,13},{13,9},{2,6},{6,2},{1... | collective-permute-start | bytes 12308 | tf_op jit(solution)/shard_map/ppermute | solution.py:93
  5.1 9.0 %copy-start.9 = (s32[512]{0:T(512)S(1)}, s32[512]{0:T(512)}, u32[]{:S(2)}) copy-start(s32[512]{0:T(512)} %param.11) | copy-start | bytes 6148
  5.1 9.0 %copy-start.8 = (s32[512]{0:T(512)S(1)}, s32[512]{0:T(512)}, u32[]{:S(2)}) copy-start(s32[512]{0:T(512)} %param.12) | copy-start | bytes 6148
  19.2 4.6 %collective-permute-start.3 = (s32[2,1025]{1,0:T(2,128)S(1)}, s32[2,1025]{1,0:T(2,128)S(1)}, u32[]{:S(2)}, u32[]{:S(2)}) collective-permute-start(s32[2,1025]{1,0:T(2,128)S(1)} %add_select_fusion.1), channel_id=1, source_target_pairs={{0,8},{4,12},{8,0},{12,4},{1,9},{5,13},{9,1},{13,5},{2,10},{6,14},... | collective-permute-start | bytes 24608 | tf_op jit(solution)/shard_map/ppermute | solution.py:93
  27.5 3.8 %copy-start.7 = (bf16[320,4,1024]{2,1,0:T(4,128)(2,1)S(1)}, bf16[320,4,1024]{2,1,0:T(4,128)(2,1)}, u32[]{:S(2)}) copy-start(bf16[320,4,1024]{2,1,0:T(4,128)(2,1)} %get-tuple-element.163) | copy-start | bytes 7864324
  31.3 2.0 copy-start.6
  35.3 13.5 %slice-start = ((s8[5242880]{0:T(1024)(128)(4,1)}), s8[4194304]{0:T(1024)(128)(4,1)S(1)}, s32[]{:S(2)}) async-start(s8[5242880]{0:T(1024)(128)(4,1)} %bitcast.100), calls=%async_computation | async-start | bytes 8388608
  37.3 11.5 %slice-start.1 = ((s8[5242880]{0:T(1024)(128)(4,1)}), s8[1048576]{0:T(1024)(128)(4,1)S(1)}, s32[]{:S(2)}) async-start(s8[5242880]{0:T(1024)(128)(4,1)} %bitcast.100), calls=%async_computation.1 | async-start | bytes 2097152
  37.6 57.9 %collective-permute-start.5 = (bf16[4,160,1024]{2,1,0:T(8,128)(2,1)S(1)}, bf16[4,160,1024]{2,1,0:T(8,128)(2,1)}, u32[]{:S(2)}, u32[]{:S(2)}) collective-permute-start(bf16[4,160,1024]{2,1,0:T(8,128)(2,1)S(1)} %fusion.31), channel_id=1, source_target_pairs={{4,0},{8,4},{12,8},{0,12},{5,1},{9,5},{13,9},{1,13},{6,2},{10,6},{... | collective-permute-start | bytes 3932168 | tf_op jit(solution)/shard_map/ppermute | solution.py:81
  41.6 58.1 %collective-permute-start.4 = (bf16[4,160,1024]{2,1,0:T(8,128)(2,1)}, bf16[4,160,1024]{2,1,0:T(8,128)(2,1)}, u32[]{:S(2)}, u32[]{:S(2)}) collective-permute-start(bf16[4,160,1024]{2,1,0:T(8,128)(2,1)} %fusion.33), channel_id=1, source_target_pairs={{0,4},{4,8},{8,12},{12,0},{1,5},{5,9},{9,13},{13,1},{2,6},{6,10},{... | collective-permute-start | bytes 3932168 | tf_op jit(solution)/shard_map/ppermute | solution.py:81
  42.9 82.8 %collective-permute-start.7 = (bf16[4,160,1024]{2,1,0:T(8,128)(2,1)}, bf16[4,160,1024]{2,1,0:T(8,128)(2,1)}, u32[]{:S(2)}, u32[]{:S(2)}) collective-permute-start(bf16[4,160,1024]{2,1,0:T(8,128)(2,1)} %fusion.27), channel_id=1, source_target_pairs={{4,0},{8,4},{12,8},{0,12},{5,1},{9,5},{13,9},{1,13},{6,2},{10,6},{... | collective-permute-start | bytes 3932168 | tf_op jit(solution)/shard_map/ppermute | solution.py:81
  48.1 105.1 %collective-permute-start.6 = (bf16[4,160,1024]{2,1,0:T(8,128)(2,1)}, bf16[4,160,1024]{2,1,0:T(8,128)(2,1)}, u32[]{:S(2)}, u32[]{:S(2)}) collective-permute-start(bf16[4,160,1024]{2,1,0:T(8,128)(2,1)} %fusion.29), channel_id=1, source_target_pairs={{0,4},{4,8},{8,12},{12,0},{1,5},{5,9},{9,13},{13,1},{2,6},{6,10},{... | collective-permute-start | bytes 3932168 | tf_op jit(solution)/shard_map/ppermute | solution.py:81
  59.6 13.0 %copy-start.3 = (bf16[320,8,1024]{2,1,0:T(8,128)(2,1)S(1)}, bf16[320,8,1024]{2,1,0:T(8,128)(2,1)}, u32[]{:S(2)}) copy-start(bf16[320,8,1024]{2,1,0:T(8,128)(2,1)} %fusion.23) | copy-start | bytes 15728644
  59.6 13.0 %copy-start.10 = (s32[512]{0:T(512)S(1)}, s32[512]{0:T(512)}, u32[]{:S(2)}) copy-start(s32[512]{0:T(512)} %param.10) | copy-start | bytes 6148
  109.4 53.5 %copy-start.4 = (f32[4,512,128]{2,1,0:T(8,128)S(1)}, f32[4,512,128]{2,1,0:T(8,128)}, u32[]{:S(2)}) copy-start(f32[4,512,128]{2,1,0:T(8,128)} %shard_map.86) | copy-start | bytes 3145732
  172.9 3.4 %copy-start.11 = (f32[8]{0:T(128)S(1)}, f32[8]{0:T(128)}, u32[]{:S(2)}) copy-start(f32[8]{0:T(128)} %param.15) | copy-start | bytes 100
  172.9 3.4 %copy-start.12 = (s32[8]{0:T(128)S(1)}, s32[8]{0:T(128)}, u32[]{:S(2)}) copy-start(s32[8]{0:T(128)} %param.14) | copy-start | bytes 100
  173.0 12.5 %copy-start.2 = (f32[8,512,128]{2,1,0:T(8,128)S(1)}, f32[8,512,128]{2,1,0:T(8,128)}, u32[]{:S(2)}) copy-start(f32[8,512,128]{2,1,0:T(8,128)} %get-tuple-element.60) | copy-start | bytes 6291460
  173.0 1.6 collective-permute-start.8
  174.7 8.4 %collective-permute-start.9 = (f32[512,128]{1,0:T(8,128)S(1)}, f32[512,128]{1,0:T(8,128)S(1)}, u32[]{:S(2)}, u32[]{:S(2)}) collective-permute-start(f32[512,128]{1,0:T(8,128)S(1)} %add.139), channel_id=1, source_target_pairs={{0,2},{1,3},{2,0},{3,1},{4,6},{5,7},{6,4},{7,5},{8,10},{9,11},{10,... | collective-permute-start | bytes 786440 | tf_op jit(solution)/shard_map/ppermute | solution.py:72
  186.3 1.6 collective-permute-start.10
  187.9 8.5 %collective-permute-start.11 = (f32[512,128]{1,0:T(8,128)S(1)}, f32[512,128]{1,0:T(8,128)S(1)}, u32[]{:S(2)}, u32[]{:S(2)}) collective-permute-start(f32[512,128]{1,0:T(8,128)S(1)} %add.145), channel_id=1, source_target_pairs={{0,2},{1,3},{2,0},{3,1},{4,6},{5,7},{6,4},{7,5},{8,10},{9,11},{10,... | collective-permute-start | bytes 786440 | tf_op jit(solution)/shard_map/ppermute | solution.py:72
  189.5 1.2 collective-permute-start.12
  190.7 5.7 %collective-permute-start.13 = (f32[512]{0:T(512)S(1)}, f32[512]{0:T(512)S(1)}, u32[]{:S(2)}, u32[]{:S(2)}) collective-permute-start(f32[512]{0:T(512)S(1)} %add.147), channel_id=1, source_target_pairs={{0,2},{1,3},{2,0},{3,1},{4,6},{5,7},{6,4},{7,5},{8,10},{9,11},{10,... | collective-permute-start | bytes 6152 | tf_op jit(solution)/shard_map/ppermute | solution.py:72

commit v6 on v5

--- a/solution.py
+++ b/solution.py
@@ -229,7 +229,7 @@
         for c in range(chunks)
     ])
 
-    def add_spill(corr):
+    def spill_extra(_):
         (got_before, got_after), _ = gather_rows(fast_rows, spill_rows, spectra)
         spill_sels = [
             onehot(before_row - fast_rows, spill_rows, use_before).astype(jnp.bfloat16),
@@ -242,9 +242,13 @@
                        transform)
             for c in range(chunks)
         ])
-        return corr + extra
-
-    corr_full = lax.cond(spill, add_spill, lambda corr: corr, corr_full)
+        return extra
+
+    def no_extra(_):
+        return jnp.zeros((local_wins, pair_slots, lag_count), jnp.float32)
+
+    spill_late, _ = lax.optimization_barrier((spill, fast[0]))
+    corr_full = corr_full + lax.cond(spill_late, spill_extra, no_extra, 0)
     corr_all = lax.reduce_precision(corr_full, exponent_bits=8, mantissa_bits=7)
     running = jnp.sum(corr_full, axis=0)
 

time: 201 us -> 190 us (0.945)
  waiting for transfers between devices: 81.3 us -> 73.4 us
  other arithmetic: 30.1 us -> 24.9 us
  matrix products: 30.2 us -> 35 us
  local copies, waits for them, and re-layouts: 14.6 us -> 10.2 us
  loops' own time: 2.32 us -> 4.49 us
    ppermute x2, waiting for transfers between devices: 31.6 us -> 23.7 us  [ring_exchange(): lax.ppermute(down_rows, axis, down)]
    dot_general x2, matrix products: 20.5 us -> 25.3 us  [pick(): jnp.einsum('sc,cwf->wsf', selector.astype(jnp.bfloat16), rows, preferred_...]
    cond x2 -> x0, local copies, waits for them, and re-layouts: 3.75 us -> none
    reduce_sum x1 -> x0, other arithmetic: 2.47 us -> none  [window_weights_wm(): corr_rms = jnp.sqrt(jnp.mean(corr_f * corr_f, axis=-1) + EPS_LAG)]
    another operation x1, loops' own time: 2.32 us -> 4.49 us  [local(): corr_full = corr_full + lax.cond(spill_late, spill_extra, no_extra, 0)]
  transfers between devices with their start and end apart: 12 -> 12, of which waited for: 10 -> 10; matrix products, arithmetic and copies ran while one was open for 24% -> 27% of each run, Pallas kernels for 5% -> 5%
where the time goes in v6:
time: 190 us; the launch traced here: 187 us
  waiting for transfers between devices  73.4 us (39%)
  matrix products  35 us (18%)
  other arithmetic  24.9 us (13%)
  Pallas kernels  19.6 us (10%)
  starting transfers between devices  16.1 us (8%)
  local copies, waits for them, and re-layouts  10.2 us (5%)
  loops' own time  4.49 us (2%)
  between operations  3.17 us (2%)
    ppermute x2, waiting for transfers between devices, ring_exchange(): lax.ppermute(up_rows, axis, up)  31.6 us
    dot_general x2, matrix products, pick(): jnp.einsum('sc,cwf->wsf', selector.astype(jnp.bfloat16), rows, preferred_...  25.3 us
    ppermute x2, waiting for transfers between devices, ring_exchange(): lax.ppermute(down_rows, axis, down)  23.7 us
    pallas_call x2, Pallas kernels, halo_cross(): pl.pallas_call(cross_kernel, grid=(slots // group,), in_specs=[row_spec,...  19.6 us
    ppermute x6, waiting for transfers between devices, butterfly_sum(): value = jax.tree.map(jnp.add, value, lax.ppermute(value, axis, pairs))  16.1 us
    convert_element_type x5, other arithmetic, whiten(): return (spectra_f * lax.rsqrt(power_mean + EPS_POWER)).astype(jnp.bfloat16)  8.99 us
    slice x1, local copies, waits for them, and re-layouts, local(): spectra[:, c * chunk_wins:(c + 1) * chunk_wins]  8.17 us
    ppermute x2, starting transfers between devices, ring_exchange(): lax.ppermute(down_rows, axis, down)  6.34 us
  transfers between devices with their start and end apart: 12, of which 10 were waited for; matrix products, arithmetic and copies ran while one was open for 27% of the time, Pallas kernels for 5%

profile of v6, /device:TPU:0, one launch (start us, length us, event | category | flops | bytes accessed | tf_op | source)
XLA Modules:
  0.0 186.8 jit_solution(10827338518344821459)
XLA Ops:
  1.3 0.7 pad_add_fusion
  2.0 3.1 %collective-permute-start.2 = (s32[1,1025]{1,0:T(1,128)S(1)}, s32[1,1025]{1,0:T(1,128)S(1)}, u32[]{:S(2)}, u32[]{:S(2)}) collective-permute-start(s32[1,1025]{1,0:T(1,128)S(1)} %broadcast_in_dim.41), channel_id=1, source_target_pairs={{0,4},{4,0},{8,12},{12,8},{1,5},{5,1},{9,13},{13,9},{2,6},{6,2},{1... | collective-permute-start | bytes 12308 | tf_op jit(solution)/shard_map/ppermute | solution.py:93
  5.1 8.2 %fusion.98 = (bf16[320,4,1024]{2,1,0:T(4,128)(2,1)}, bf16[320,4,1024]{2,1,0:T(4,128)(2,1)S(1)}) fusion(bf16[320,8,1024]{2,1,0:T(8,128)(2,1)} %param.9), kind=kLoop, calls=%fused_computation.180 | loop fusion | bytes 10485760 | tf_op jit(solution)/shard_map/slice | solution.py:201
  13.3 0.2 fusion.60
  13.6 0.3 reduce-window.50
  14.0 0.1 slice_reduce_fusion.1
  14.2 0.3 reduce-window.48
  14.6 0.1 slice_reduce_fusion.2
  14.8 0.2 select_reduce_fusion
  15.0 1.1 fusion.62
  16.2 1.7 fusion.70
  17.9 2.7 %collective-permute-start.3 = (s32[2,1025]{1,0:T(2,128)S(1)}, s32[2,1025]{1,0:T(2,128)S(1)}, u32[]{:S(2)}, u32[]{:S(2)}) collective-permute-start(s32[2,1025]{1,0:T(2,128)S(1)} %add_select_fusion.1), channel_id=1, source_target_pairs={{0,8},{4,12},{8,0},{12,4},{1,9},{5,13},{9,1},{13,5},{2,10},{6,14},... | collective-permute-start | bytes 24608 | tf_op jit(solution)/shard_map/ppermute | solution.py:93
  20.6 1.9 %collective-permute-done.3 = s32[2,1025]{1,0:T(2,128)S(1)} collective-permute-done((s32[2,1025]{1,0:T(2,128)S(1)}, s32[2,1025]{1,0:T(2,128)S(1)}, u32[]{:S(2)}, u32[]{:S(2)}) %collective-permute-start.3) | collective-permute-done | bytes 8232 | tf_op jit(solution)/shard_map/ppermute | solution.py:93
  22.6 0.7 fusion.99
  23.3 1.3 fusion.92
  24.6 0.2 fusion.53
  24.8 0.3 reduce-window.36
  25.2 0.1 slice_reduce_fusion.3
  25.4 0.2 fusion.51
  25.6 0.3 reduce-window.34
  26.0 0.1 slice_reduce_fusion.4
  26.2 3.8 %fusion.26 = (f32[4,160]{1,0:T(4,128)S(1)}, bf16[160,4,1024]{2,0,1:T(8,128)(2,1)S(1)}) fusion(bf16[320,4,1024]{2,1,0:T(4,128)(2,1)} %get-tuple-element.136, s32[320]{0:T(512)S(1)} %slice_add_fusion.2, pred[320]{0:T(512)(128)(4,1)S(1)} %fusion.53), kind=kOutput, calls=%fused_computation.45 | convolution fusion | flops 421498240 | bytes 3936320 | tf_op jit(solution)/shard_map/jc,cwf->wjf/dot_general | solution.py:194
  30.1 2.0 %fusion.28 = (f32[4,160]{1,0:T(4,128)S(1)}, bf16[160,4,1024]{2,0,1:T(8,128)(2,1)S(1)}) fusion(bf16[320,4,1024]{2,1,0:T(4,128)(2,1)S(1)} %copy-done.3, s32[320]{0:T(512)S(1)} %slice_add_fusion.3, pred[320]{0:T(512)(128)(4,1)S(1)} %fusion.51), kind=kOutput, calls=%fused_computation.49 | convolution fusion | flops 421498240 | bytes 3936320 | tf_op jit(solution)/shard_map/jc,cwf->wjf/dot_general | solution.py:192
  32.0 2.0 %fusion.30 = (f32[4,160]{1,0:T(4,128)S(1)}, bf16[160,4,1024]{2,0,1:T(8,128)(2,1)S(1)}) fusion(bf16[320,4,1024]{2,1,0:T(4,128)(2,1)S(1)} %get-tuple-element.137, s32[320]{0:T(512)S(1)} %slice_add_fusion.2, pred[320]{0:T(512)(128)(4,1)S(1)} %fusion.53), kind=kOutput, calls=%fused_computation.53 | convolution fusion | flops 421498240 | bytes 3936320 | tf_op jit(solution)/shard_map/jc,cwf->wjf/dot_general | solution.py:194
  34.0 2.0 %fusion.32 = (f32[4,160]{1,0:T(4,128)S(1)}, bf16[160,4,1024]{2,0,1:T(8,128)(2,1)S(1)}) fusion(bf16[320,4,1024]{2,1,0:T(4,128)(2,1)S(1)} %get-tuple-element.137, s32[320]{0:T(512)S(1)} %slice_add_fusion.3, pred[320]{0:T(512)(128)(4,1)S(1)} %fusion.51), kind=kOutput, calls=%fused_computation.57 | convolution fusion | flops 421498240 | bytes 3936320 | tf_op jit(solution)/shard_map/jc,cwf->wjf/dot_general | solution.py:192
  36.0 0.3 fusion.31
  36.3 2.5 %collective-permute-start.5 = (bf16[4,160,1024]{2,1,0:T(8,128)(2,1)S(1)}, bf16[4,160,1024]{2,1,0:T(8,128)(2,1)}, u32[]{:S(2)}, u32[]{:S(2)}) collective-permute-start(bf16[4,160,1024]{2,1,0:T(8,128)(2,1)S(1)} %fusion.31), channel_id=1, source_target_pairs={{4,0},{8,4},{12,8},{0,12},{5,1},{9,5},{13,9},{1,13},{6,2},{10,6},{... | collective-permute-start | bytes 3932168 | tf_op jit(solution)/shard_map/ppermute | solution.py:81
  38.8 0.3 fusion.33
  39.2 1.3 fusion.27
  40.5 3.8 %collective-permute-start.7 = (bf16[4,160,1024]{2,1,0:T(8,128)(2,1)}, bf16[4,160,1024]{2,1,0:T(8,128)(2,1)}, u32[]{:S(2)}, u32[]{:S(2)}) collective-permute-start(bf16[4,160,1024]{2,1,0:T(8,128)(2,1)} %fusion.27), channel_id=1, source_target_pairs={{4,0},{8,4},{12,8},{0,12},{5,1},{9,5},{13,9},{1,13},{6,2},{10,6},{... | collective-permute-start | bytes 3932168 | tf_op jit(solution)/shard_map/ppermute | solution.py:81
  44.3 1.4 fusion.29
  45.7 0.2 collective-permute-start.6
  45.8 0.1 slice_reduce_fusion
  46.0 1.1 fusion.22
  47.2 0.2 copy.51
  47.3 5.7 %fusion.23 = bf16[320,8,1024]{2,1,0:T(8,128)(2,1)} fusion(bf16[320,8,1024]{2,1,0:T(8,128)(2,1)} %param.9, f32[320,8]{1,0:T(8,128)S(1)} %copy.51), kind=kLoop, calls=%fused_computation.38 | loop fusion | flops 7864320 | bytes 10496000 | tf_op jit(solution)/shard_map/convert_element_type | solution.py:18
  53.1 0.8 fusion.37
  54.0 0.1 convert_reduce_fusion
  54.1 0.7 reduce_max.18
  54.8 0.7 reduce_max.19
  55.5 12.6 %convolution_bitcast_fusion.1.anchor_ref = bf16[8,512,1024]{2,1,0:T(8,128)(2,1)} fusion(bf16[320,8,1024]{2,1,0:T(8,128)(2,1)} %fusion.23, s32[512]{0:T(512)S(1)} %copy-done.6, pred[512]{0:T(512)(128)(4,1)S(1)} %iota_compare_fusion.17), kind=kOutput, calls=%fused_computation.40 | convolution fusion | flops 2684682240 | bytes 13634048 | tf_op jit(solution)/shard_map/sc,cwf->wsf/dot_general | solution.py:214
  69.4 12.7 %convolution_bitcast_fusion.own_ref = bf16[8,512,1024]{2,1,0:T(8,128)(2,1)} fusion(bf16[320,8,1024]{2,1,0:T(8,128)(2,1)} %fusion.23, s32[512]{0:T(512)S(1)} %copy-done.4, pred[512]{0:T(512)(128)(4,1)S(1)} %get-tuple-element.146), kind=kOutput, calls=%fused_computation.39 | convolution fusion | flops 2684682240 | bytes 13634048 | tf_op jit(solution)/shard_map/sc,cwf->wsf/dot_general | solution.py:214
  82.1 12.1 %collective-permute-done.5.af_ref = bf16[4,160,1024]{2,1,0:T(8,128)(2,1)} collective-permute-done((bf16[4,160,1024]{2,1,0:T(8,128)(2,1)S(1)}, bf16[4,160,1024]{2,1,0:T(8,128)(2,1)}, u32[]{:S(2)}, u32[]{:S(2)}) %collective-permute-start.5) | collective-permute-done | bytes 1310752 | tf_op jit(solution)/shard_map/ppermute | solution.py:81
  94.2 4.2 %collective-permute-done.4.bf_ref = bf16[4,160,1024]{2,1,0:T(8,128)(2,1)} collective-permute-done((bf16[4,160,1024]{2,1,0:T(8,128)(2,1)S(1)}, bf16[4,160,1024]{2,1,0:T(8,128)(2,1)}, u32[]{:S(2)}, u32[]{:S(2)}) %collective-permute-start.4) | collective-permute-done | bytes 1310752 | tf_op jit(solution)/shard_map/ppermute | solution.py:81
  98.3 4.6 %conditional.1 = (f32[8,512,128]{2,1,0:T(8,128)S(1)}) conditional(s32[]{:T(128)} %convert_element_type.113, () %tuple.18, (s32[512]{0:T(512)S(1)}, pred[512]{0:T(512)(128)(4,1)S(1)}, s32[512]{0:T(512)S(1)}, pred[512]{0:T(512)(128)(4,1)S(1)}, s32[320]{0:T(512)S(1)}, /*index=5*/pred[320]{0:T(512)(128)(4,1)S(1)}, bf16[320,8,1024]{2,1,0:T(8,128)(2,1)}, ...), branch_computations={%region_25.26_spmd, %region_26.29_spmd} | conditional | flops 1694675072 | bytes 95810832 | solution.py:251
  98.3 0.1 broadcast.235
  102.9 9.8 %shard_map.86 = f32[4,512,128]{2,1,0:T(8,128)} custom-call(bf16[8,512,1024]{2,1,0:T(8,128)(2,1)} %convolution_bitcast_fusion.1.anchor_ref, bf16[8,512,1024]{2,1,0:T(8,128)(2,1)} %convolution_bitcast_fusion.own_ref, bf16[512,160]{1,0:T(8,128)(2,1)} %get-tuple-element.163.sbf_ref, bf16[512,160]{1,0:T(8,128)(2,1)} %get-tuple-element.164.saf_ref, ...), custom_call_target="tpu_custom_call" | custom-call | tf_op jit(solution)/shard_map/pallas_call | solution.py:153
  112.7 11.6 %collective-permute-done.7.af_ref = bf16[4,160,1024]{2,1,0:T(8,128)(2,1)} collective-permute-done((bf16[4,160,1024]{2,1,0:T(8,128)(2,1)}, bf16[4,160,1024]{2,1,0:T(8,128)(2,1)}, u32[]{:S(2)}, u32[]{:S(2)}) %collective-permute-start.7) | collective-permute-done | bytes 1310752 | tf_op jit(solution)/shard_map/ppermute | solution.py:81
  124.4 27.5 %collective-permute-done.6.bf_ref = bf16[4,160,1024]{2,1,0:T(8,128)(2,1)} collective-permute-done((bf16[4,160,1024]{2,1,0:T(8,128)(2,1)}, bf16[4,160,1024]{2,1,0:T(8,128)(2,1)}, u32[]{:S(2)}, u32[]{:S(2)}) %collective-permute-start.6) | collective-permute-done | bytes 1310752 | tf_op jit(solution)/shard_map/ppermute | solution.py:81
  151.9 9.8 %shard_map.87 = f32[4,512,128]{2,1,0:T(8,128)} custom-call(bf16[8,512,1024]{2,1,0:T(8,128)(2,1)} %convolution_bitcast_fusion.1.anchor_ref, bf16[8,512,1024]{2,1,0:T(8,128)(2,1)} %convolution_bitcast_fusion.own_ref, bf16[512,160]{1,0:T(8,128)(2,1)} %get-tuple-element.163.sbf_ref, bf16[512,160]{1,0:T(8,128)(2,1)} %get-tuple-element.164.saf_ref, ...), custom_call_target="tpu_custom_call" | custom-call | tf_op jit(solution)/shard_map/pallas_call | solution.py:153
  161.7 1.5 fusion.95
  163.3 1.5 collective-permute-done.8
  164.8 1.6 collective-permute-start.9
  166.4 0.2 select_reduce_fusion.2
  166.6 6.7 %collective-permute-done.9 = f32[512,128]{1,0:T(8,128)S(1)} collective-permute-done((f32[512,128]{1,0:T(8,128)S(1)}, f32[512,128]{1,0:T(8,128)S(1)}, u32[]{:S(2)}, u32[]{:S(2)}) %collective-permute-start.9) | collective-permute-done | bytes 262176 | tf_op jit(solution)/shard_map/ppermute | solution.py:72
  173.2 0.1 multiply_reduce_fusion.3
  173.4 1.2 multiply_reduce_fusion.2
  174.7 0.7 multiply_reduce_fusion
  175.5 1.5 collective-permute-done.10
  177.0 1.6 collective-permute-start.11
  178.6 1.2 collective-permute-done.12
  179.7 0.5 collective-permute-start.13
  180.3 5.2 %collective-permute-done.13 = f32[512]{0:T(512)S(1)} collective-permute-done((f32[512]{0:T(512)S(1)}, f32[512]{0:T(512)S(1)}, u32[]{:S(2)}, u32[]{:S(2)}) %collective-permute-start.13) | collective-permute-done | bytes 2080 | tf_op jit(solution)/shard_map/ppermute | solution.py:72
  185.5 1.0 divide_select_fusion
  (69 shorter events, 1.6 us)
Async XLA Ops:
  2.0 15.9 %collective-permute-start.2 = (s32[1,1025]{1,0:T(1,128)S(1)}, s32[1,1025]{1,0:T(1,128)S(1)}, u32[]{:S(2)}, u32[]{:S(2)}) collective-permute-start(s32[1,1025]{1,0:T(1,128)S(1)} %broadcast_in_dim.41), channel_id=1, source_target_pairs={{0,4},{4,0},{8,12},{12,8},{1,5},{5,1},{9,13},{13,9},{2,6},{6,2},{1... | collective-permute-start | bytes 12308 | tf_op jit(solution)/shard_map/ppermute | solution.py:93
  5.1 8.2 %copy-start.5 = (s32[512]{0:T(512)S(1)}, s32[512]{0:T(512)}, u32[]{:S(2)}) copy-start(s32[512]{0:T(512)} %param.11) | copy-start | bytes 6148
  5.1 8.2 %copy-start.4 = (s32[512]{0:T(512)S(1)}, s32[512]{0:T(512)}, u32[]{:S(2)}) copy-start(s32[512]{0:T(512)} %param.12) | copy-start | bytes 6148
  17.9 4.6 %collective-permute-start.3 = (s32[2,1025]{1,0:T(2,128)S(1)}, s32[2,1025]{1,0:T(2,128)S(1)}, u32[]{:S(2)}, u32[]{:S(2)}) collective-permute-start(s32[2,1025]{1,0:T(2,128)S(1)} %add_select_fusion.1), channel_id=1, source_target_pairs={{0,8},{4,12},{8,0},{12,4},{1,9},{5,13},{9,1},{13,5},{2,10},{6,14},... | collective-permute-start | bytes 24608 | tf_op jit(solution)/shard_map/ppermute | solution.py:93
  26.2 3.8 %copy-start.3 = (bf16[320,4,1024]{2,1,0:T(4,128)(2,1)S(1)}, bf16[320,4,1024]{2,1,0:T(4,128)(2,1)}, u32[]{:S(2)}) copy-start(bf16[320,4,1024]{2,1,0:T(4,128)(2,1)} %get-tuple-element.136) | copy-start | bytes 7864324
  34.0 12.0 %slice-start = ((s8[5242880]{0:T(1024)(128)(4,1)}), s8[4194304]{0:T(1024)(128)(4,1)S(1)}, s32[]{:S(2)}) async-start(s8[5242880]{0:T(1024)(128)(4,1)} %bitcast.101), calls=%async_computation | async-start | bytes 8388608
  36.0 10.0 %slice-start.1 = ((s8[5242880]{0:T(1024)(128)(4,1)}), s8[1048576]{0:T(1024)(128)(4,1)S(1)}, s32[]{:S(2)}) async-start(s8[5242880]{0:T(1024)(128)(4,1)} %bitcast.101), calls=%async_computation.1 | async-start | bytes 2097152
  36.3 57.9 %collective-permute-start.5 = (bf16[4,160,1024]{2,1,0:T(8,128)(2,1)S(1)}, bf16[4,160,1024]{2,1,0:T(8,128)(2,1)}, u32[]{:S(2)}, u32[]{:S(2)}) collective-permute-start(bf16[4,160,1024]{2,1,0:T(8,128)(2,1)S(1)} %fusion.31), channel_id=1, source_target_pairs={{4,0},{8,4},{12,8},{0,12},{5,1},{9,5},{13,9},{1,13},{6,2},{10,6},{... | collective-permute-start | bytes 3932168 | tf_op jit(solution)/shard_map/ppermute | solution.py:81
  39.1 59.2 %collective-permute-start.4 = (bf16[4,160,1024]{2,1,0:T(8,128)(2,1)S(1)}, bf16[4,160,1024]{2,1,0:T(8,128)(2,1)}, u32[]{:S(2)}, u32[]{:S(2)}) collective-permute-start(bf16[4,160,1024]{2,1,0:T(8,128)(2,1)S(1)} %fusion.33), channel_id=1, source_target_pairs={{0,4},{4,8},{8,12},{12,0},{1,5},{5,9},{9,13},{13,1},{2,6},{6,10},{... | collective-permute-start | bytes 3932168 | tf_op jit(solution)/shard_map/ppermute | solution.py:81
  40.5 83.9 %collective-permute-start.7 = (bf16[4,160,1024]{2,1,0:T(8,128)(2,1)}, bf16[4,160,1024]{2,1,0:T(8,128)(2,1)}, u32[]{:S(2)}, u32[]{:S(2)}) collective-permute-start(bf16[4,160,1024]{2,1,0:T(8,128)(2,1)} %fusion.27), channel_id=1, source_target_pairs={{4,0},{8,4},{12,8},{0,12},{5,1},{9,5},{13,9},{1,13},{6,2},{10,6},{... | collective-permute-start | bytes 3932168 | tf_op jit(solution)/shard_map/ppermute | solution.py:81
  45.7 106.2 %collective-permute-start.6 = (bf16[4,160,1024]{2,1,0:T(8,128)(2,1)}, bf16[4,160,1024]{2,1,0:T(8,128)(2,1)}, u32[]{:S(2)}, u32[]{:S(2)}) collective-permute-start(bf16[4,160,1024]{2,1,0:T(8,128)(2,1)} %fusion.29), channel_id=1, source_target_pairs={{0,4},{4,8},{8,12},{12,0},{1,5},{5,9},{9,13},{13,1},{2,6},{6,10},{... | collective-permute-start | bytes 3932168 | tf_op jit(solution)/shard_map/ppermute | solution.py:81
  47.3 8.2 %copy-start.6 = (s32[512]{0:T(512)S(1)}, s32[512]{0:T(512)}, u32[]{:S(2)}) copy-start(s32[512]{0:T(512)} %param.10) | copy-start | bytes 6148
  112.7 48.9 %copy-start.1 = (f32[4,512,128]{2,1,0:T(8,128)S(1)}, f32[4,512,128]{2,1,0:T(8,128)}, u32[]{:S(2)}) copy-start(f32[4,512,128]{2,1,0:T(8,128)} %shard_map.86) | copy-start | bytes 3145732
  161.7 4.7 %copy-start.7 = (f32[8]{0:T(128)S(1)}, f32[8]{0:T(128)}, u32[]{:S(2)}) copy-start(f32[8]{0:T(128)} %param.15) | copy-start | bytes 100
  161.7 4.7 %copy-start.8 = (s32[8]{0:T(128)S(1)}, s32[8]{0:T(128)}, u32[]{:S(2)}) copy-start(s32[8]{0:T(128)} %param.14) | copy-start | bytes 100
  163.2 1.6 collective-permute-start.8
  164.8 8.4 %collective-permute-start.9 = (f32[512,128]{1,0:T(8,128)S(1)}, f32[512,128]{1,0:T(8,128)S(1)}, u32[]{:S(2)}, u32[]{:S(2)}) collective-permute-start(f32[512,128]{1,0:T(8,128)S(1)} %add.142), channel_id=1, source_target_pairs={{0,2},{1,3},{2,0},{3,1},{4,6},{5,7},{6,4},{7,5},{8,10},{9,11},{10,... | collective-permute-start | bytes 786440 | tf_op jit(solution)/shard_map/ppermute | solution.py:72
  175.4 1.6 collective-permute-start.10
  177.0 8.5 %collective-permute-start.11 = (f32[512,128]{1,0:T(8,128)S(1)}, f32[512,128]{1,0:T(8,128)S(1)}, u32[]{:S(2)}, u32[]{:S(2)}) collective-permute-start(f32[512,128]{1,0:T(8,128)S(1)} %add.148), channel_id=1, source_target_pairs={{0,2},{1,3},{2,0},{3,1},{4,6},{5,7},{6,4},{7,5},{8,10},{9,11},{10,... | collective-permute-start | bytes 786440 | tf_op jit(solution)/shard_map/ppermute | solution.py:72
  178.6 1.2 collective-permute-start.12
  179.7 5.7 %collective-permute-start.13 = (f32[512]{0:T(512)S(1)}, f32[512]{0:T(512)S(1)}, u32[]{:S(2)}, u32[]{:S(2)}) collective-permute-start(f32[512]{0:T(512)S(1)} %add.150), channel_id=1, source_target_pairs={{0,2},{1,3},{2,0},{3,1},{4,6},{5,7},{6,4},{7,5},{8,10},{9,11},{10,... | collective-permute-start | bytes 6152 | tf_op jit(solution)/shard_map/ppermute | solution.py:72
